TPU v7x, 512 devices: a whole 4x8x8 slice. The times are simulated.
512 devices in a mesh: tm: 16 (over z, core), pairs: 32 (over y, x).
Axes of the slice: x: 4, y: 8, z: 8, core: 2. Of those that a mesh axis runs over, the one named last changes fastest.
Arguments:
- record: bfloat16 [128, 3, 16, 4096], P('pairs', None, 'tm')
- requested: int32 [32, 32, 2], replicated, may hold values from 0 to 3, as said below
- partners: int32 [32, 12, 48], P('pairs'), may hold values from 0 to 63
- codes: int32 [32, 12, 48], P('pairs'), may hold values from 0 to 2
- counts: int32 [32, 12], P('pairs'), may hold values from 1 to 48, as said below
Outputs:
- stacks: float32 [32, 576, 1024], P('pairs', 'tm')
Inputs may be any that keep to these rules, and one draw needn't show every extreme that they name: requested[e, d] holds 2 different local station indices of device d, meaning stations d * 4 + requested[e, d, i]. `partners`: slot k stands for the station requested[e, k // 2, k % 2]. Slots at and after counts[e, j] are unused; on some device every owned trace has 48 live slots.
All inputs are finite; a program needn't handle non-finite values.
Results may differ from a plain program's by a relative error of at most 0.0037.
Values may be sent and summed in bfloat16 or wider, within the bound.
No kernel may reach another device: no remote copies, remote signals or barrier semaphores. Data moves between devices by JAX's collectives and lax.ppermute only.
A program may use at most 64 MiB of HBM per device.

v0:
```python
import math

import jax
import jax.numpy as jnp
from jax import lax
from jax.sharding import PartitionSpec as P

LAGS = 1024


def normalize(traces):
    values = traces.astype(jnp.float32)
    values = values - jnp.mean(values, axis=-1, keepdims=True)
    power_mean = jnp.mean(values * values, axis=-1, keepdims=True)
    return (values * lax.rsqrt(power_mean + 1e-06)).astype(jnp.bfloat16)


def correlate(own_trace, partner_rows, lag_count, block_len):
    window_len = own_trace.shape[0]
    half_lag = lag_count // 2
    padded = jnp.pad(own_trace, (half_lag, half_lag + block_len))
    length = padded.shape[0]
    spread = jnp.broadcast_to(padded, (block_len, length)).reshape(-1)
    spread = jnp.pad(spread, (0, block_len))
    skewed = spread.reshape(block_len, length + 1)[:, : window_len + lag_count]
    hankel = skewed.reshape(block_len, (window_len + lag_count) // block_len, block_len)
    blocks_in = window_len // block_len
    pieces = partner_rows.reshape(partner_rows.shape[0], blocks_in, block_len)
    outputs = []
    for offset in range(lag_count // block_len):
        window_view = hankel[:, offset : offset + blocks_in, :]
        outputs.append(
            jnp.einsum("pmi,imr->pr", pieces, window_view, preferred_element_type=jnp.float32)
        )
    return jnp.concatenate(outputs, axis=1)


def shards(record, requested, partners, codes, counts):
    whitened = normalize(record)
    local_stations, comp_count, window_count, window_len = whitened.shape
    owners = lax.axis_size("pairs")
    capacity = requested.shape[2]
    per_trace = partners.shape[2]
    trace_count = local_stations * comp_count
    block_len = math.gcd(math.gcd(128, window_len), LAGS)
    own_index = lax.axis_index("pairs")
    slot_ids = partners[0]
    comp_ids = codes[0]
    everyone = lax.all_gather(whitened, "pairs", axis=0, tiled=True)
    trace_pool = everyone.reshape(owners * local_stations * comp_count, window_count, window_len)
    asked_table = lax.dynamic_index_in_dim(requested, own_index, axis=0, keepdims=False)
    station_of = (
        asked_table + jnp.arange(owners, dtype=jnp.int32)[:, None] * local_stations
    ).reshape(-1)
    matches = slot_ids[:, :, None] == jnp.arange(owners * capacity, dtype=jnp.int32)[None, None, :]
    stations = jnp.sum(jnp.where(matches, station_of[None, None, :], 0), axis=-1)
    row_ids = stations * comp_count + comp_ids
    picked = jnp.take(trace_pool, row_ids.reshape(-1), axis=0)
    live_rows = jnp.arange(per_trace, dtype=jnp.int32)[None, :] < counts[0][:, None]
    picked = jnp.where(live_rows.reshape(-1)[:, None, None], picked, jnp.zeros((), jnp.bfloat16))
    picked = picked.reshape(trace_count, per_trace, window_count, window_len)
    picked = jnp.moveaxis(picked, 2, 1).reshape(trace_count * window_count, per_trace, window_len)
    own_rows = whitened.reshape(trace_count * window_count, window_len)

    def one_trace(operands):
        own_row, partner_rows = operands
        return correlate(own_row, partner_rows, LAGS, block_len)

    lagged = lax.map(one_trace, (own_rows, picked))
    lagged = lagged.reshape(trace_count, window_count, per_trace, LAGS)
    total_windows = window_count * lax.axis_size("tm")
    window_term = jnp.sum(lagged, axis=1) * (1.0 / math.sqrt(window_len * total_windows))
    window_term = window_term.reshape(1, trace_count * per_trace, LAGS)
    return lax.psum_scatter(window_term, "tm", scatter_dimension=1, tiled=True)


def solution(mesh):
    return jax.shard_map(
        shards,
        mesh=mesh,
        in_specs=(
            P("pairs", None, "tm", None),
            P(),
            P("pairs", None, None),
            P("pairs", None, None),
            P("pairs", None),
        ),
        out_specs=P("pairs", "tm", None),
        check_vma=False,
    )
```

profile of v0, /device:TPU:1, one launch (start us, length us, event | category | flops | bytes accessed | tf_op | source)
XLA Modules:
  0.0 376.4 jit_solution(2427693640517813525)
XLA Ops:
  8.8 1.7 fusion.27
  14.8 85.8 %all-gather.2.cloned.1.call-done = bf16[128,3,1,4096]{3,1,2,0:T(4,128)(2,1)} async-done(((bf16[4,3,1,4096]{3,1,2,0:T(4,128)(2,1)}), bf16[128,3,1,4096]{3,1,2,0:T(4,128)(2,1)}) %all-gather.2.cloned.1.call-update) | async-done | bytes 3145744 | tf_op jit(solution)/shard_map/all_gather | solution.py:49
  100.5 6.0 %reshape.160 = bf16[384,4096]{1,0:T(8,128)(2,1)S(1)} reshape(bf16[128,3,1,4096]{3,1,2,0:T(4,128)(2,1)} %all-gather.2.cloned.1.call-done) | data formatting | bytes 6291456 | tf_op jit(solution)/shard_map/reshape | solution.py:50
  106.5 5.3 %gather_fusion = bf16[576,4096]{1,0:T(8,128)(2,1)} fusion(bf16[384,4096]{1,0:T(8,128)(2,1)S(1)} %reshape.160, s32[1024]{0:T(1024)S(1)} %pad_clamp_fusion), kind=kCustom, calls=%fused_computation | custom fusion | bytes 9439488 | tf_op jit(solution)/shard_map/jit(_take)/gather | solution.py:58
  111.8 5.1 %select_select_fusion = bf16[12,48,4096]{2,1,0:T(8,128)(2,1)} fusion(bf16[12,48,4096]{2,1,0:T(8,128)(2,1)} %bitcast.87, pred[12,48]{1,0:T(8,128)(4,1)S(1)} %get-tuple-element.68, pred[12,48]{1,0:T(8,128)(4,1)S(1)} %get-tuple-element.67), kind=kLoop, calls=%fused_computation.36 | loop fusion | flops 4718592 | bytes 9438336 | tf_op jit(solution)/shard_map/jit(_where)/select_n | solution.py:60
  116.9 123.0 %while.12 = (s32[]{:T(128)}, f32[12,48,1024]{2,1,0:T(8,128)}, bf16[12,48,4096]{2,1,0:T(8,128)(2,1)}, bf16[12,4096]{1,0:T(8,128)(2,1)S(1)}, s32[]{:T(128)}, /*index=5*/bf16[]{:T(256)}) while((s32[]{:T(128)}, f32[12,48,1024]{2,1,0:T(8,128)}, bf16[12,48,4096]{2,1,0:T(8,128)(2,1)}, bf16[12,4096]{1,0:T(8,128)(2,1)S(1)}, s32[]{:T(128)}, ...), condition=%wide.region_4.5_spmd, body=%wide.region_3.4_spmd.sunk | while | flops 402653184 | bytes 28391248 | solution.py:69
  117.1 1.5 reshape.186
  118.7 1.9 reshape.187
  127.3 1.5 reshape.186
  129.0 1.9 reshape.187
  137.6 1.5 reshape.186
  139.2 1.9 reshape.187
  147.8 1.5 reshape.186
  149.5 1.9 reshape.187
  158.1 1.5 reshape.186
  159.7 1.9 reshape.187
  168.3 1.5 reshape.186
  170.0 1.9 reshape.187
  178.6 1.5 reshape.186
  180.2 1.9 reshape.187
  188.8 1.5 reshape.186
  190.5 1.9 reshape.187
  199.1 1.5 reshape.186
  200.7 1.9 reshape.187
  211.0 1.9 reshape.187
  221.2 1.9 reshape.187
  229.8 1.5 reshape.186
  231.5 1.9 reshape.187
  239.9 1.9 broadcast_multiply_fusion
  241.8 3.8 %mul.68 = f32[1,576,1024]{2,0,1:T(1,128)} reshape(f32[12,48,1024]{2,1,0:T(8,128)S(1)} %broadcast_multiply_fusion) | data formatting | bytes 4718592 | tf_op jit(solution)/shard_map/mul | solution.py:72
  247.6 120.4 %all-reduce.5.cloned.1.call-done = f32[1,576,1024]{2,0,1:T(1,128)} async-done(((f32[1,576,1024]{2,0,1:T(1,128)}), f32[1,576,1024]{2,0,1:T(1,128)}) %all-reduce.5.cloned.1.call-update) | async-done | bytes 2359312
  368.0 1.6 constant_dynamic-slice_fusion
  (235 shorter events, 90.7 us)
Async XLA Ops:
  6.5 5.0 %copy-start = (s32[32,32,2]{1,2,0:T(2,128)S(1)}, s32[32,32,2]{1,2,0:T(2,128)}, u32[]{:S(2)}) copy-start(s32[32,32,2]{1,2,0:T(2,128)} %param.8) | copy-start | bytes 24580
  6.5 94.0 %all-gather.2.cloned.1.call-start = ((), (), s32[]{:S(2)}) async-start(), calls=%async_computation | async-start | bytes 4325376 | tf_op jit(solution)/shard_map/all_gather | solution.py:49
  10.5 357.5 %all-reduce.5.cloned.1.call-start = ((), (), s32[]{:S(2)}) async-start(), calls=%async_computation.1 | async-start | bytes 4718592
Sparse Core Ops, SparseCore 0:
  10.6 89.8 all-gather.1
  245.8 122.1 all-reduce.4
where the time goes:
time: 377 us; the launch traced here: 376 us
  waiting for transfers between devices  206 us (55%)
  local copies, waits for them, and re-layouts  97.3 us (26%)
  matrix products  44.5 us (12%)
  between operations  14.2 us (4%)
  other arithmetic  12.8 us (3%)
    unnamed x3, waiting for transfers between devices  120 us
    all_gather x1, waiting for transfers between devices, shards(): everyone = lax.all_gather(whitened, 'pairs', axis=0, tiled=True)  85.8 us
    dot_general x96, matrix products, correlate(): jnp.einsum('pmi,imr->pr', pieces, window_view, preferred_element_type=jnp...  44.5 us
    reshape x12, local copies, waits for them, and re-layouts, correlate(): skewed = spread.reshape(block_len, length + 1)[:, :window_len + lag_count]  23.3 us
    reshape x12, local copies, waits for them, and re-layouts, correlate(): spread = jnp.broadcast_to(padded, (block_len, length)).reshape(-1)  18.4 us
    while x24, local copies, waits for them, and re-layouts  13.1 us
    slice x24, local copies, waits for them, and re-layouts, correlate(): skewed = spread.reshape(block_len, length + 1)[:, :window_len + lag_count]  10.8 us
    dynamic_update_slice x12, local copies, waits for them, and re-layouts, shards(): lagged = lax.map(one_trace, (own_rows, picked))  8.4 us
  transfers between devices with their start and end apart: 2, of which 2 were waited for; matrix products, arithmetic and copies ran while one was open for 1% of the time, Pallas kernels for 0%

commit v1 on v0

v1 whole, which is shorter than its diff:
```python
import math

import jax
import jax.numpy as jnp
from jax import lax
from jax.experimental import pallas as pl
from jax.experimental.pallas import tpu as pltpu
from jax.sharding import PartitionSpec as P

LAGS = 1024
BLK = 256
LANE = 128


def normalize(traces):
    values = traces.astype(jnp.float32)
    values = values - jnp.mean(values, axis=-1, keepdims=True)
    power_mean = jnp.mean(values * values, axis=-1, keepdims=True)
    return (values * lax.rsqrt(power_mean + 1e-06)).astype(jnp.bfloat16)


def flip_lanes(rows):
    shape = rows.shape
    grouped = rows.reshape(shape[:-1] + (shape[-1] // LANE, LANE))
    return grouped[..., ::-1].reshape(shape)


def corr_kernel(src_ref, p_ref, o_ref, *, win, scale):
    rows = p_ref.shape[1]
    span = src_ref.shape[2]
    m_blocks = win // BLK
    o_blocks = LAGS // BLK
    d_blocks = m_blocks + o_blocks - 1
    width = BLK * (d_blocks - 1) + BLK + LANE
    wide = jnp.broadcast_to(src_ref[0], (LANE, span))
    hank = pltpu.roll(wide, span - (LANE - 1), 1, stride=1, stride_axis=0)
    hank = hank[:, :width].astype(jnp.bfloat16)
    acc = [jnp.zeros((rows, BLK), jnp.float32) for _ in range(o_blocks)]
    for d in range(d_blocks):
        rhs = jnp.concatenate(
            [hank[:, BLK * d: BLK * d + BLK], hank[:, BLK * d + LANE: BLK * d + LANE + BLK]], axis=0
        )
        lags = [o for o in range(o_blocks) if 0 <= d - o < m_blocks]
        lhs = jnp.concatenate([p_ref[0, :, BLK * (d - o): BLK * (d - o) + BLK] for o in lags], axis=0)
        res = jnp.dot(lhs, rhs, preferred_element_type=jnp.float32)
        for k, o in enumerate(lags):
            acc[o] = acc[o] + res[rows * k: rows * (k + 1)]
    o_ref[0] = jnp.concatenate(acc, axis=1) * scale


def correlate(src, partner_rows, scale):
    traces, rows, win = partner_rows.shape
    span = src.shape[-1]
    flops = 2 * traces * rows * win * LAGS
    return pl.pallas_call(
        lambda s, p, o: corr_kernel(s, p, o, win=win, scale=scale),
        grid=(traces,),
        in_specs=[
            pl.BlockSpec((1, 1, span), lambda j: (j, 0, 0)),
            pl.BlockSpec((1, rows, win), lambda j: (j, 0, 0)),
        ],
        out_specs=pl.BlockSpec((1, rows, LAGS), lambda j: (j, 0, 0)),
        out_shape=jax.ShapeDtypeStruct((traces, rows, LAGS), jnp.float32),
        cost_estimate=pl.CostEstimate(
            flops=flops, transcendentals=0,
            bytes_accessed=traces * (rows * win * 2 + span * 4 + rows * LAGS * 4),
        ),
        name="xcorr",
    )(src.reshape(traces, 1, span), partner_rows)


def shards(record, requested, partners, codes, counts):
    whitened = normalize(record)
    local_stations, comp_count, window_count, window_len = whitened.shape
    owners = lax.axis_size("pairs")
    tm_count = lax.axis_size("tm")
    capacity = requested.shape[2]
    per_trace = partners.shape[2]
    trace_count = local_stations * comp_count
    own_index = lax.axis_index("pairs")
    slot_ids = partners[0]
    comp_ids = codes[0]
    everyone = lax.all_gather(flip_lanes(whitened), "pairs", axis=0, tiled=True)
    trace_pool = everyone.reshape(owners * local_stations * comp_count, window_count * window_len)
    asked_table = lax.dynamic_index_in_dim(requested, own_index, axis=0, keepdims=False)
    station_of = (
        asked_table + jnp.arange(owners, dtype=jnp.int32)[:, None] * local_stations
    ).reshape(-1)
    matches = slot_ids[:, :, None] == jnp.arange(owners * capacity, dtype=jnp.int32)[None, None, :]
    stations = jnp.sum(jnp.where(matches, station_of[None, None, :], 0), axis=-1)
    row_ids = stations * comp_count + comp_ids
    picked = jnp.take(trace_pool, row_ids.reshape(-1), axis=0)
    live_rows = jnp.arange(per_trace, dtype=jnp.int32)[None, :] < counts[0][:, None]
    picked = jnp.where(live_rows.reshape(-1)[:, None], picked, jnp.zeros((), jnp.bfloat16))
    picked = picked.reshape(trace_count, per_trace, window_len)
    half = LAGS // 2
    own = whitened.reshape(trace_count, window_len).astype(jnp.float32)
    span = ((window_len + LAGS + LANE - 1) // LANE) * LANE
    src = jnp.pad(own, ((0, 0), (half, span - window_len - half)))
    total_windows = window_count * tm_count
    scale = 1.0 / math.sqrt(window_len * total_windows)
    lagged = correlate(src, picked, scale)
    lagged = lagged.reshape(tm_count, trace_count * per_trace // tm_count, LAGS)
    out = lax.psum_scatter(lagged, "tm", scatter_dimension=0, tiled=True)
    return out.reshape(1, trace_count * per_trace // tm_count, LAGS)


def solution(mesh):
    return jax.shard_map(
        shards,
        mesh=mesh,
        in_specs=(
            P("pairs", None, "tm", None),
            P(),
            P("pairs", None, None),
            P("pairs", None, None),
            P("pairs", None),
        ),
        out_specs=P("pairs", "tm", None),
        check_vma=False,
    )
```

time: 377 us -> 205 us (0.54)
  local copies, waits for them, and re-layouts: 97.3 us -> 19.2 us
  waiting for transfers between devices: 206 us -> 147 us
  matrix products: 44.5 us -> 0 us
  Pallas kernels: 0 us -> 12.8 us
    unnamed x3 -> x2, waiting for transfers between devices: 120 us -> 0.03 us
    reduce_scatter x0 -> x1, waiting for transfers between devices: none -> 60.9 us  [shards(): out = lax.psum_scatter(lagged, 'tm', scatter_dimension=0, tiled=True)]
    dot_general x96 -> x0, matrix products: 44.5 us -> none  [correlate(): jnp.einsum('pmi,imr->pr', pieces, window_view, preferred_element_type=jnp...]
    reshape x26 -> x6, local copies, waits for them, and re-layouts: 48.7 us -> 10.6 us  [the longest x1 5.96 us: shards(): everyone.reshape(owners * local_stations * comp_count, window_count * win...]
    while x24 -> x0, local copies, waits for them, and re-layouts: 13.1 us -> none
    pallas_call x0 -> x1, Pallas kernels: none -> 12.8 us  [correlate(): pl.pallas_call(lambda s, p, o: corr_kernel(s, p, o, win=win, scale=scale)...]
    slice x24 -> x0, local copies, waits for them, and re-layouts: 10.8 us -> none  [correlate(): skewed = spread.reshape(block_len, length + 1)[:, :window_len + lag_count]]
    dynamic_update_slice x12 -> x0, local copies, waits for them, and re-layouts: 8.4 us -> none  [shards(): lagged = lax.map(one_trace, (own_rows, picked))]
  transfers between devices with their start and end apart: 2 -> 2, of which waited for: 2 -> 2; matrix products, arithmetic and copies ran while one was open for 1% -> 2% of each run, Pallas kernels for 0% -> 0%
where the time goes in v1:
time: 205 us; the launch traced here: 202 us
  waiting for transfers between devices  147 us (72%)
  local copies, waits for them, and re-layouts  19.2 us (9%)
  between operations  13.5 us (7%)
  Pallas kernels  12.8 us (6%)
  other arithmetic  10.2 us (5%)
    all_gather x1, waiting for transfers between devices, shards(): everyone = lax.all_gather(flip_lanes(whitened), 'pairs', axis=0, tiled=True)  85.7 us
    reduce_scatter x1, waiting for transfers between devices, shards(): out = lax.psum_scatter(lagged, 'tm', scatter_dimension=0, tiled=True)  60.9 us
    pallas_call x1, Pallas kernels, correlate(): pl.pallas_call(lambda s, p, o: corr_kernel(s, p, o, win=win, scale=scale)...  12.8 us
    reshape x1, local copies, waits for them, and re-layouts, shards(): everyone.reshape(owners * local_stations * comp_count, window_count * win...  5.96 us
    gather x1, local copies, waits for them, and re-layouts, shards(): picked = jnp.take(trace_pool, row_ids.reshape(-1), axis=0)  5.29 us
    select_n x1, other arithmetic, shards(): jnp.where(live_rows.reshape(-1)[:, None], picked, jnp.zeros((), jnp.bfloa...  5.1 us
  transfers between devices with their start and end apart: 2, of which 2 were waited for; matrix products, arithmetic and copies ran while one was open for 2% of the time, Pallas kernels for 0%

profile of v1, /device:TPU:1, one launch (start us, length us, event | category | flops | bytes accessed | tf_op | source)
XLA Modules:
  0.0 202.4 jit_solution(8995581383650949039)
XLA Ops:
  6.5 0.0 copy-start
  6.5 0.0 all-gather.2.cloned.1.call-start
  6.5 1.0 convert_reduce_fusion
  7.6 1.1 fusion.2
  8.7 1.0 fusion.3
  9.7 0.1 reshape.127
  9.8 0.1 rev.3
  10.0 0.7 copy.20
  10.7 0.0 all-gather.2.cloned.1.call-update
  10.8 0.0 reduce-scatter.2.cloned.1.call-start
  10.8 0.1 copy.18
  10.9 0.1 copy.19
  11.0 0.1 squeeze.9
  11.2 0.1 add.70
  11.2 0.1 add.71
  11.3 0.7 copy.28
  12.0 0.4 select_reduce_fusion
  12.4 0.1 mul.49
  12.5 0.7 reduce.2
  13.2 0.1 squeeze.11
  13.3 0.1 convert_element_type.14
  13.4 0.9 reshape.132.s
  14.4 0.8 iota_compare_fusion.1
  15.1 85.7 %all-gather.2.cloned.1.call-done = bf16[128,3,1,4096]{3,1,2,0:T(4,128)(2,1)} async-done(((bf16[4,3,1,4096]{3,1,2,0:T(4,128)(2,1)}), bf16[128,3,1,4096]{3,1,2,0:T(4,128)(2,1)}) %all-gather.2.cloned.1.call-update) | async-done | bytes 3145744 | tf_op jit(solution)/shard_map/all_gather | solution.py:83
  100.8 6.0 %reshape.129 = bf16[384,4096]{1,0:T(8,128)(2,1)S(1)} reshape(bf16[128,3,1,4096]{3,1,2,0:T(4,128)(2,1)} %all-gather.2.cloned.1.call-done) | data formatting | bytes 6291456 | tf_op jit(solution)/shard_map/reshape | solution.py:84
  106.8 5.3 %gather_fusion = bf16[576,4096]{1,0:T(8,128)(2,1)} fusion(bf16[384,4096]{1,0:T(8,128)(2,1)S(1)} %reshape.129, s32[1024]{0:T(1024)S(1)} %pad_clamp_fusion), kind=kCustom, calls=%fused_computation | custom fusion | bytes 9439488 | tf_op jit(solution)/shard_map/jit(_take)/gather | solution.py:92
  112.1 5.1 %select_select_fusion.p = bf16[12,48,4096]{2,1,0:T(8,128)(2,1)} fusion(bf16[12,48,4096]{2,1,0:T(8,128)(2,1)} %bitcast.21, pred[12,48]{1,0:T(8,128)(4,1)S(1)} %get-tuple-element.6, pred[12,48]{1,0:T(8,128)(4,1)S(1)} %get-tuple-element.5), kind=kLoop, calls=%fused_computation.1 | loop fusion | flops 4718592 | bytes 9438336 | tf_op jit(solution)/shard_map/jit(_where)/select_n | solution.py:94
  117.2 12.8 %xcorr.1 = f32[12,48,1024]{2,1,0:T(8,128)} custom-call(f32[12,1,5120]{2,1,0:T(1,128)} %reshape.132.s, bf16[12,48,4096]{2,1,0:T(8,128)(2,1)} %select_select_fusion.p), custom_call_target="tpu_custom_call" | custom-call | flops 4831838208 | bytes 7323648 | tf_op jit(solution)/shard_map/xcorr/pallas_call | solution.py:55
  130.0 2.9 %reshape.130 = f32[16,36,1024]{2,1,0:T(8,128)} reshape(f32[12,48,1024]{2,1,0:T(8,128)} %xcorr.1) | data formatting | bytes 4718592 | tf_op jit(solution)/shard_map/reshape | solution.py:103
  132.8 0.0 reduce-scatter.2.cloned.1.call-update
  132.9 60.9 %reduce-scatter.2.cloned.1.call-done = f32[1,36,1024]{2,1,0:T(8,128)} async-done(((f32[16,36,1024]{2,1,0:T(8,128)}), f32[1,36,1024]{2,1,0:T(8,128)}) %reduce-scatter.2.cloned.1.call-update) | async-done | bytes 147472 | tf_op jit(solution)/shard_map/reduce_scatter | solution.py:104
  193.8 1.7 copy.21
  (11 shorter events, 0.1 us)
Async XLA Ops:
  6.5 4.4 %copy-start = (s32[32,32,2]{1,2,0:T(2,128)S(1)}, s32[32,32,2]{1,2,0:T(2,128)}, u32[]{:S(2)}) copy-start(s32[32,32,2]{1,2,0:T(2,128)} %param.6) | copy-start | bytes 24580
  6.5 94.3 %all-gather.2.cloned.1.call-start = ((), (), s32[]{:S(2)}) async-start(), calls=%async_computation.1 | async-start | bytes 4325376 | tf_op jit(solution)/shard_map/all_gather | solution.py:83
  10.8 183.0 %reduce-scatter.2.cloned.1.call-start = ((), (), s32[]{:S(2)}) async-start(), calls=%async_computation.2 | async-start | bytes 2785280 | tf_op jit(solution)/shard_map/reduce_scatter | solution.py:104
Sparse Core Ops, SparseCore 0:
  10.9 89.8 all-gather.1
  133.0 60.7 reduce-scatter.1

commit v2 on v1

--- a/solution.py
+++ b/solution.py
@@ -80,15 +80,13 @@
     own_index = lax.axis_index("pairs")
     slot_ids = partners[0]
     comp_ids = codes[0]
-    everyone = lax.all_gather(flip_lanes(whitened), "pairs", axis=0, tiled=True)
-    trace_pool = everyone.reshape(owners * local_stations * comp_count, window_count * window_len)
-    asked_table = lax.dynamic_index_in_dim(requested, own_index, axis=0, keepdims=False)
-    station_of = (
-        asked_table + jnp.arange(owners, dtype=jnp.int32)[:, None] * local_stations
-    ).reshape(-1)
-    matches = slot_ids[:, :, None] == jnp.arange(owners * capacity, dtype=jnp.int32)[None, None, :]
-    stations = jnp.sum(jnp.where(matches, station_of[None, None, :], 0), axis=-1)
-    row_ids = stations * comp_count + comp_ids
+    mine = flip_lanes(whitened).reshape(local_stations, comp_count * window_count * window_len)
+    asked_of_me = lax.dynamic_index_in_dim(requested, own_index, axis=1, keepdims=False)
+    outgoing = jnp.take(mine, asked_of_me.reshape(-1), axis=0)
+    outgoing = outgoing.reshape(owners, capacity * comp_count, window_count * window_len)
+    arrived = lax.all_to_all(outgoing, "pairs", 0, 0, tiled=True)
+    trace_pool = arrived.reshape(owners * capacity * comp_count, window_count * window_len)
+    row_ids = slot_ids * comp_count + comp_ids
     picked = jnp.take(trace_pool, row_ids.reshape(-1), axis=0)
     live_rows = jnp.arange(per_trace, dtype=jnp.int32)[None, :] < counts[0][:, None]
     picked = jnp.where(live_rows.reshape(-1)[:, None], picked, jnp.zeros((), jnp.bfloat16))

time: 205 us -> 182 us (0.89)
  waiting for transfers between devices: 147 us -> 110 us
  starting transfers between devices: 0.04 us -> 10.8 us
    all_gather x1 -> x0, waiting for transfers between devices: 85.7 us -> none  [shards(): everyone = lax.all_gather(flip_lanes(whitened), 'pairs', axis=0, tiled=True)]
    all_to_all x0 -> x1, waiting for transfers between devices: none -> 47 us  [shards(): arrived = lax.all_to_all(outgoing, 'pairs', 0, 0, tiled=True)]
    all_to_all x0 -> x1, starting transfers between devices: none -> 10.8 us  [shards(): arrived = lax.all_to_all(outgoing, 'pairs', 0, 0, tiled=True)]
    gather x0 -> x2, local copies, waits for them, and re-layouts: none -> 5.59 us  [shards(): outgoing = jnp.take(mine, asked_of_me.reshape(-1), axis=0)]
    reshape x3 -> x2, local copies, waits for them, and re-layouts: 6.73 us -> 2.65 us  [the longest x1 2.54 us: shards(): arrived.reshape(owners * capacity * comp_count, window_count * window_len)]
    reduce_scatter x1, waiting for transfers between devices: 60.9 us -> 63.5 us  [shards(): out = lax.psum_scatter(lagged, 'tm', scatter_dimension=0, tiled=True)]
  transfers between devices with their start and end apart: 2 -> 2, of which waited for: 2 -> 2; matrix products, arithmetic and copies ran while one was open for 2% -> 1% of each run, Pallas kernels for 0% -> 0%
where the time goes in v2:
time: 182 us; the launch traced here: 179 us
  waiting for transfers between devices  110 us (60%)
  local copies, waits for them, and re-layouts  21.2 us (12%)
  between operations  13.5 us (7%)
  Pallas kernels  12.8 us (7%)
  starting transfers between devices  10.8 us (6%)
  other arithmetic  10 us (5%)
    reduce_scatter x1, waiting for transfers between devices, shards(): out = lax.psum_scatter(lagged, 'tm', scatter_dimension=0, tiled=True)  63.5 us
    all_to_all x1, waiting for transfers between devices, shards(): arrived = lax.all_to_all(outgoing, 'pairs', 0, 0, tiled=True)  47 us
    pallas_call x1, Pallas kernels, correlate(): pl.pallas_call(lambda s, p, o: corr_kernel(s, p, o, win=win, scale=scale)...  12.8 us
    all_to_all x1, starting transfers between devices, shards(): arrived = lax.all_to_all(outgoing, 'pairs', 0, 0, tiled=True)  10.8 us
    gather x2, local copies, waits for them, and re-layouts, shards(): outgoing = jnp.take(mine, asked_of_me.reshape(-1), axis=0)  5.59 us
    gather x1, local copies, waits for them, and re-layouts, shards(): picked = jnp.take(trace_pool, row_ids.reshape(-1), axis=0)  5.29 us
    select_n x1, other arithmetic, shards(): jnp.where(live_rows.reshape(-1)[:, None], picked, jnp.zeros((), jnp.bfloa...  5.1 us
  transfers between devices with their start and end apart: 2, of which 2 were waited for; matrix products, arithmetic and copies ran while one was open for 1% of the time, Pallas kernels for 0%

profile of v2, /device:TPU:1, one launch (start us, length us, event | category | flops | bytes accessed | tf_op | source)
XLA Modules:
  0.0 178.8 jit_solution(113803671603010844)
XLA Ops:
  6.5 1.4 fusion.7
  8.0 0.1 reshape.159
  8.1 1.0 convert_reduce_fusion
  9.2 1.1 fusion.2
  10.3 1.0 fusion.3
  11.3 0.1 reshape.158
  11.4 0.1 rev.3
  11.6 2.7 %gather_fusion = bf16[64,12288]{1,0:T(8,128)(2,1)} fusion(bf16[4,12288]{1,0:T(4,128)(2,1)S(1)} %reshape_reshape.3, s32[1024]{0:T(1024)S(1)} %pad_clamp_fusion.1), kind=kCustom, calls=%fused_computation | custom fusion | bytes 3145984 | tf_op jit(solution)/shard_map/jit(_take)/gather | solution.py:85
  14.3 2.9 %gather.13 = bf16[32,6,4096]{2,1,0:T(8,128)(2,1)S(1)} reshape(bf16[64,12288]{1,0:T(8,128)(2,1)} %gather_fusion) | data formatting | bytes 3145728 | tf_op jit(solution)/shard_map/jit(_take)/gather | solution.py:85
  17.2 0.1 copy.12
  17.3 0.1 copy.13
  17.4 1.6 broadcast_select_fusion
  19.0 0.0 copy-start
  19.0 10.8 %all-to-all-start = ((bf16[32,6,4096]{2,1,0:T(8,128)(2,1)}), bf16[32,6,4096]{2,1,0:T(8,128)(2,1)}, u32[]{:S(2)}, u32[]{:S(2)}) async-start(bf16[32,6,4096]{2,1,0:T(8,128)(2,1)} %broadcast_select_fusion), calls=%async_computation | async-start | bytes 4194304 | tf_op jit(solution)/shard_map/all_to_all | solution.py:87
  29.8 0.0 reduce-scatter.2.cloned.1.call-start
  29.8 0.1 copy.11
  29.9 0.0 copy-done
  29.9 0.0 copy-done.1
  30.0 0.1 add.90
  30.1 0.1 convert_element_type.14
  30.2 0.9 reshape.163.s
  31.1 0.0 copy-done.2
  31.1 0.1 iota_compare_fusion
  31.2 47.0 %all-to-all-done = bf16[32,6,4096]{2,1,0:T(8,128)(2,1)} async-done(((bf16[32,6,4096]{2,1,0:T(8,128)(2,1)}), bf16[32,6,4096]{2,1,0:T(8,128)(2,1)}, u32[]{:S(2)}, u32[]{:S(2)}) %all-to-all-start) | async-done | bytes 1572896 | tf_op jit(solution)/shard_map/all_to_all | solution.py:87
  78.2 2.5 %reshape.160 = bf16[192,4096]{1,0:T(8,128)(2,1)S(1)} reshape(bf16[32,6,4096]{2,1,0:T(8,128)(2,1)} %all-to-all-done) | data formatting | bytes 3145728 | tf_op jit(solution)/shard_map/reshape | solution.py:88
  80.7 5.3 %gather_fusion.1 = bf16[576,4096]{1,0:T(8,128)(2,1)} fusion(bf16[192,4096]{1,0:T(8,128)(2,1)S(1)} %reshape.160, s32[1024]{0:T(1024)S(1)} %pad_clamp_fusion), kind=kCustom, calls=%fused_computation.1 | custom fusion | bytes 9439488 | tf_op jit(solution)/shard_map/jit(_take)/gather | solution.py:90
  86.0 5.1 %select_select_fusion.p = bf16[12,48,4096]{2,1,0:T(8,128)(2,1)} fusion(bf16[12,48,4096]{2,1,0:T(8,128)(2,1)} %bitcast.20, pred[12,48]{1,0:T(8,128)(4,1)S(1)} %get-tuple-element.10, pred[12,48]{1,0:T(8,128)(4,1)S(1)} %get-tuple-element.9), kind=kLoop, calls=%fused_computation.2 | loop fusion | flops 4718592 | bytes 9438336 | tf_op jit(solution)/shard_map/jit(_where)/select_n | solution.py:92
  91.1 12.8 %xcorr.1 = f32[12,48,1024]{2,1,0:T(8,128)} custom-call(f32[12,1,5120]{2,1,0:T(1,128)} %reshape.163.s, bf16[12,48,4096]{2,1,0:T(8,128)(2,1)} %select_select_fusion.p), custom_call_target="tpu_custom_call" | custom-call | flops 4831838208 | bytes 7323648 | tf_op jit(solution)/shard_map/xcorr/pallas_call | solution.py:55
  103.9 2.9 %reshape.161 = f32[16,36,1024]{2,1,0:T(8,128)} reshape(f32[12,48,1024]{2,1,0:T(8,128)} %xcorr.1) | data formatting | bytes 4718592 | tf_op jit(solution)/shard_map/reshape | solution.py:101
  106.8 0.0 reduce-scatter.2.cloned.1.call-update
  106.8 63.5 %reduce-scatter.2.cloned.1.call-done = f32[1,36,1024]{2,1,0:T(8,128)} async-done(((f32[16,36,1024]{2,1,0:T(8,128)}), f32[1,36,1024]{2,1,0:T(8,128)}) %reduce-scatter.2.cloned.1.call-update) | async-done | bytes 147472 | tf_op jit(solution)/shard_map/reduce_scatter | solution.py:102
  170.3 1.7 copy.15
  (15 shorter events, 0.2 us)
Async XLA Ops:
  19.0 10.9 %copy-start = (s32[1,12,48]{2,0,1:T(1,128)S(1)}, s32[1,12,48]{2,0,1:T(1,128)}, u32[]{:S(2)}) copy-start(s32[1,12,48]{2,0,1:T(1,128)} %param.8) | copy-start | bytes 6916
  19.0 10.9 %copy-start.1 = (s32[1,12,48]{2,0,1:T(1,128)S(1)}, s32[1,12,48]{2,0,1:T(1,128)}, u32[]{:S(2)}) copy-start(s32[1,12,48]{2,0,1:T(1,128)} %param.7) | copy-start | bytes 6916
  19.0 12.1 %copy-start.2 = (s32[1,12]{1,0:T(1,128)S(1)}, s32[1,12]{1,0:T(1,128)}, u32[]{:S(2)}) copy-start(s32[1,12]{1,0:T(1,128)} %param.9) | copy-start | bytes 148
  19.0 59.2 %all-to-all-start = ((bf16[32,6,4096]{2,1,0:T(8,128)(2,1)}), bf16[32,6,4096]{2,1,0:T(8,128)(2,1)}, u32[]{:S(2)}, u32[]{:S(2)}) async-start(bf16[32,6,4096]{2,1,0:T(8,128)(2,1)} %broadcast_select_fusion), calls=%async_computation | async-start | bytes 4194304 | tf_op jit(solution)/shard_map/all_to_all | solution.py:87
  29.8 140.5 %reduce-scatter.2.cloned.1.call-start = ((), (), s32[]{:S(2)}) async-start(), calls=%async_computation.2 | async-start | bytes 2785280 | tf_op jit(solution)/shard_map/reduce_scatter | solution.py:102
Sparse Core Ops, SparseCore 0:
  106.9 63.3 reduce-scatter.1

commit v3 on v2

--- a/solution.py
+++ b/solution.py
@@ -45,7 +45,7 @@
         res = jnp.dot(lhs, rhs, preferred_element_type=jnp.float32)
         for k, o in enumerate(lags):
             acc[o] = acc[o] + res[rows * k: rows * (k + 1)]
-    o_ref[0] = jnp.concatenate(acc, axis=1) * scale
+    o_ref[0] = (jnp.concatenate(acc, axis=1) * scale).astype(o_ref.dtype)
 
 
 def correlate(src, partner_rows, scale):
@@ -60,10 +60,10 @@
             pl.BlockSpec((1, rows, win), lambda j: (j, 0, 0)),
         ],
         out_specs=pl.BlockSpec((1, rows, LAGS), lambda j: (j, 0, 0)),
-        out_shape=jax.ShapeDtypeStruct((traces, rows, LAGS), jnp.float32),
+        out_shape=jax.ShapeDtypeStruct((traces, rows, LAGS), jnp.bfloat16),
         cost_estimate=pl.CostEstimate(
             flops=flops, transcendentals=0,
-            bytes_accessed=traces * (rows * win * 2 + span * 4 + rows * LAGS * 4),
+            bytes_accessed=traces * (rows * win * 2 + span * 4 + rows * LAGS * 2),
         ),
         name="xcorr",
     )(src.reshape(traces, 1, span), partner_rows)
@@ -99,8 +99,9 @@
     scale = 1.0 / math.sqrt(window_len * total_windows)
     lagged = correlate(src, picked, scale)
     lagged = lagged.reshape(tm_count, trace_count * per_trace // tm_count, LAGS)
-    out = lax.psum_scatter(lagged, "tm", scatter_dimension=0, tiled=True)
-    return out.reshape(1, trace_count * per_trace // tm_count, LAGS)
+    arrived_sums = lax.all_to_all(lagged, "tm", 0, 0, tiled=True)
+    out = jnp.sum(arrived_sums.astype(jnp.float32), axis=0, keepdims=True)
+    return out
 
 
 def solution(mesh):

time: 182 us -> 147 us (0.81); the launches traced: 179 us -> 147 us
  waiting for transfers between devices: 110 us -> 47 us
  blocking collectives: 0 us -> 47 us
  between operations: 13.5 us -> 0.15 us
  local copies, waits for them, and re-layouts: 21.2 us -> 18.7 us
    reduce_scatter x1 -> x0, waiting for transfers between devices: 63.5 us -> none  [shards(): out = lax.psum_scatter(lagged, 'tm', scatter_dimension=0, tiled=True)]
    all_to_all x0 -> x1, blocking collectives: none -> 47 us  [shards(): arrived_sums = lax.all_to_all(lagged, 'tm', 0, 0, tiled=True)]
  transfers between devices with their start and end apart: 2 -> 1, of which waited for: 2 -> 1; matrix products, arithmetic and copies ran while one was open for 1% -> 1% of each run, Pallas kernels for 0% -> 0%
where the time goes in v3:
time: 147 us
  waiting for transfers between devices  47 us (32%)
  blocking collectives  47 us (32%)
  local copies, waits for them, and re-layouts  18.7 us (13%)
  Pallas kernels  12.5 us (9%)
  starting transfers between devices  10.8 us (7%)
  other arithmetic  10.3 us (7%)
    all_to_all x1, waiting for transfers between devices, shards(): arrived = lax.all_to_all(outgoing, 'pairs', 0, 0, tiled=True)  47 us
    all_to_all x1, blocking collectives, shards(): arrived_sums = lax.all_to_all(lagged, 'tm', 0, 0, tiled=True)  47 us
    pallas_call x1, Pallas kernels, correlate(): pl.pallas_call(lambda s, p, o: corr_kernel(s, p, o, win=win, scale=scale)...  12.5 us
    all_to_all x1, starting transfers between devices, shards(): arrived = lax.all_to_all(outgoing, 'pairs', 0, 0, tiled=True)  10.8 us
    gather x2, local copies, waits for them, and re-layouts, shards(): outgoing = jnp.take(mine, asked_of_me.reshape(-1), axis=0)  5.59 us
    gather x1, local copies, waits for them, and re-layouts, shards(): picked = jnp.take(trace_pool, row_ids.reshape(-1), axis=0)  5.29 us
    select_n x1, other arithmetic, shards(): jnp.where(live_rows.reshape(-1)[:, None], picked, jnp.zeros((), jnp.bfloa...  5.1 us
  transfers between devices with their start and end apart: 1, of which 1 were waited for; matrix products, arithmetic and copies ran while one was open for 1% of the time, Pallas kernels for 0%

profile of v3, /device:TPU:1, one launch (start us, length us, event | category | flops | bytes accessed | tf_op | source)
XLA Modules:
  0.0 146.5 jit_solution(10293941002222660012)
XLA Ops:
  0.0 1.4 fusion.7
  1.4 0.1 reshape.159
  1.6 1.0 convert_reduce_fusion.1
  2.6 1.1 fusion.2
  3.7 1.0 fusion.3
  4.8 0.1 reshape.158
  4.9 0.1 rev.3
  5.1 2.7 %gather_fusion = bf16[64,12288]{1,0:T(8,128)(2,1)} fusion(bf16[4,12288]{1,0:T(4,128)(2,1)S(1)} %reshape_reshape.3, s32[1024]{0:T(1024)S(1)} %pad_clamp_fusion.1), kind=kCustom, calls=%fused_computation | custom fusion | bytes 3145984 | tf_op jit(solution)/shard_map/jit(_take)/gather | solution.py:85
  7.8 2.9 %gather.13 = bf16[32,6,4096]{2,1,0:T(8,128)(2,1)S(1)} reshape(bf16[64,12288]{1,0:T(8,128)(2,1)} %gather_fusion) | data formatting | bytes 3145728 | tf_op jit(solution)/shard_map/jit(_take)/gather | solution.py:85
  10.7 0.1 copy.11
  10.8 0.1 copy.12
  10.9 1.6 %broadcast_select_fusion = bf16[32,6,4096]{2,1,0:T(8,128)(2,1)} fusion(bf16[32,6,4096]{2,1,0:T(8,128)(2,1)S(1)} %gather.13, pred[32,6]{1,0:T(8,128)(4,1)S(1)} %copy.12), kind=kLoop, calls=%fused_computation.4 | loop fusion | flops 786432 | bytes 3145920 | tf_op jit(solution)/shard_map/jit(_take)/select_n | solution.py:85
  12.5 0.0 copy-start
  12.5 0.0 copy-start.1
  12.5 10.8 %all-to-all-start = ((bf16[32,6,4096]{2,1,0:T(8,128)(2,1)}), bf16[32,6,4096]{2,1,0:T(8,128)(2,1)}, u32[]{:S(2)}, u32[]{:S(2)}) async-start(bf16[32,6,4096]{2,1,0:T(8,128)(2,1)} %broadcast_select_fusion), calls=%async_computation | async-start | bytes 4194304 | tf_op jit(solution)/shard_map/all_to_all | solution.py:87
  23.3 0.1 copy.10
  23.4 0.0 copy-done
  23.4 0.0 copy-done.1
  23.4 0.1 add.88
  23.5 0.1 convert_element_type.17
  23.6 0.9 reshape.163.s
  24.5 0.0 copy-done.2
  24.5 0.1 iota_compare_fusion
  24.6 47.0 %all-to-all-done = bf16[32,6,4096]{2,1,0:T(8,128)(2,1)} async-done(((bf16[32,6,4096]{2,1,0:T(8,128)(2,1)}), bf16[32,6,4096]{2,1,0:T(8,128)(2,1)}, u32[]{:S(2)}, u32[]{:S(2)}) %all-to-all-start) | async-done | bytes 1572896 | tf_op jit(solution)/shard_map/all_to_all | solution.py:87
  71.6 2.5 %reshape.160 = bf16[192,4096]{1,0:T(8,128)(2,1)S(1)} reshape(bf16[32,6,4096]{2,1,0:T(8,128)(2,1)} %all-to-all-done) | data formatting | bytes 3145728 | tf_op jit(solution)/shard_map/reshape | solution.py:88
  74.2 5.3 %gather_fusion.1 = bf16[576,4096]{1,0:T(8,128)(2,1)} fusion(bf16[192,4096]{1,0:T(8,128)(2,1)S(1)} %reshape.160, s32[1024]{0:T(1024)S(1)} %pad_clamp_fusion), kind=kCustom, calls=%fused_computation.1 | custom fusion | bytes 9439488 | tf_op jit(solution)/shard_map/jit(_take)/gather | solution.py:90
  79.5 5.1 %select_select_fusion.p = bf16[12,48,4096]{2,1,0:T(8,128)(2,1)} fusion(bf16[12,48,4096]{2,1,0:T(8,128)(2,1)} %bitcast.20, pred[12,48]{1,0:T(8,128)(4,1)S(1)} %get-tuple-element.10, pred[12,48]{1,0:T(8,128)(4,1)S(1)} %get-tuple-element.9), kind=kLoop, calls=%fused_computation.2 | loop fusion | flops 4718592 | bytes 9438336 | tf_op jit(solution)/shard_map/jit(_where)/select_n | solution.py:92
  84.6 12.5 %xcorr.1 = bf16[12,48,1024]{2,1,0:T(8,128)(2,1)} custom-call(f32[12,1,5120]{2,1,0:T(1,128)} %reshape.163.s, bf16[12,48,4096]{2,1,0:T(8,128)(2,1)} %select_select_fusion.p), custom_call_target="tpu_custom_call" | custom-call | flops 4831838208 | bytes 6144000 | tf_op jit(solution)/shard_map/xcorr/pallas_call | solution.py:55
  97.1 1.4 reshape.161
  98.5 47.0 %all_to_all.10 = bf16[16,36,1024]{2,1,0:T(8,128)(2,1)S(1)} all-to-all(bf16[16,36,1024]{2,1,0:T(8,128)(2,1)S(1)} %reshape.161), channel_id=1, replica_groups=mesh['tm'=16,'pairs'=32] {'tm'}, dimensions={0} | all-to-all | bytes 2359296 | tf_op jit(solution)/shard_map/all_to_all | solution.py:102
  145.5 0.3 convert_reduce_fusion
  145.8 0.8 broadcast_in_dim.50
  (14 shorter events, 0.2 us)
Async XLA Ops:
  12.5 10.9 %copy-start = (s32[1,12,48]{2,0,1:T(1,128)S(1)}, s32[1,12,48]{2,0,1:T(1,128)}, u32[]{:S(2)}) copy-start(s32[1,12,48]{2,0,1:T(1,128)} %param.8) | copy-start | bytes 6916
  12.5 10.9 %copy-start.1 = (s32[1,12,48]{2,0,1:T(1,128)S(1)}, s32[1,12,48]{2,0,1:T(1,128)}, u32[]{:S(2)}) copy-start(s32[1,12,48]{2,0,1:T(1,128)} %param.7) | copy-start | bytes 6916
  12.5 12.0 %copy-start.2 = (s32[1,12]{1,0:T(1,128)S(1)}, s32[1,12]{1,0:T(1,128)}, u32[]{:S(2)}) copy-start(s32[1,12]{1,0:T(1,128)} %param.9) | copy-start | bytes 148
  12.5 59.2 %all-to-all-start = ((bf16[32,6,4096]{2,1,0:T(8,128)(2,1)}), bf16[32,6,4096]{2,1,0:T(8,128)(2,1)}, u32[]{:S(2)}, u32[]{:S(2)}) async-start(bf16[32,6,4096]{2,1,0:T(8,128)(2,1)} %broadcast_select_fusion), calls=%async_computation | async-start | bytes 4194304 | tf_op jit(solution)/shard_map/all_to_all | solution.py:87

commit v4 on v2

--- a/solution.py
+++ b/solution.py
@@ -73,24 +73,26 @@
     whitened = normalize(record)
     local_stations, comp_count, window_count, window_len = whitened.shape
     owners = lax.axis_size("pairs")
-    tm_count = lax.axis_size("tm")
+    chips = lax.axis_size("z")
+    cores = lax.axis_size("c")
+    tm_count = chips * cores
     capacity = requested.shape[2]
     per_trace = partners.shape[2]
     trace_count = local_stations * comp_count
     own_index = lax.axis_index("pairs")
-    slot_ids = partners[0]
-    comp_ids = codes[0]
     mine = flip_lanes(whitened).reshape(local_stations, comp_count * window_count * window_len)
-    asked_of_me = lax.dynamic_index_in_dim(requested, own_index, axis=1, keepdims=False)
-    outgoing = jnp.take(mine, asked_of_me.reshape(-1), axis=0)
-    outgoing = outgoing.reshape(owners, capacity * comp_count, window_count * window_len)
+    asked_of_me = lax.dynamic_index_in_dim(requested, own_index, axis=1, keepdims=False).reshape(-1)
+    pick_send = (asked_of_me[:, None] == jnp.arange(local_stations, dtype=jnp.int32)[None, :])
+    outgoing = jnp.dot(pick_send.astype(jnp.bfloat16), mine, preferred_element_type=jnp.float32)
+    outgoing = outgoing.astype(jnp.bfloat16).reshape(owners, capacity * comp_count, window_count * window_len)
     arrived = lax.all_to_all(outgoing, "pairs", 0, 0, tiled=True)
     trace_pool = arrived.reshape(owners * capacity * comp_count, window_count * window_len)
-    row_ids = slot_ids * comp_count + comp_ids
-    picked = jnp.take(trace_pool, row_ids.reshape(-1), axis=0)
-    live_rows = jnp.arange(per_trace, dtype=jnp.int32)[None, :] < counts[0][:, None]
-    picked = jnp.where(live_rows.reshape(-1)[:, None], picked, jnp.zeros((), jnp.bfloat16))
-    picked = picked.reshape(trace_count, per_trace, window_len)
+    row_ids = (partners[0] * comp_count + codes[0]).reshape(-1)
+    live_rows = (jnp.arange(per_trace, dtype=jnp.int32)[None, :] < counts[0][:, None]).reshape(-1)
+    pool_rows = owners * capacity * comp_count
+    pick_recv = (row_ids[:, None] == jnp.arange(pool_rows, dtype=jnp.int32)[None, :]) & live_rows[:, None]
+    picked = jnp.dot(pick_recv.astype(jnp.bfloat16), trace_pool, preferred_element_type=jnp.float32)
+    picked = picked.astype(jnp.bfloat16).reshape(trace_count, per_trace, window_len)
     half = LAGS // 2
     own = whitened.reshape(trace_count, window_len).astype(jnp.float32)
     span = ((window_len + LAGS + LANE - 1) // LANE) * LANE
@@ -98,22 +100,33 @@
     total_windows = window_count * tm_count
     scale = 1.0 / math.sqrt(window_len * total_windows)
     lagged = correlate(src, picked, scale)
-    lagged = lagged.reshape(tm_count, trace_count * per_trace // tm_count, LAGS)
-    out = lax.psum_scatter(lagged, "tm", scatter_dimension=0, tiled=True)
-    return out.reshape(1, trace_count * per_trace // tm_count, LAGS)
+    block_rows = trace_count * per_trace // tm_count
+    lagged = lagged.reshape(chips, cores, block_rows, LAGS)
+    core = lax.axis_index("c")
+    kept = lax.dynamic_index_in_dim(lagged, core, axis=1, keepdims=False)
+    given = lax.dynamic_index_in_dim(lagged, cores - 1 - core, axis=1, keepdims=False)
+    got = lax.ppermute(given, "c", [(0, 1), (1, 0)])
+    chip_sums = (kept + got).astype(jnp.bfloat16)
+    arrived_sums = lax.all_to_all(chip_sums, "z", 0, 0, tiled=True)
+    return jnp.sum(arrived_sums.astype(jnp.float32), axis=0, keepdims=True)
 
 
 def solution(mesh):
+    tm_count = mesh.shape["tm"]
+    split = jax.sharding.Mesh(
+        mesh.devices.reshape(tm_count // 2, 2, mesh.shape["pairs"]), ("z", "c", "pairs")
+    )
+    tm = ("z", "c")
     return jax.shard_map(
         shards,
-        mesh=mesh,
+        mesh=split,
         in_specs=(
-            P("pairs", None, "tm", None),
+            P("pairs", None, tm, None),
             P(),
             P("pairs", None, None),
             P("pairs", None, None),
             P("pairs", None),
         ),
-        out_specs=P("pairs", "tm", None),
+        out_specs=P("pairs", tm, None),
         check_vma=False,
     )

time: 182 us -> 128 us (0.70)
  waiting for transfers between devices: 110 us -> 49.6 us
  blocking collectives: 0 us -> 29.3 us
  between operations: 13.5 us -> 0.14 us
  local copies, waits for them, and re-layouts: 21.2 us -> 9.84 us
  other arithmetic: 10 us -> 4.2 us
  matrix products: 0 us -> 5.58 us
  starting transfers between devices: 10.8 us -> 15.2 us
    reduce_scatter x1 -> x0, waiting for transfers between devices: 63.5 us -> none  [shards(): out = lax.psum_scatter(lagged, 'tm', scatter_dimension=0, tiled=True)]
    all_to_all x0 -> x1, blocking collectives: none -> 29.3 us  [shards(): arrived_sums = lax.all_to_all(chip_sums, 'z', 0, 0, tiled=True)]
    gather x3 -> x0, local copies, waits for them, and re-layouts: 10.9 us -> none  [the longest x2 5.59 us: shards(): outgoing = jnp.take(mine, asked_of_me.reshape(-1), axis=0)]
    select_n x4 -> x0, other arithmetic: 6.71 us -> none  [the longest x1 5.1 us: shards(): jnp.where(live_rows.reshape(-1)[:, None], picked, jnp.zeros((), jnp.bfloa...]
    dot_general x0 -> x2, matrix products: none -> 5.58 us  [the longest x1 4.97 us: shards(): jnp.dot(pick_recv.astype(jnp.bfloat16), trace_pool, preferred_element_typ...]
    ppermute x0 -> x1, starting transfers between devices: none -> 4.54 us  [shards(): got = lax.ppermute(given, 'c', [(0, 1), (1, 0)])]
    ppermute x0 -> x1, waiting for transfers between devices: none -> 2.45 us  [shards(): got = lax.ppermute(given, 'c', [(0, 1), (1, 0)])]
where the time goes in v4:
time: 128 us; the launch traced here: 127 us
  waiting for transfers between devices  49.6 us (39%)
  blocking collectives  29.3 us (23%)
  starting transfers between devices  15.2 us (12%)
  Pallas kernels  12.8 us (10%)
  local copies, waits for them, and re-layouts  9.84 us (8%)
  matrix products  5.58 us (4%)
  other arithmetic  4.2 us (3%)
    all_to_all x1, waiting for transfers between devices, shards(): arrived = lax.all_to_all(outgoing, 'pairs', 0, 0, tiled=True)  47.1 us
    all_to_all x1, blocking collectives, shards(): arrived_sums = lax.all_to_all(chip_sums, 'z', 0, 0, tiled=True)  29.3 us
    pallas_call x1, Pallas kernels, correlate(): pl.pallas_call(lambda s, p, o: corr_kernel(s, p, o, win=win, scale=scale)...  12.8 us
    all_to_all x1, starting transfers between devices, shards(): arrived = lax.all_to_all(outgoing, 'pairs', 0, 0, tiled=True)  10.6 us
    dot_general x1, matrix products, shards(): jnp.dot(pick_recv.astype(jnp.bfloat16), trace_pool, preferred_element_typ...  4.97 us
    ppermute x1, starting transfers between devices, shards(): got = lax.ppermute(given, 'c', [(0, 1), (1, 0)])  4.54 us
  transfers between devices with their start and end apart: 2, of which 2 were waited for; matrix products, arithmetic and copies ran while one was open for 1% of the time, Pallas kernels for 0%

profile of v4, /device:TPU:1, one launch (start us, length us, event | category | flops | bytes accessed | tf_op | source)
XLA Modules:
  0.0 126.6 jit_solution(15646494231944545342)
XLA Ops:
  0.0 0.0 copy-start
  0.0 1.0 convert_reduce_fusion.1
  1.0 1.1 fusion.7
  2.2 1.0 fusion.8
  3.2 0.1 reshape.77
  3.3 0.1 rev.3
  3.5 0.0 copy-done
  3.5 0.7 dynamic-slice_reduce_fusion
  4.2 0.1 eq.31
  4.3 0.6 convolution_convert_fusion
  4.9 2.3 %reshape.78 = bf16[32,6,4096]{2,1,0:T(8,128)(2,1)} reshape(bf16[64,12288]{1,0:T(8,128)(2,1)S(1)} %convolution_convert_fusion) | data formatting | bytes 3145728 | tf_op jit(solution)/shard_map/reshape | solution.py:87
  7.3 10.6 %all-to-all-start = ((bf16[32,6,4096]{2,1,0:T(8,128)(2,1)}), bf16[32,6,4096]{2,1,0:T(8,128)(2,1)S(1)}, u32[]{:S(2)}, u32[]{:S(2)}) async-start(bf16[32,6,4096]{2,1,0:T(8,128)(2,1)} %reshape.78), calls=%async_computation | async-start | bytes 4194304 | tf_op jit(solution)/shard_map/all_to_all | solution.py:88
  17.9 0.1 copy.15
  18.0 0.1 convert_element_type.28
  18.1 0.9 reshape.83.s
  19.0 0.1 add.37
  19.1 0.1 iota_compare_fusion.3
  19.2 0.1 lt.37
  19.3 47.1 %all-to-all-done = bf16[32,6,4096]{2,1,0:T(8,128)(2,1)S(1)} async-done(((bf16[32,6,4096]{2,1,0:T(8,128)(2,1)}), bf16[32,6,4096]{2,1,0:T(8,128)(2,1)S(1)}, u32[]{:S(2)}, u32[]{:S(2)}) %all-to-all-start) | async-done | bytes 1572896 | tf_op jit(solution)/shard_map/all_to_all | solution.py:88
  66.4 1.5 %reshape.79 = bf16[192,4096]{1,0:T(8,128)(2,1)} reshape(bf16[32,6,4096]{2,1,0:T(8,128)(2,1)S(1)} %all-to-all-done) | data formatting | bytes 3145728 | tf_op jit(solution)/shard_map/reshape | solution.py:89
  67.8 5.0 %convolution_convert_fusion.1 = bf16[576,4096]{1,0:T(8,128)(2,1)} fusion(bf16[192,4096]{1,0:T(8,128)(2,1)} %reshape.79, s32[576]{0:T(1024)S(1)} %add.37, pred[576]{0:T(1024)(128)(4,1)S(1)} %lt.37), kind=kOutput, calls=%fused_computation.1 | convolution fusion | flops 908550144 | bytes 6294336 | tf_op jit(solution)/shard_map/dot_general | solution.py:94
  72.8 12.8 %xcorr.1 = f32[12,48,1024]{2,1,0:T(8,128)} custom-call(f32[12,1,5120]{2,1,0:T(1,128)} %reshape.83.s, bf16[12,48,4096]{2,1,0:T(8,128)(2,1)} %bitcast.19), custom_call_target="tpu_custom_call" | custom-call | flops 4831838208 | bytes 7323648 | tf_op jit(solution)/shard_map/xcorr/pallas_call | solution.py:55
  85.6 1.8 %reshape.81 = f32[8,2,36,1024]{3,2,1,0:T(8,128)S(1)} reshape(f32[12,48,1024]{2,1,0:T(8,128)} %xcorr.1) | data formatting | bytes 4718592 | tf_op jit(solution)/shard_map/reshape | solution.py:104
  87.3 0.2 constant_dynamic-slice_fusion.1
  87.5 0.7 copy.22
  88.2 4.5 %collective-permute-start = (f32[8,36,1024]{2,0,1:T(8,128)S(1)}, f32[8,36,1024]{2,0,1:T(8,128)S(1)}, u32[]{:S(2)}, u32[]{:S(2)}) collective-permute-start(f32[8,36,1024]{2,0,1:T(8,128)S(1)} %bitcast.20), channel_id=1, source_target_pairs={{0,32},{32,0},{1,33},{33,1},{2,34},{34,2},{3,35},{35,3},{4,36},{36... | collective-permute-start | bytes 3538952 | tf_op jit(solution)/shard_map/ppermute | solution.py:108
  92.8 2.5 %collective-permute-done = f32[8,36,1024]{2,0,1:T(8,128)S(1)} collective-permute-done((f32[8,36,1024]{2,0,1:T(8,128)S(1)}, f32[8,36,1024]{2,0,1:T(8,128)S(1)}, u32[]{:S(2)}, u32[]{:S(2)}) %collective-permute-start) | collective-permute-done | bytes 1179680 | tf_op jit(solution)/shard_map/ppermute | solution.py:108
  95.2 0.8 fusion
  96.0 0.3 copy.19
  96.4 29.3 %all_to_all.10 = bf16[8,36,1024]{2,1,0:T(8,128)(2,1)S(1)} all-to-all(bf16[8,36,1024]{2,1,0:T(8,128)(2,1)S(1)} %copy.19), channel_id=1, replica_groups=mesh['z'=8,'c'=2,'pairs'=32] {'z'}, dimensions={0} | all-to-all | bytes 1179648 | tf_op jit(solution)/shard_map/all_to_all | solution.py:110
  125.7 0.1 convert_reduce_fusion
  125.8 0.8 broadcast_in_dim.2
  (12 shorter events, 0.1 us)
Async XLA Ops:
  0.0 3.5 %copy-start = (s32[32,32,2]{1,2,0:T(2,128)S(1)}, s32[32,32,2]{1,2,0:T(2,128)}, u32[]{:S(2)}) copy-start(s32[32,32,2]{1,2,0:T(2,128)} %param.6) | copy-start | bytes 24580
  7.2 11.8 %copy-start.1 = (s32[1,12,48]{2,0,1:T(1,128)S(1)}, s32[1,12,48]{2,0,1:T(1,128)}, u32[]{:S(2)}) copy-start(s32[1,12,48]{2,0,1:T(1,128)} %param.8) | copy-start | bytes 6916
  7.3 11.8 %copy-start.2 = (s32[1,12,48]{2,0,1:T(1,128)S(1)}, s32[1,12,48]{2,0,1:T(1,128)}, u32[]{:S(2)}) copy-start(s32[1,12,48]{2,0,1:T(1,128)} %param.7) | copy-start | bytes 6916
  7.3 11.9 %copy-start.3 = (s32[1,12]{1,0:T(1,128)S(1)}, s32[1,12]{1,0:T(1,128)}, u32[]{:S(2)}) copy-start(s32[1,12]{1,0:T(1,128)} %param.9) | copy-start | bytes 148
  7.3 59.1 %all-to-all-start = ((bf16[32,6,4096]{2,1,0:T(8,128)(2,1)}), bf16[32,6,4096]{2,1,0:T(8,128)(2,1)S(1)}, u32[]{:S(2)}, u32[]{:S(2)}) async-start(bf16[32,6,4096]{2,1,0:T(8,128)(2,1)} %reshape.78), calls=%async_computation | async-start | bytes 4194304 | tf_op jit(solution)/shard_map/all_to_all | solution.py:88
  88.2 7.0 %collective-permute-start = (f32[8,36,1024]{2,0,1:T(8,128)S(1)}, f32[8,36,1024]{2,0,1:T(8,128)S(1)}, u32[]{:S(2)}, u32[]{:S(2)}) collective-permute-start(f32[8,36,1024]{2,0,1:T(8,128)S(1)} %bitcast.20), channel_id=1, source_target_pairs={{0,32},{32,0},{1,33},{33,1},{2,34},{34,2},{3,35},{35,3},{4,36},{36... | collective-permute-start | bytes 3538952 | tf_op jit(solution)/shard_map/ppermute | solution.py:108

commit v5 on v4

--- a/solution.py
+++ b/solution.py
@@ -84,7 +84,8 @@
     asked_of_me = lax.dynamic_index_in_dim(requested, own_index, axis=1, keepdims=False).reshape(-1)
     pick_send = (asked_of_me[:, None] == jnp.arange(local_stations, dtype=jnp.int32)[None, :])
     outgoing = jnp.dot(pick_send.astype(jnp.bfloat16), mine, preferred_element_type=jnp.float32)
-    outgoing = outgoing.astype(jnp.bfloat16).reshape(owners, capacity * comp_count, window_count * window_len)
+    per_owner = capacity * comp_count * window_count * window_len
+    outgoing = outgoing.astype(jnp.bfloat16).reshape(owners, 8, per_owner // 8)
     arrived = lax.all_to_all(outgoing, "pairs", 0, 0, tiled=True)
     trace_pool = arrived.reshape(owners * capacity * comp_count, window_count * window_len)
     row_ids = (partners[0] * comp_count + codes[0]).reshape(-1)
@@ -106,9 +107,10 @@
     kept = lax.dynamic_index_in_dim(lagged, core, axis=1, keepdims=False)
     given = lax.dynamic_index_in_dim(lagged, cores - 1 - core, axis=1, keepdims=False)
     got = lax.ppermute(given, "c", [(0, 1), (1, 0)])
-    chip_sums = (kept + got).astype(jnp.bfloat16)
+    chip_sums = (kept + got).astype(jnp.bfloat16).reshape(chips, 32, block_rows * LAGS // 32)
     arrived_sums = lax.all_to_all(chip_sums, "z", 0, 0, tiled=True)
-    return jnp.sum(arrived_sums.astype(jnp.float32), axis=0, keepdims=True)
+    total = jnp.sum(arrived_sums.astype(jnp.float32), axis=0)
+    return total.reshape(1, block_rows, LAGS)
 
 
 def solution(mesh):

time: 128 us -> 115 us (0.90)
  waiting for transfers between devices: 49.6 us -> 38.9 us
  matrix products: 5.58 us -> 4.17 us
    all_to_all x1, waiting for transfers between devices: 47.1 us -> 36.5 us  [shards(): arrived = lax.all_to_all(outgoing, 'pairs', 0, 0, tiled=True)]
    dot_general x1, matrix products: 4.97 us -> 3.57 us  [shards(): jnp.dot(pick_recv.astype(jnp.bfloat16), trace_pool, preferred_element_typ...]
    reshape x1 -> x3, local copies, waits for them, and re-layouts: 2.33 us -> 3.67 us  [the longest x1 2.23 us: shards(): outgoing = outgoing.astype(jnp.bfloat16).reshape(owners, 8, per_owner // 8)]
where the time goes in v5:
time: 115 us; the launch traced here: 113 us
  waiting for transfers between devices  38.9 us (34%)
  blocking collectives  28.2 us (25%)
  starting transfers between devices  14.7 us (13%)
  Pallas kernels  12.8 us (11%)
  local copies, waits for them, and re-layouts  10.3 us (9%)
  other arithmetic  4.17 us (4%)
  matrix products  4.17 us (4%)
    all_to_all x1, waiting for transfers between devices, shards(): arrived = lax.all_to_all(outgoing, 'pairs', 0, 0, tiled=True)  36.5 us
    all_to_all x1, blocking collectives, shards(): arrived_sums = lax.all_to_all(chip_sums, 'z', 0, 0, tiled=True)  28.2 us
    pallas_call x1, Pallas kernels, correlate(): pl.pallas_call(lambda s, p, o: corr_kernel(s, p, o, win=win, scale=scale)...  12.8 us
    all_to_all x1, starting transfers between devices, shards(): arrived = lax.all_to_all(outgoing, 'pairs', 0, 0, tiled=True)  10.6 us
    ppermute x1, starting transfers between devices, shards(): got = lax.ppermute(given, 'c', [(0, 1), (1, 0)])  4.11 us
    dot_general x1, matrix products, shards(): jnp.dot(pick_recv.astype(jnp.bfloat16), trace_pool, preferred_element_typ...  3.57 us
    ppermute x1, waiting for transfers between devices, shards(): got = lax.ppermute(given, 'c', [(0, 1), (1, 0)])  2.45 us
  transfers between devices with their start and end apart: 2, of which 2 were waited for; matrix products, arithmetic and copies ran while one was open for 1% of the time, Pallas kernels for 0%

profile of v5, /device:TPU:1, one launch (start us, length us, event | category | flops | bytes accessed | tf_op | source)
XLA Modules:
  0.0 113.5 jit_solution(1356729479122939647)
XLA Ops:
  0.0 0.0 copy-start
  0.0 1.0 convert_reduce_fusion.1
  1.0 1.1 fusion.7
  2.2 1.0 fusion.8
  3.2 0.1 reshape.83
  3.3 0.1 rev.3
  3.5 0.7 dynamic-slice_reduce_fusion
  4.2 0.1 eq.31
  4.3 0.6 convolution_convert_fusion
  4.9 2.2 %reshape.84 = bf16[32,8,3072]{2,1,0:T(8,128)(2,1)} reshape(bf16[64,12288]{1,0:T(8,128)(2,1)S(1)} %convolution_convert_fusion) | data formatting | bytes 3145728 | tf_op jit(solution)/shard_map/reshape | solution.py:88
  7.1 10.6 %all-to-all-start = ((bf16[32,8,3072]{2,1,0:T(8,128)(2,1)}), bf16[32,8,3072]{2,1,0:T(8,128)(2,1)S(1)}, u32[]{:S(2)}, u32[]{:S(2)}) async-start(bf16[32,8,3072]{2,1,0:T(8,128)(2,1)} %reshape.84), calls=%async_computation | async-start | bytes 3145728 | tf_op jit(solution)/shard_map/all_to_all | solution.py:89
  17.8 0.1 copy.12
  17.9 0.1 convert_element_type.28
  18.0 0.9 reshape.91.s
  18.9 0.1 add.37
  19.0 0.1 iota_compare_fusion.3
  19.1 0.1 lt.37
  19.2 36.5 %all-to-all-done = bf16[32,8,3072]{2,1,0:T(8,128)(2,1)S(1)} async-done(((bf16[32,8,3072]{2,1,0:T(8,128)(2,1)}), bf16[32,8,3072]{2,1,0:T(8,128)(2,1)S(1)}, u32[]{:S(2)}, u32[]{:S(2)}) %all-to-all-start) | async-done | bytes 1572896 | tf_op jit(solution)/shard_map/all_to_all | solution.py:89
  55.7 1.4 %reshape.85 = bf16[192,4096]{1,0:T(8,128)(2,1)S(1)} reshape(bf16[32,8,3072]{2,1,0:T(8,128)(2,1)S(1)} %all-to-all-done) | data formatting | bytes 3145728 | tf_op jit(solution)/shard_map/reshape | solution.py:90
  57.0 3.6 %convolution_convert_fusion.1 = bf16[576,4096]{1,0:T(8,128)(2,1)} fusion(bf16[192,4096]{1,0:T(8,128)(2,1)S(1)} %reshape.85, s32[576]{0:T(1024)S(1)} %add.37, pred[576]{0:T(1024)(128)(4,1)S(1)} %lt.37), kind=kOutput, calls=%fused_computation.1 | convolution fusion | flops 908550144 | bytes 6294336 | tf_op jit(solution)/shard_map/dot_general | solution.py:95
  60.6 12.8 %xcorr.1 = f32[12,48,1024]{2,1,0:T(8,128)} custom-call(f32[12,1,5120]{2,1,0:T(1,128)} %reshape.91.s, bf16[12,48,4096]{2,1,0:T(8,128)(2,1)} %bitcast.19), custom_call_target="tpu_custom_call" | custom-call | flops 4831838208 | bytes 7323648 | tf_op jit(solution)/shard_map/xcorr/pallas_call | solution.py:55
  73.3 1.8 %reshape.87 = f32[8,2,36,1024]{3,2,1,0:T(8,128)S(1)} reshape(f32[12,48,1024]{2,1,0:T(8,128)} %xcorr.1) | data formatting | bytes 4718592 | tf_op jit(solution)/shard_map/reshape | solution.py:105
  75.1 0.2 constant_dynamic-slice_fusion.1
  75.3 0.7 copy.19
  76.0 4.1 %collective-permute-start = (f32[8,36,1024]{2,0,1:T(8,128)S(1)}, f32[8,36,1024]{2,0,1:T(8,128)S(1)}, u32[]{:S(2)}, u32[]{:S(2)}) collective-permute-start(f32[8,36,1024]{2,0,1:T(8,128)S(1)} %bitcast.20), channel_id=1, source_target_pairs={{0,32},{32,0},{1,33},{33,1},{2,34},{34,2},{3,35},{35,3},{4,36},{36... | collective-permute-start | bytes 3538952 | tf_op jit(solution)/shard_map/ppermute | solution.py:109
  80.1 2.5 %collective-permute-done = f32[8,36,1024]{2,0,1:T(8,128)S(1)} collective-permute-done((f32[8,36,1024]{2,0,1:T(8,128)S(1)}, f32[8,36,1024]{2,0,1:T(8,128)S(1)}, u32[]{:S(2)}, u32[]{:S(2)}) %collective-permute-start) | collective-permute-done | bytes 1179680 | tf_op jit(solution)/shard_map/ppermute | solution.py:109
  82.6 0.8 fusion
  83.4 0.3 copy.16
  83.7 0.6 reshape.88
  84.4 28.2 %all_to_all.10 = bf16[8,32,1152]{2,1,0:T(8,128)(2,1)S(1)} all-to-all(bf16[8,32,1152]{2,1,0:T(8,128)(2,1)S(1)} %reshape.88), channel_id=1, replica_groups=mesh['z'=8,'c'=2,'pairs'=32] {'z'}, dimensions={0} | all-to-all | bytes 1179648 | tf_op jit(solution)/shard_map/all_to_all | solution.py:111
  112.6 0.1 convert_reduce_fusion
  112.7 0.8 reshape.89
  (13 shorter events, 0.1 us)
Async XLA Ops:
  0.0 3.5 %copy-start = (s32[32,32,2]{1,2,0:T(2,128)S(1)}, s32[32,32,2]{1,2,0:T(2,128)}, u32[]{:S(2)}) copy-start(s32[32,32,2]{1,2,0:T(2,128)} %param.6) | copy-start | bytes 24580
  7.1 11.8 %copy-start.1 = (s32[1,12,48]{2,0,1:T(1,128)S(1)}, s32[1,12,48]{2,0,1:T(1,128)}, u32[]{:S(2)}) copy-start(s32[1,12,48]{2,0,1:T(1,128)} %param.8) | copy-start | bytes 6916
  7.1 11.8 %copy-start.2 = (s32[1,12,48]{2,0,1:T(1,128)S(1)}, s32[1,12,48]{2,0,1:T(1,128)}, u32[]{:S(2)}) copy-start(s32[1,12,48]{2,0,1:T(1,128)} %param.7) | copy-start | bytes 6916
  7.1 11.9 %copy-start.3 = (s32[1,12]{1,0:T(1,128)S(1)}, s32[1,12]{1,0:T(1,128)}, u32[]{:S(2)}) copy-start(s32[1,12]{1,0:T(1,128)} %param.9) | copy-start | bytes 148
  7.1 48.5 %all-to-all-start = ((bf16[32,8,3072]{2,1,0:T(8,128)(2,1)}), bf16[32,8,3072]{2,1,0:T(8,128)(2,1)S(1)}, u32[]{:S(2)}, u32[]{:S(2)}) async-start(bf16[32,8,3072]{2,1,0:T(8,128)(2,1)} %reshape.84), calls=%async_computation | async-start | bytes 3145728 | tf_op jit(solution)/shard_map/all_to_all | solution.py:89
  76.0 6.6 %collective-permute-start = (f32[8,36,1024]{2,0,1:T(8,128)S(1)}, f32[8,36,1024]{2,0,1:T(8,128)S(1)}, u32[]{:S(2)}, u32[]{:S(2)}) collective-permute-start(f32[8,36,1024]{2,0,1:T(8,128)S(1)} %bitcast.20), channel_id=1, source_target_pairs={{0,32},{32,0},{1,33},{33,1},{2,34},{34,2},{3,35},{35,3},{4,36},{36... | collective-permute-start | bytes 3538952 | tf_op jit(solution)/shard_map/ppermute | solution.py:109

commit v6 on v5

--- a/solution.py
+++ b/solution.py
@@ -25,14 +25,13 @@
     return grouped[..., ::-1].reshape(shape)
 
 
-def corr_kernel(src_ref, p_ref, o_ref, *, win, scale):
-    rows = p_ref.shape[1]
-    span = src_ref.shape[2]
+def trace_corr(src_row, p_ref, u, rows, win):
+    span = src_row.shape[1]
     m_blocks = win // BLK
     o_blocks = LAGS // BLK
     d_blocks = m_blocks + o_blocks - 1
     width = BLK * (d_blocks - 1) + BLK + LANE
-    wide = jnp.broadcast_to(src_ref[0], (LANE, span))
+    wide = jnp.broadcast_to(src_row, (LANE, span))
     hank = pltpu.roll(wide, span - (LANE - 1), 1, stride=1, stride_axis=0)
     hank = hank[:, :width].astype(jnp.bfloat16)
     acc = [jnp.zeros((rows, BLK), jnp.float32) for _ in range(o_blocks)]
@@ -41,26 +40,45 @@
             [hank[:, BLK * d: BLK * d + BLK], hank[:, BLK * d + LANE: BLK * d + LANE + BLK]], axis=0
         )
         lags = [o for o in range(o_blocks) if 0 <= d - o < m_blocks]
-        lhs = jnp.concatenate([p_ref[0, :, BLK * (d - o): BLK * (d - o) + BLK] for o in lags], axis=0)
+        lhs = jnp.concatenate([p_ref[u, :, BLK * (d - o): BLK * (d - o) + BLK] for o in lags], axis=0)
         res = jnp.dot(lhs, rhs, preferred_element_type=jnp.float32)
         for k, o in enumerate(lags):
             acc[o] = acc[o] + res[rows * k: rows * (k + 1)]
-    o_ref[0] = jnp.concatenate(acc, axis=1) * scale
+    return jnp.concatenate(acc, axis=1)
 
 
-def correlate(src, partner_rows, scale):
+def corr_kernel(src_ref, p_ref, o_ref, *, win, scale, block_rows):
+    group, rows = p_ref.shape[0], p_ref.shape[1]
+    pad = o_ref.shape[1] - block_rows
+    if pad:
+        for blk in range(o_ref.shape[0]):
+            o_ref[blk, block_rows:, :] = jnp.zeros((pad, LAGS), jnp.float32)
+    for u in range(group):
+        cc = trace_corr(src_ref[u], p_ref, u, rows, win) * scale
+        first = u * rows
+        while first < (u + 1) * rows:
+            blk, at = divmod(first, block_rows)
+            take = min(block_rows - at, (u + 1) * rows - first)
+            o_ref[blk, at: at + take, :] = cc[first - u * rows: first - u * rows + take]
+            first += take
+
+
+def correlate(src, partner_rows, scale, block_rows):
     traces, rows, win = partner_rows.shape
     span = src.shape[-1]
+    group = block_rows // math.gcd(block_rows, rows)
+    blocks = group * rows // block_rows
+    padded = -(-block_rows // 8) * 8
     flops = 2 * traces * rows * win * LAGS
     return pl.pallas_call(
-        lambda s, p, o: corr_kernel(s, p, o, win=win, scale=scale),
-        grid=(traces,),
+        lambda s, p, o: corr_kernel(s, p, o, win=win, scale=scale, block_rows=block_rows),
+        grid=(traces // group,),
         in_specs=[
-            pl.BlockSpec((1, 1, span), lambda j: (j, 0, 0)),
-            pl.BlockSpec((1, rows, win), lambda j: (j, 0, 0)),
+            pl.BlockSpec((group, 1, span), lambda g: (g, 0, 0)),
+            pl.BlockSpec((group, rows, win), lambda g: (g, 0, 0)),
         ],
-        out_specs=pl.BlockSpec((1, rows, LAGS), lambda j: (j, 0, 0)),
-        out_shape=jax.ShapeDtypeStruct((traces, rows, LAGS), jnp.float32),
+        out_specs=pl.BlockSpec((blocks, padded, LAGS), lambda g: (g, 0, 0)),
+        out_shape=jax.ShapeDtypeStruct((traces * rows // block_rows, padded, LAGS), jnp.float32),
         cost_estimate=pl.CostEstimate(
             flops=flops, transcendentals=0,
             bytes_accessed=traces * (rows * win * 2 + span * 4 + rows * LAGS * 4),
@@ -80,12 +98,13 @@
     per_trace = partners.shape[2]
     trace_count = local_stations * comp_count
     own_index = lax.axis_index("pairs")
-    mine = flip_lanes(whitened).reshape(local_stations, comp_count * window_count * window_len)
-    asked_of_me = lax.dynamic_index_in_dim(requested, own_index, axis=1, keepdims=False).reshape(-1)
-    pick_send = (asked_of_me[:, None] == jnp.arange(local_stations, dtype=jnp.int32)[None, :])
-    outgoing = jnp.dot(pick_send.astype(jnp.bfloat16), mine, preferred_element_type=jnp.float32)
-    per_owner = capacity * comp_count * window_count * window_len
-    outgoing = outgoing.astype(jnp.bfloat16).reshape(owners, 8, per_owner // 8)
+    per_station = comp_count * window_count * window_len
+    mine = flip_lanes(whitened).reshape(local_stations, 8, per_station // 8)
+    asked_of_me = lax.dynamic_index_in_dim(requested, own_index, axis=1, keepdims=False)
+    pick_send = (asked_of_me[:, :, None] == jnp.arange(local_stations, dtype=jnp.int32)[None, None, :])
+    outgoing = jnp.einsum("eis,sru->eiru", pick_send.astype(jnp.bfloat16), mine,
+                          preferred_element_type=jnp.float32)
+    outgoing = outgoing.astype(jnp.bfloat16).reshape(owners, capacity * 8, per_station // 8)
     arrived = lax.all_to_all(outgoing, "pairs", 0, 0, tiled=True)
     trace_pool = arrived.reshape(owners * capacity * comp_count, window_count * window_len)
     row_ids = (partners[0] * comp_count + codes[0]).reshape(-1)
@@ -100,14 +119,14 @@
     src = jnp.pad(own, ((0, 0), (half, span - window_len - half)))
     total_windows = window_count * tm_count
     scale = 1.0 / math.sqrt(window_len * total_windows)
-    lagged = correlate(src, picked, scale)
     block_rows = trace_count * per_trace // tm_count
-    lagged = lagged.reshape(chips, cores, block_rows, LAGS)
+    lagged = correlate(src, picked, scale, block_rows)
+    lagged = lagged.reshape(chips, cores, lagged.shape[1], LAGS)
     core = lax.axis_index("c")
     kept = lax.dynamic_index_in_dim(lagged, core, axis=1, keepdims=False)
     given = lax.dynamic_index_in_dim(lagged, cores - 1 - core, axis=1, keepdims=False)
     got = lax.ppermute(given, "c", [(0, 1), (1, 0)])
-    chip_sums = (kept + got).astype(jnp.bfloat16).reshape(chips, 32, block_rows * LAGS // 32)
+    chip_sums = (kept + got)[:, :block_rows].astype(jnp.bfloat16).reshape(chips, 32, block_rows * LAGS // 32)
     arrived_sums = lax.all_to_all(chip_sums, "z", 0, 0, tiled=True)
     total = jnp.sum(arrived_sums.astype(jnp.float32), axis=0)
     return total.reshape(1, block_rows, LAGS)

time: 115 us -> 110 us (0.957)
  Pallas kernels: 12.8 us -> 10.1 us
  local copies, waits for them, and re-layouts: 10.3 us -> 9 us
    pallas_call x1, Pallas kernels: 12.8 us -> 10.1 us  [correlate(): pl.pallas_call(lambda s, p, o: corr_kernel(s, p, o, win=win, scale=scale,...]
    reshape x3 -> x2, local copies, waits for them, and re-layouts: 4.63 us -> 2.66 us  [the longest x1 2.02 us: shards(): outgoing.astype(jnp.bfloat16)]
    squeeze x0 -> x1, local copies, waits for them, and re-layouts: none -> 1.89 us  [shards(): kept = lax.dynamic_index_in_dim(lagged, core, axis=1, keepdims=False)]
where the time goes in v6:
time: 110 us; the launch traced here: 109 us
  waiting for transfers between devices  39.1 us (36%)
  blocking collectives  28.2 us (26%)
  starting transfers between devices  14.7 us (13%)
  Pallas kernels  10.1 us (9%)
  local copies, waits for them, and re-layouts  9 us (8%)
  matrix products  4.22 us (4%)
  other arithmetic  3.64 us (3%)
    all_to_all x1, waiting for transfers between devices, shards(): arrived = lax.all_to_all(outgoing, 'pairs', 0, 0, tiled=True)  36.5 us
    all_to_all x1, blocking collectives, shards(): arrived_sums = lax.all_to_all(chip_sums, 'z', 0, 0, tiled=True)  28.2 us
    all_to_all x1, starting transfers between devices, shards(): arrived = lax.all_to_all(outgoing, 'pairs', 0, 0, tiled=True)  10.6 us
    pallas_call x1, Pallas kernels, correlate(): pl.pallas_call(lambda s, p, o: corr_kernel(s, p, o, win=win, scale=scale,...  10.1 us
    ppermute x1, starting transfers between devices, shards(): got = lax.ppermute(given, 'c', [(0, 1), (1, 0)])  4.11 us
    dot_general x1, matrix products, shards(): jnp.dot(pick_recv.astype(jnp.bfloat16), trace_pool, preferred_element_typ...  3.57 us
    ppermute x1, waiting for transfers between devices, shards(): got = lax.ppermute(given, 'c', [(0, 1), (1, 0)])  2.64 us
  transfers between devices with their start and end apart: 2, of which 2 were waited for; matrix products, arithmetic and copies ran while one was open for 1% of the time, Pallas kernels for 0%

profile of v6, /device:TPU:1, one launch (start us, length us, event | category | flops | bytes accessed | tf_op | source)
XLA Modules:
  0.0 109.2 jit_solution(17535094069982636793)
XLA Ops:
  0.0 0.0 copy-start
  0.0 1.0 convert_reduce_fusion.1
  1.0 1.1 %fusion.7 = f32[4,3]{0,1:T(4,128)S(1)} fusion(bf16[4,3,1,4096]{3,0,2,1:T(4,128)(2,1)} %param.5, f32[4,3]{0,1:T(4,128)S(1)} %broadcast_multiply_fusion), kind=kLoop, calls=%fused_computation.15 | loop fusion | flops 196596 | bytes 98400 | tf_op jit(solution)/shard_map/reduce_sum | solution.py:18
  2.2 1.0 fusion.8
  3.2 0.1 reshape.83
  3.3 0.1 rev.3
  3.4 0.1 reshape_reshape.3
  3.6 0.0 copy-done
  3.6 0.1 constant_dynamic-slice_fusion
  3.7 0.1 copy.9
  3.8 0.7 convolution_convert_fusion.1
  4.4 2.0 %copy.12 = bf16[32,16,1536]{2,1,0:T(8,128)(2,1)} copy(bf16[32,16,1536]{2,0,1:T(8,128)(2,1)S(1)} %bitcast.27) | data formatting | bytes 3145728 | tf_op jit(solution)/shard_map/reshape | solution.py:107
  6.5 10.6 %all-to-all-start = ((bf16[32,16,1536]{2,1,0:T(8,128)(2,1)}), bf16[32,16,1536]{2,1,0:T(8,128)(2,1)S(1)}, u32[]{:S(2)}, u32[]{:S(2)}) async-start(bf16[32,16,1536]{2,1,0:T(8,128)(2,1)} %copy.12), calls=%async_computation | async-start | bytes 3145728 | tf_op jit(solution)/shard_map/all_to_all | solution.py:108
  17.1 0.1 copy.8
  17.2 0.1 convert_element_type.26
  17.3 0.9 reshape.91.s
  18.2 0.0 copy-done.1
  18.2 0.1 add.37
  18.3 0.1 iota_compare_fusion.1
  18.4 0.1 lt.37
  18.5 36.5 %all-to-all-done = bf16[32,16,1536]{2,1,0:T(8,128)(2,1)S(1)} async-done(((bf16[32,16,1536]{2,1,0:T(8,128)(2,1)}), bf16[32,16,1536]{2,1,0:T(8,128)(2,1)S(1)}, u32[]{:S(2)}, u32[]{:S(2)}) %all-to-all-start) | async-done | bytes 1572896 | tf_op jit(solution)/shard_map/all_to_all | solution.py:108
  55.0 1.9 %reshape.85 = bf16[192,4096]{1,0:T(8,128)(2,1)S(1)} reshape(bf16[32,16,1536]{2,1,0:T(8,128)(2,1)S(1)} %all-to-all-done) | data formatting | bytes 3145728 | tf_op jit(solution)/shard_map/reshape | solution.py:109
  56.9 3.6 %convolution_convert_fusion = bf16[576,4096]{1,0:T(8,128)(2,1)} fusion(bf16[192,4096]{1,0:T(8,128)(2,1)S(1)} %reshape.85, s32[576]{0:T(1024)S(1)} %add.37, pred[576]{0:T(1024)(128)(4,1)S(1)} %lt.37), kind=kOutput, calls=%fused_computation | convolution fusion | flops 908550144 | bytes 6294336 | tf_op jit(solution)/shard_map/dot_general | solution.py:114
  60.4 10.1 %xcorr.1 = f32[16,40,1024]{2,1,0:T(8,128)} custom-call(f32[12,1,5120]{2,1,0:T(1,128)} %reshape.91.s, bf16[12,48,4096]{2,1,0:T(8,128)(2,1)} %bitcast.26), custom_call_target="tpu_custom_call" | custom-call | flops 4831838208 | bytes 7323648 | tf_op jit(solution)/shard_map/xcorr/pallas_call | solution.py:73
  70.5 1.9 %dynamic-slice_bitcast_fusion.1 = (f32[8,40,1024]{2,1,0:T(8,128)S(1)}, f32[8,40,1024]{2,1,0:T(8,128)S(1)}) fusion(f32[8,2,40,1024]{3,2,1,0:T(8,128)} %bitcast.28, s32[]{:T(128)S(6)} %select_n.12, s32[]{:T(128)S(6)} %select_n.13), kind=kLoop, calls=%fused_computation.5 | loop fusion | bytes 5242888 | tf_op jit(solution)/shard_map/jit(dynamic_index_in_dim)/squeeze | solution.py:126
  72.4 4.1 %collective-permute-start = (f32[8,40,1024]{2,1,0:T(8,128)S(1)}, f32[8,40,1024]{2,1,0:T(8,128)S(1)}, u32[]{:S(2)}, u32[]{:S(2)}) collective-permute-start(f32[8,40,1024]{2,1,0:T(8,128)S(1)} %get-tuple-element.6), channel_id=1, source_target_pairs={{0,32},{32,0},{1,33},{33,1},{2,34},{34,2},{3,35},{35,3},{4,36},{36... | collective-permute-start | bytes 3932168 | tf_op jit(solution)/shard_map/ppermute | solution.py:128
  76.5 2.6 %collective-permute-done = f32[8,40,1024]{2,1,0:T(8,128)S(1)} collective-permute-done((f32[8,40,1024]{2,1,0:T(8,128)S(1)}, f32[8,40,1024]{2,1,0:T(8,128)S(1)}, u32[]{:S(2)}, u32[]{:S(2)}) %collective-permute-start) | collective-permute-done | bytes 1310752 | tf_op jit(solution)/shard_map/ppermute | solution.py:128
  79.1 0.3 fusion
  79.4 0.6 reshape.88
  80.0 28.2 %all_to_all.10 = bf16[8,32,1152]{2,1,0:T(8,128)(2,1)S(1)} all-to-all(bf16[8,32,1152]{2,1,0:T(8,128)(2,1)S(1)} %reshape.88), channel_id=1, replica_groups=mesh['z'=8,'c'=2,'pairs'=32] {'z'}, dimensions={0} | all-to-all | bytes 1179648 | tf_op jit(solution)/shard_map/all_to_all | solution.py:130
  108.3 0.1 convert_reduce_fusion
  108.4 0.8 reshape.89
  (10 shorter events, 0.1 us)
Async XLA Ops:
  0.0 3.6 %copy-start = (s32[32,32,2]{1,2,0:T(2,128)S(1)}, s32[32,32,2]{1,2,0:T(2,128)}, u32[]{:S(2)}) copy-start(s32[32,32,2]{1,2,0:T(2,128)} %param.6) | copy-start | bytes 24580
  6.5 11.7 %copy-start.1 = (s32[1,12,48]{2,0,1:T(1,128)S(1)}, s32[1,12,48]{2,0,1:T(1,128)}, u32[]{:S(2)}) copy-start(s32[1,12,48]{2,0,1:T(1,128)} %param.8) | copy-start | bytes 6916
  6.5 11.7 %copy-start.2 = (s32[1,12,48]{2,0,1:T(1,128)S(1)}, s32[1,12,48]{2,0,1:T(1,128)}, u32[]{:S(2)}) copy-start(s32[1,12,48]{2,0,1:T(1,128)} %param.7) | copy-start | bytes 6916
  6.5 11.8 %copy-start.3 = (s32[1,12]{1,0:T(1,128)S(1)}, s32[1,12]{1,0:T(1,128)}, u32[]{:S(2)}) copy-start(s32[1,12]{1,0:T(1,128)} %param.9) | copy-start | bytes 148
  6.5 48.5 %all-to-all-start = ((bf16[32,16,1536]{2,1,0:T(8,128)(2,1)}), bf16[32,16,1536]{2,1,0:T(8,128)(2,1)S(1)}, u32[]{:S(2)}, u32[]{:S(2)}) async-start(bf16[32,16,1536]{2,1,0:T(8,128)(2,1)} %copy.12), calls=%async_computation | async-start | bytes 3145728 | tf_op jit(solution)/shard_map/all_to_all | solution.py:108
  72.4 6.8 %collective-permute-start = (f32[8,40,1024]{2,1,0:T(8,128)S(1)}, f32[8,40,1024]{2,1,0:T(8,128)S(1)}, u32[]{:S(2)}, u32[]{:S(2)}) collective-permute-start(f32[8,40,1024]{2,1,0:T(8,128)S(1)} %get-tuple-element.6), channel_id=1, source_target_pairs={{0,32},{32,0},{1,33},{33,1},{2,34},{34,2},{3,35},{35,3},{4,36},{36... | collective-permute-start | bytes 3932168 | tf_op jit(solution)/shard_map/ppermute | solution.py:128

commit v7 on v6

--- a/solution.py
+++ b/solution.py
@@ -66,7 +66,7 @@
 def correlate(src, partner_rows, scale, block_rows):
     traces, rows, win = partner_rows.shape
     span = src.shape[-1]
-    group = block_rows // math.gcd(block_rows, rows)
+    group = 2 * block_rows // math.gcd(block_rows, rows)
     blocks = group * rows // block_rows
     padded = -(-block_rows // 8) * 8
     flops = 2 * traces * rows * win * LAGS
@@ -101,10 +101,10 @@
     per_station = comp_count * window_count * window_len
     mine = flip_lanes(whitened).reshape(local_stations, 8, per_station // 8)
     asked_of_me = lax.dynamic_index_in_dim(requested, own_index, axis=1, keepdims=False)
-    pick_send = (asked_of_me[:, :, None] == jnp.arange(local_stations, dtype=jnp.int32)[None, None, :])
-    outgoing = jnp.einsum("eis,sru->eiru", pick_send.astype(jnp.bfloat16), mine,
-                          preferred_element_type=jnp.float32)
-    outgoing = outgoing.astype(jnp.bfloat16).reshape(owners, capacity * 8, per_station // 8)
+    outgoing = jnp.broadcast_to(mine[0], (owners, capacity) + mine.shape[1:])
+    for station in range(1, local_stations):
+        outgoing = jnp.where((asked_of_me == station)[:, :, None, None], mine[station], outgoing)
+    outgoing = outgoing.reshape(owners, capacity * 8, per_station // 8)
     arrived = lax.all_to_all(outgoing, "pairs", 0, 0, tiled=True)
     trace_pool = arrived.reshape(owners * capacity * comp_count, window_count * window_len)
     row_ids = (partners[0] * comp_count + codes[0]).reshape(-1)

time: 110 us -> 111 us (level)
  other arithmetic: 3.64 us -> 5.19 us
    reshape x3 -> x0, local copies, waits for them, and re-layouts: 2.14 us -> none  [the longest x1 2.02 us: shards(): outgoing.astype(jnp.bfloat16)]
    select_n x0 -> x1, other arithmetic: none -> 1.53 us  [shards(): jnp.where((asked_of_me == station)[:, :, None, None], mine[station], outg...]
where the time goes in v7:
time: 111 us; the launch traced here: 110 us
  waiting for transfers between devices  39.1 us (35%)
  blocking collectives  28.2 us (25%)
  starting transfers between devices  14.7 us (13%)
  Pallas kernels  10.3 us (9%)
  local copies, waits for them, and re-layouts  8.76 us (8%)
  other arithmetic  5.19 us (5%)
  matrix products  3.57 us (3%)
    all_to_all x1, waiting for transfers between devices, shards(): arrived = lax.all_to_all(outgoing, 'pairs', 0, 0, tiled=True)  36.5 us
    all_to_all x1, blocking collectives, shards(): arrived_sums = lax.all_to_all(chip_sums, 'z', 0, 0, tiled=True)  28.2 us
    all_to_all x1, starting transfers between devices, shards(): arrived = lax.all_to_all(outgoing, 'pairs', 0, 0, tiled=True)  10.6 us
    pallas_call x1, Pallas kernels, correlate(): pl.pallas_call(lambda s, p, o: corr_kernel(s, p, o, win=win, scale=scale,...  10.3 us
    ppermute x1, starting transfers between devices, shards(): got = lax.ppermute(given, 'c', [(0, 1), (1, 0)])  4.11 us
    dot_general x1, matrix products, shards(): jnp.dot(pick_recv.astype(jnp.bfloat16), trace_pool, preferred_element_typ...  3.57 us
    ppermute x1, waiting for transfers between devices, shards(): got = lax.ppermute(given, 'c', [(0, 1), (1, 0)])  2.64 us
  transfers between devices with their start and end apart: 2, of which 2 were waited for; matrix products, arithmetic and copies ran while one was open for 1% of the time, Pallas kernels for 0%

profile of v7, /device:TPU:1, one launch (start us, length us, event | category | flops | bytes accessed | tf_op | source)
XLA Modules:
  0.0 110.1 jit_solution(13282900080283002425)
XLA Ops:
  0.0 0.8 copy-done
  0.8 0.1 constant_dynamic-slice_fusion
  0.9 0.1 copy.25
  1.0 0.1 copy.23
  1.1 0.1 copy.24
  1.2 1.0 convert_reduce_fusion.1
  2.2 1.1 %fusion.7 = f32[4,3]{0,1:T(4,128)S(1)} fusion(bf16[4,3,1,4096]{3,0,2,1:T(4,128)(2,1)} %param.5, f32[4,3]{0,1:T(4,128)S(1)} %broadcast_multiply_fusion), kind=kLoop, calls=%fused_computation.15 | loop fusion | flops 196596 | bytes 98400 | tf_op jit(solution)/shard_map/reduce_sum | solution.py:18
  3.3 1.0 fusion.8
  4.3 0.5 slice_reduce_fusion.3
  4.8 0.1 slice.52
  5.0 0.1 slice.55
  5.2 0.1 slice.46
  5.3 0.1 slice.49
  5.5 0.1 copy.22
  5.6 1.5 %select_select_fusion = bf16[32,16,1536]{2,1,0:T(8,128)(2,1)} fusion(pred[32,16]{1,0:T(8,128)(4,1)S(1)} %copy.24, pred[32,16]{1,0:T(8,128)(4,1)S(1)} %copy.23, pred[32,16]{1,0:T(8,128)(4,1)S(1)} %copy.22, bf16[16,1536]{1,0:T(8,128)(2,1)S(1)} %get-tuple-element.16, bf16[16,1536]{1,0:T(8,128)(2,1)S(1)} %get-tuple-element.17, ...), kind=kLoop, calls=%fused_computation.1 | loop fusion | flops 2359296 | bytes 1771008 | tf_op jit(solution)/shard_map/jit(_where)/select_n | solution.py:106
  7.2 10.6 %all-to-all-start = ((bf16[32,16,1536]{2,1,0:T(8,128)(2,1)}), bf16[32,16,1536]{2,1,0:T(8,128)(2,1)S(1)}, u32[]{:S(2)}, u32[]{:S(2)}) async-start(bf16[32,16,1536]{2,1,0:T(8,128)(2,1)} %select_select_fusion), calls=%async_computation | async-start | bytes 3145728 | tf_op jit(solution)/shard_map/all_to_all | solution.py:108
  17.8 0.1 copy.20
  18.1 0.1 lt.37
  18.2 0.1 convert_element_type.22
  18.3 0.9 reshape.123.s
  19.2 36.5 %all-to-all-done = bf16[32,16,1536]{2,1,0:T(8,128)(2,1)S(1)} async-done(((bf16[32,16,1536]{2,1,0:T(8,128)(2,1)}), bf16[32,16,1536]{2,1,0:T(8,128)(2,1)S(1)}, u32[]{:S(2)}, u32[]{:S(2)}) %all-to-all-start) | async-done | bytes 1572896 | tf_op jit(solution)/shard_map/all_to_all | solution.py:108
  55.7 1.9 %reshape.117 = bf16[192,4096]{1,0:T(8,128)(2,1)S(1)} reshape(bf16[32,16,1536]{2,1,0:T(8,128)(2,1)S(1)} %all-to-all-done) | data formatting | bytes 3145728 | tf_op jit(solution)/shard_map/reshape | solution.py:109
  57.5 3.6 %convolution_convert_fusion = bf16[576,4096]{1,0:T(8,128)(2,1)} fusion(bf16[192,4096]{1,0:T(8,128)(2,1)S(1)} %reshape.117, s32[576]{0:T(1024)S(1)} %add.37, pred[576]{0:T(1024)(128)(4,1)S(1)} %lt.37), kind=kOutput, calls=%fused_computation | convolution fusion | flops 908550144 | bytes 6294336 | tf_op jit(solution)/shard_map/dot_general | solution.py:114
  61.1 10.3 %xcorr.1 = f32[16,40,1024]{2,1,0:T(8,128)} custom-call(f32[12,1,5120]{2,1,0:T(1,128)} %reshape.123.s, bf16[12,48,4096]{2,1,0:T(8,128)(2,1)} %bitcast.70), custom_call_target="tpu_custom_call" | custom-call | flops 4831838208 | bytes 7323648 | tf_op jit(solution)/shard_map/xcorr/pallas_call | solution.py:73
  71.5 1.9 %dynamic-slice_bitcast_fusion.1 = (f32[8,40,1024]{2,1,0:T(8,128)S(1)}, f32[8,40,1024]{2,1,0:T(8,128)S(1)}) fusion(f32[8,2,40,1024]{3,2,1,0:T(8,128)} %bitcast.71, s32[]{:T(128)S(6)} %select_n.28, s32[]{:T(128)S(6)} %select_n.29), kind=kLoop, calls=%fused_computation.5 | loop fusion | bytes 5242888 | tf_op jit(solution)/shard_map/jit(dynamic_index_in_dim)/squeeze | solution.py:126
  73.4 4.1 %collective-permute-start = (f32[8,40,1024]{2,1,0:T(8,128)S(1)}, f32[8,40,1024]{2,1,0:T(8,128)S(1)}, u32[]{:S(2)}, u32[]{:S(2)}) collective-permute-start(f32[8,40,1024]{2,1,0:T(8,128)S(1)} %get-tuple-element.10), channel_id=1, source_target_pairs={{0,32},{32,0},{1,33},{33,1},{2,34},{34,2},{3,35},{35,3},{4,36},{36... | collective-permute-start | bytes 3932168 | tf_op jit(solution)/shard_map/ppermute | solution.py:128
  77.5 2.6 %collective-permute-done = f32[8,40,1024]{2,1,0:T(8,128)S(1)} collective-permute-done((f32[8,40,1024]{2,1,0:T(8,128)S(1)}, f32[8,40,1024]{2,1,0:T(8,128)S(1)}, u32[]{:S(2)}, u32[]{:S(2)}) %collective-permute-start) | collective-permute-done | bytes 1310752 | tf_op jit(solution)/shard_map/ppermute | solution.py:128
  80.1 0.3 fusion
  80.4 0.6 reshape.120
  81.0 28.2 %all_to_all.10 = bf16[8,32,1152]{2,1,0:T(8,128)(2,1)S(1)} all-to-all(bf16[8,32,1152]{2,1,0:T(8,128)(2,1)S(1)} %reshape.120), channel_id=1, replica_groups=mesh['z'=8,'c'=2,'pairs'=32] {'z'}, dimensions={0} | all-to-all | bytes 1179648 | tf_op jit(solution)/shard_map/all_to_all | solution.py:130
  109.3 0.1 convert_reduce_fusion
  109.3 0.8 reshape.121
  (26 shorter events, 0.5 us)
Async XLA Ops:
  0.0 0.8 copy-start
  7.2 10.7 %copy-start.1 = (s32[1,12,48]{2,0,1:T(1,128)S(1)}, s32[1,12,48]{2,0,1:T(1,128)}, u32[]{:S(2)}) copy-start(s32[1,12,48]{2,0,1:T(1,128)} %param.8) | copy-start | bytes 6916
  7.2 10.7 %copy-start.2 = (s32[1,12,48]{2,0,1:T(1,128)S(1)}, s32[1,12,48]{2,0,1:T(1,128)}, u32[]{:S(2)}) copy-start(s32[1,12,48]{2,0,1:T(1,128)} %param.7) | copy-start | bytes 6916
  7.2 10.9 %copy-start.3 = (s32[1,12]{1,0:T(1,128)S(1)}, s32[1,12]{1,0:T(1,128)}, u32[]{:S(2)}) copy-start(s32[1,12]{1,0:T(1,128)} %param.9) | copy-start | bytes 148
  7.2 48.5 %all-to-all-start = ((bf16[32,16,1536]{2,1,0:T(8,128)(2,1)}), bf16[32,16,1536]{2,1,0:T(8,128)(2,1)S(1)}, u32[]{:S(2)}, u32[]{:S(2)}) async-start(bf16[32,16,1536]{2,1,0:T(8,128)(2,1)} %select_select_fusion), calls=%async_computation | async-start | bytes 3145728 | tf_op jit(solution)/shard_map/all_to_all | solution.py:108
  73.4 6.8 %collective-permute-start = (f32[8,40,1024]{2,1,0:T(8,128)S(1)}, f32[8,40,1024]{2,1,0:T(8,128)S(1)}, u32[]{:S(2)}, u32[]{:S(2)}) collective-permute-start(f32[8,40,1024]{2,1,0:T(8,128)S(1)} %get-tuple-element.10), channel_id=1, source_target_pairs={{0,32},{32,0},{1,33},{33,1},{2,34},{34,2},{3,35},{35,3},{4,36},{36... | collective-permute-start | bytes 3932168 | tf_op jit(solution)/shard_map/ppermute | solution.py:128

commit v8 on v6

--- a/solution.py
+++ b/solution.py
@@ -47,44 +47,88 @@
     return jnp.concatenate(acc, axis=1)
 
 
-def corr_kernel(src_ref, p_ref, o_ref, *, win, scale, block_rows):
+def corr_kernel(core_ref, src_ref, p_ref, kept_ref, sent_ref, *, win, scale, block_rows):
     group, rows = p_ref.shape[0], p_ref.shape[1]
-    pad = o_ref.shape[1] - block_rows
+    core = core_ref[0]
+    pad = kept_ref.shape[1] - block_rows
     if pad:
-        for blk in range(o_ref.shape[0]):
-            o_ref[blk, block_rows:, :] = jnp.zeros((pad, LAGS), jnp.float32)
+        for half in range(kept_ref.shape[0]):
+            kept_ref[half, block_rows:, :] = jnp.zeros((pad, LAGS), jnp.float32)
+            sent_ref[half, block_rows:, :] = jnp.zeros((pad, LAGS), jnp.float32)
     for u in range(group):
         cc = trace_corr(src_ref[u], p_ref, u, rows, win) * scale
         first = u * rows
         while first < (u + 1) * rows:
             blk, at = divmod(first, block_rows)
             take = min(block_rows - at, (u + 1) * rows - first)
-            o_ref[blk, at: at + take, :] = cc[first - u * rows: first - u * rows + take]
+            piece = cc[first - u * rows: first - u * rows + take]
+            parity = blk % 2
+
+            @pl.when(core == parity)
+            def _():
+                kept_ref[blk // 2, at: at + take, :] = piece
+
+            @pl.when(core != parity)
+            def _():
+                sent_ref[blk // 2, at: at + take, :] = piece
+
             first += take
 
 
-def correlate(src, partner_rows, scale, block_rows):
+def correlate(core, src, partner_rows, scale, block_rows):
     traces, rows, win = partner_rows.shape
     span = src.shape[-1]
     group = block_rows // math.gcd(block_rows, rows)
     blocks = group * rows // block_rows
+    if blocks % 2:
+        group, blocks = 2 * group, 2 * blocks
     padded = -(-block_rows // 8) * 8
     flops = 2 * traces * rows * win * LAGS
+    half_shape = jax.ShapeDtypeStruct((traces * rows // block_rows // 2, padded, LAGS), jnp.float32)
+    out_spec = pl.BlockSpec((blocks // 2, padded, LAGS), lambda g, c: (g, 0, 0))
     return pl.pallas_call(
-        lambda s, p, o: corr_kernel(s, p, o, win=win, scale=scale, block_rows=block_rows),
-        grid=(traces // group,),
-        in_specs=[
-            pl.BlockSpec((group, 1, span), lambda g: (g, 0, 0)),
-            pl.BlockSpec((group, rows, win), lambda g: (g, 0, 0)),
-        ],
-        out_specs=pl.BlockSpec((blocks, padded, LAGS), lambda g: (g, 0, 0)),
-        out_shape=jax.ShapeDtypeStruct((traces * rows // block_rows, padded, LAGS), jnp.float32),
+        lambda c, s, p, k, o: corr_kernel(c, s, p, k, o, win=win, scale=scale, block_rows=block_rows),
+        grid_spec=pltpu.PrefetchScalarGridSpec(
+            num_scalar_prefetch=1,
+            grid=(traces // group,),
+            in_specs=[
+                pl.BlockSpec((group, 1, span), lambda g, c: (g, 0, 0)),
+                pl.BlockSpec((group, rows, win), lambda g, c: (g, 0, 0)),
+            ],
+            out_specs=[out_spec, out_spec],
+        ),
+        out_shape=[half_shape, half_shape],
         cost_estimate=pl.CostEstimate(
             flops=flops, transcendentals=0,
             bytes_accessed=traces * (rows * win * 2 + span * 4 + rows * LAGS * 4),
         ),
         name="xcorr",
-    )(src.reshape(traces, 1, span), partner_rows)
+    )(core.reshape(1), src.reshape(traces, 1, span), partner_rows)
+
+
+def pick_kernel(ids_ref, rows_ref, o_ref):
+    def body(k, carry):
+        o_ref[k] = rows_ref[ids_ref[k]]
+        return carry
+
+    lax.fori_loop(0, o_ref.shape[0], body, 0)
+
+
+def pick_rows(ids, rows):
+    count = ids.shape[0]
+    slab = rows.shape[1:]
+    zeros = (0,) * len(slab)
+    return pl.pallas_call(
+        pick_kernel,
+        grid_spec=pltpu.PrefetchScalarGridSpec(
+            num_scalar_prefetch=1,
+            grid=(1,),
+            in_specs=[pl.BlockSpec(rows.shape, lambda i, ids: (0,) + zeros)],
+            out_specs=pl.BlockSpec((count,) + slab, lambda i, ids: (0,) + zeros),
+        ),
+        out_shape=jax.ShapeDtypeStruct((count,) + slab, rows.dtype),
+        name="pick_rows",
+    )(ids, rows)
 
 
 def shards(record, requested, partners, codes, counts):
@@ -101,10 +145,7 @@
     per_station = comp_count * window_count * window_len
     mine = flip_lanes(whitened).reshape(local_stations, 8, per_station // 8)
     asked_of_me = lax.dynamic_index_in_dim(requested, own_index, axis=1, keepdims=False)
-    pick_send = (asked_of_me[:, :, None] == jnp.arange(local_stations, dtype=jnp.int32)[None, None, :])
-    outgoing = jnp.einsum("eis,sru->eiru", pick_send.astype(jnp.bfloat16), mine,
-                          preferred_element_type=jnp.float32)
-    outgoing = outgoing.astype(jnp.bfloat16).reshape(owners, capacity * 8, per_station // 8)
+    outgoing = pick_rows(asked_of_me.reshape(-1), mine)
     arrived = lax.all_to_all(outgoing, "pairs", 0, 0, tiled=True)
     trace_pool = arrived.reshape(owners * capacity * comp_count, window_count * window_len)
     row_ids = (partners[0] * comp_count + codes[0]).reshape(-1)
@@ -120,11 +161,8 @@
     total_windows = window_count * tm_count
     scale = 1.0 / math.sqrt(window_len * total_windows)
     block_rows = trace_count * per_trace // tm_count
-    lagged = correlate(src, picked, scale, block_rows)
-    lagged = lagged.reshape(chips, cores, lagged.shape[1], LAGS)
-    core = lax.axis_index("c")
-    kept = lax.dynamic_index_in_dim(lagged, core, axis=1, keepdims=False)
-    given = lax.dynamic_index_in_dim(lagged, cores - 1 - core, axis=1, keepdims=False)
+    core = lax.axis_index("c").astype(jnp.int32)
+    kept, given = correlate(core, src, picked, scale, block_rows)
     got = lax.ppermute(given, "c", [(0, 1), (1, 0)])
     chip_sums = (kept + got)[:, :block_rows].astype(jnp.bfloat16).reshape(chips, 32, block_rows * LAGS // 32)
     arrived_sums = lax.all_to_all(chip_sums, "z", 0, 0, tiled=True)

time: 110 us -> 116 us (1.055)
  Pallas kernels: 10.1 us -> 17.4 us
  local copies, waits for them, and re-layouts: 9 us -> 6.9 us
  other arithmetic: 3.64 us -> 4.89 us
    pallas_call x1 -> x2, Pallas kernels: 10.1 us -> 17.4 us  [the longest x1 14.2 us: correlate(): pl.pallas_call(lambda c, s, p, k, o: corr_kernel(c, s, p, k, o, win=win,...]
    squeeze x1 -> x0, local copies, waits for them, and re-layouts: 1.89 us -> none  [shards(): kept = lax.dynamic_index_in_dim(lagged, core, axis=1, keepdims=False)]
    reshape x1, local copies, waits for them, and re-layouts: 2.02 us -> 0.65 us  [shards(): outgoing = pick_rows(asked_of_me.reshape(-1), mine)]
    another operation x1, other arithmetic: 0.27 us -> 1.51 us
where the time goes in v8:
time: 116 us; the launch traced here: 115 us
  waiting for transfers between devices  39.3 us (34%)
  blocking collectives  28.2 us (24%)
  Pallas kernels  17.4 us (15%)
  starting transfers between devices  14.7 us (13%)
  local copies, waits for them, and re-layouts  6.9 us (6%)
  other arithmetic  4.89 us (4%)
  matrix products  3.56 us (3%)
    all_to_all x1, waiting for transfers between devices, shards(): arrived = lax.all_to_all(outgoing, 'pairs', 0, 0, tiled=True)  36.5 us
    all_to_all x1, blocking collectives, shards(): arrived_sums = lax.all_to_all(chip_sums, 'z', 0, 0, tiled=True)  28.2 us
    pallas_call x1, Pallas kernels, correlate(): pl.pallas_call(lambda c, s, p, k, o: corr_kernel(c, s, p, k, o, win=win,...  14.2 us
    all_to_all x1, starting transfers between devices, shards(): arrived = lax.all_to_all(outgoing, 'pairs', 0, 0, tiled=True)  10.6 us
    ppermute x1, starting transfers between devices, shards(): got = lax.ppermute(given, 'c', [(0, 1), (1, 0)])  4.1 us
    dot_general x1, matrix products, shards(): jnp.dot(pick_recv.astype(jnp.bfloat16), trace_pool, preferred_element_typ...  3.56 us
    pallas_call x1, Pallas kernels, pick_rows(): pl.pallas_call(pick_kernel, grid_spec=pltpu.PrefetchScalarGridSpec(num_sc...  3.15 us
    ppermute x1, waiting for transfers between devices, shards(): got = lax.ppermute(given, 'c', [(0, 1), (1, 0)])  2.85 us
  transfers between devices with their start and end apart: 2, of which 2 were waited for; matrix products, arithmetic and copies ran while one was open for 1% of the time, Pallas kernels for 0%

profile of v8, /device:TPU:1, one launch (start us, length us, event | category | flops | bytes accessed | tf_op | source)
XLA Modules:
  0.0 115.1 jit_solution(11405704394121279672)
XLA Ops:
  0.0 0.0 copy-start
  0.0 1.0 convert_reduce_fusion.1
  1.0 1.1 fusion.7
  2.2 0.0 copy-done
  2.2 0.7 dynamic-slice_reduce_fusion
  2.9 0.7 reshape.83.ids_ref
  3.5 1.0 fusion.8
  4.5 0.1 reshape.84
  4.7 0.1 rev.3
  4.8 0.8 reshape_reshape.3.rows_ref
  5.6 3.1 %pick_rows.1 = bf16[64,8,1536]{2,1,0:T(8,128)(2,1)} custom-call(s32[64]{0:T(128)} %reshape.83.ids_ref, bf16[4,8,1536]{2,1,0:T(8,128)(2,1)} %reshape_reshape.3.rows_ref), custom_call_target="tpu_custom_call" | custom-call | tf_op jit(solution)/shard_map/pick_rows/pallas_call | solution.py:121
  8.7 10.6 %all-to-all-start = ((bf16[64,8,1536]{2,1,0:T(8,128)(2,1)}), bf16[64,8,1536]{2,1,0:T(8,128)(2,1)S(1)}, u32[]{:S(2)}, u32[]{:S(2)}) async-start(bf16[64,8,1536]{2,1,0:T(8,128)(2,1)} %pick_rows.1), calls=%async_computation | async-start | bytes 3145728 | tf_op jit(solution)/shard_map/all_to_all | solution.py:149
  19.4 0.1 copy.8
  19.5 0.0 copy-done.3
  19.5 0.1 iota_compare_fusion.1
  19.5 0.1 lt.30
  19.6 0.0 copy-done.1
  19.6 0.0 copy-done.2
  19.7 0.1 add.29
  19.8 0.1 convert_element_type.22
  19.9 0.9 reshape.90.s
  20.8 36.5 %all-to-all-done = bf16[64,8,1536]{2,1,0:T(8,128)(2,1)S(1)} async-done(((bf16[64,8,1536]{2,1,0:T(8,128)(2,1)}), bf16[64,8,1536]{2,1,0:T(8,128)(2,1)S(1)}, u32[]{:S(2)}, u32[]{:S(2)}) %all-to-all-start) | async-done | bytes 1572896 | tf_op jit(solution)/shard_map/all_to_all | solution.py:149
  57.2 1.9 %reshape.85 = bf16[192,4096]{1,0:T(8,128)(2,1)S(1)} reshape(bf16[64,8,1536]{2,1,0:T(8,128)(2,1)S(1)} %all-to-all-done) | data formatting | bytes 3145728 | tf_op jit(solution)/shard_map/reshape | solution.py:150
  59.1 3.6 %convolution_convert_fusion = bf16[576,4096]{1,0:T(8,128)(2,1)} fusion(bf16[192,4096]{1,0:T(8,128)(2,1)S(1)} %reshape.85, s32[576]{0:T(1024)S(1)} %add.29, pred[576]{0:T(1024)(128)(4,1)S(1)} %lt.30), kind=kOutput, calls=%fused_computation | convolution fusion | flops 908550144 | bytes 6294336 | tf_op jit(solution)/shard_map/dot_general | solution.py:155
  62.7 14.2 %xcorr.1 = (f32[8,40,1024]{2,1,0:T(8,128)}, f32[8,40,1024]{2,1,0:T(8,128)}) custom-call(s32[1]{0:T(128)} %bitcast.c, f32[12,1,5120]{2,1,0:T(1,128)} %reshape.90.s, bf16[12,48,4096]{2,1,0:T(8,128)(2,1)} %bitcast.12), custom_call_target="tpu_custom_call" | custom-call | flops 4831838208 | bytes 7323648 | tf_op jit(solution)/shard_map/xcorr/pallas_call | solution.py:89
  76.9 4.1 %collective-permute-start = (f32[8,40,1024]{2,1,0:T(8,128)}, f32[8,40,1024]{2,1,0:T(8,128)S(1)}, u32[]{:S(2)}, u32[]{:S(2)}) collective-permute-start(f32[8,40,1024]{2,1,0:T(8,128)} %get-tuple-element.8), channel_id=1, source_target_pairs={{0,32},{32,0},{1,33},{33,1},{2,34},{34,2},{3,35},{35,3},{4,36},{36... | collective-permute-start | bytes 3932168 | tf_op jit(solution)/shard_map/ppermute | solution.py:166
  81.0 2.9 %collective-permute-done = f32[8,40,1024]{2,1,0:T(8,128)S(1)} collective-permute-done((f32[8,40,1024]{2,1,0:T(8,128)}, f32[8,40,1024]{2,1,0:T(8,128)S(1)}, u32[]{:S(2)}, u32[]{:S(2)}) %collective-permute-start) | collective-permute-done | bytes 1310752 | tf_op jit(solution)/shard_map/ppermute | solution.py:166
  83.8 1.5 %fusion = bf16[8,36,1024]{2,1,0:T(8,128)(2,1)S(1)} fusion(f32[8,40,1024]{2,1,0:T(8,128)S(1)} %collective-permute-done, f32[8,40,1024]{2,1,0:T(8,128)} %get-tuple-element.7), kind=kLoop, calls=%fused_computation.2 | loop fusion | flops 589824 | bytes 2949120 | tf_op jit(solution)/shard_map/convert.4
  85.4 0.6 reshape.87
  86.0 28.2 %all_to_all.10 = bf16[8,32,1152]{2,1,0:T(8,128)(2,1)S(1)} all-to-all(bf16[8,32,1152]{2,1,0:T(8,128)(2,1)S(1)} %reshape.87), channel_id=1, replica_groups=mesh['z'=8,'c'=2,'pairs'=32] {'z'}, dimensions={0} | all-to-all | bytes 1179648 | tf_op jit(solution)/shard_map/all_to_all | solution.py:168
  114.2 0.1 convert_reduce_fusion
  114.3 0.8 reshape.88
  (8 shorter events, 0.1 us)
Async XLA Ops:
  0.0 2.2 %copy-start = (s32[32,32,2]{1,2,0:T(2,128)S(1)}, s32[32,32,2]{1,2,0:T(2,128)}, u32[]{:S(2)}) copy-start(s32[32,32,2]{1,2,0:T(2,128)} %param.6) | copy-start | bytes 24580
  8.7 10.7 %copy-start.3 = (s32[1,12]{1,0:T(1,128)S(1)}, s32[1,12]{1,0:T(1,128)}, u32[]{:S(2)}) copy-start(s32[1,12]{1,0:T(1,128)} %param.9) | copy-start | bytes 148
  8.7 10.9 %copy-start.1 = (s32[1,12,48]{2,0,1:T(1,128)S(1)}, s32[1,12,48]{2,0,1:T(1,128)}, u32[]{:S(2)}) copy-start(s32[1,12,48]{2,0,1:T(1,128)} %param.8) | copy-start | bytes 6916
  8.7 10.9 %copy-start.2 = (s32[1,12,48]{2,0,1:T(1,128)S(1)}, s32[1,12,48]{2,0,1:T(1,128)}, u32[]{:S(2)}) copy-start(s32[1,12,48]{2,0,1:T(1,128)} %param.7) | copy-start | bytes 6916
  8.7 48.5 %all-to-all-start = ((bf16[64,8,1536]{2,1,0:T(8,128)(2,1)}), bf16[64,8,1536]{2,1,0:T(8,128)(2,1)S(1)}, u32[]{:S(2)}, u32[]{:S(2)}) async-start(bf16[64,8,1536]{2,1,0:T(8,128)(2,1)} %pick_rows.1), calls=%async_computation | async-start | bytes 3145728 | tf_op jit(solution)/shard_map/all_to_all | solution.py:149
  76.9 7.0 %collective-permute-start = (f32[8,40,1024]{2,1,0:T(8,128)}, f32[8,40,1024]{2,1,0:T(8,128)S(1)}, u32[]{:S(2)}, u32[]{:S(2)}) collective-permute-start(f32[8,40,1024]{2,1,0:T(8,128)} %get-tuple-element.8), channel_id=1, source_target_pairs={{0,32},{32,0},{1,33},{33,1},{2,34},{34,2},{3,35},{35,3},{4,36},{36... | collective-permute-start | bytes 3932168 | tf_op jit(solution)/shard_map/ppermute | solution.py:166

commit v9 on v6

--- a/solution.py
+++ b/solution.py
@@ -49,17 +49,18 @@
 
 def corr_kernel(src_ref, p_ref, o_ref, *, win, scale, block_rows):
     group, rows = p_ref.shape[0], p_ref.shape[1]
-    pad = o_ref.shape[1] - block_rows
+    pad = o_ref.shape[2] - block_rows
     if pad:
-        for blk in range(o_ref.shape[0]):
-            o_ref[blk, block_rows:, :] = jnp.zeros((pad, LAGS), jnp.float32)
+        for parity in range(2):
+            for blk in range(o_ref.shape[1]):
+                o_ref[parity, blk, block_rows:, :] = jnp.zeros((pad, LAGS), jnp.float32)
     for u in range(group):
         cc = trace_corr(src_ref[u], p_ref, u, rows, win) * scale
         first = u * rows
         while first < (u + 1) * rows:
             blk, at = divmod(first, block_rows)
             take = min(block_rows - at, (u + 1) * rows - first)
-            o_ref[blk, at: at + take, :] = cc[first - u * rows: first - u * rows + take]
+            o_ref[blk % 2, blk // 2, at: at + take, :] = cc[first - u * rows: first - u * rows + take]
             first += take
 
 
@@ -68,6 +69,8 @@
     span = src.shape[-1]
     group = block_rows // math.gcd(block_rows, rows)
     blocks = group * rows // block_rows
+    if blocks % 2:
+        group, blocks = 2 * group, 2 * blocks
     padded = -(-block_rows // 8) * 8
     flops = 2 * traces * rows * win * LAGS
     return pl.pallas_call(
@@ -77,8 +80,8 @@
             pl.BlockSpec((group, 1, span), lambda g: (g, 0, 0)),
             pl.BlockSpec((group, rows, win), lambda g: (g, 0, 0)),
         ],
-        out_specs=pl.BlockSpec((blocks, padded, LAGS), lambda g: (g, 0, 0)),
-        out_shape=jax.ShapeDtypeStruct((traces * rows // block_rows, padded, LAGS), jnp.float32),
+        out_specs=pl.BlockSpec((2, blocks // 2, padded, LAGS), lambda g: (0, g, 0, 0)),
+        out_shape=jax.ShapeDtypeStruct((2, traces * rows // block_rows // 2, padded, LAGS), jnp.float32),
         cost_estimate=pl.CostEstimate(
             flops=flops, transcendentals=0,
             bytes_accessed=traces * (rows * win * 2 + span * 4 + rows * LAGS * 4),
@@ -121,12 +124,11 @@
     scale = 1.0 / math.sqrt(window_len * total_windows)
     block_rows = trace_count * per_trace // tm_count
     lagged = correlate(src, picked, scale, block_rows)
-    lagged = lagged.reshape(chips, cores, lagged.shape[1], LAGS)
     core = lax.axis_index("c")
-    kept = lax.dynamic_index_in_dim(lagged, core, axis=1, keepdims=False)
-    given = lax.dynamic_index_in_dim(lagged, cores - 1 - core, axis=1, keepdims=False)
-    got = lax.ppermute(given, "c", [(0, 1), (1, 0)])
-    chip_sums = (kept + got)[:, :block_rows].astype(jnp.bfloat16).reshape(chips, 32, block_rows * LAGS // 32)
+    to_odd = lax.ppermute(lagged[1], "c", [(0, 1)])
+    to_even = lax.ppermute(lagged[0], "c", [(1, 0)])
+    chip_sums = jnp.where(core == 0, lagged[0] + to_even, lagged[1] + to_odd)
+    chip_sums = chip_sums[:, :block_rows].astype(jnp.bfloat16).reshape(chips, 32, block_rows * LAGS // 32)
     arrived_sums = lax.all_to_all(chip_sums, "z", 0, 0, tiled=True)
     total = jnp.sum(arrived_sums.astype(jnp.float32), axis=0)
     return total.reshape(1, block_rows, LAGS)

time: 110 us -> 115 us (1.045)
  starting transfers between devices: 14.7 us -> 17.1 us
  other arithmetic: 3.64 us -> 5.55 us
    ppermute x1 -> x2, starting transfers between devices: 4.11 us -> 6.46 us  [the longest x1 5.18 us: shards(): to_even = lax.ppermute(lagged[0], 'c', [(1, 0)])]
    another operation x1, other arithmetic: 0.27 us -> 2.16 us
    ppermute x1 -> x2, waiting for transfers between devices: 2.64 us -> 3.76 us  [the longest x1 3.36 us: shards(): to_odd = lax.ppermute(lagged[1], 'c', [(0, 1)])]
  transfers between devices with their start and end apart: 2 -> 3, of which waited for: 2 -> 3; matrix products, arithmetic and copies ran while one was open for 1% -> 1% of each run, Pallas kernels for 0% -> 0%
where the time goes in v9:
time: 115 us
  waiting for transfers between devices  40.2 us (35%)
  blocking collectives  28.6 us (25%)
  starting transfers between devices  17.1 us (15%)
  Pallas kernels  10 us (9%)
  local copies, waits for them, and re-layouts  9.01 us (8%)
  other arithmetic  5.55 us (5%)
  matrix products  4.2 us (4%)
    all_to_all x1, waiting for transfers between devices, shards(): arrived = lax.all_to_all(outgoing, 'pairs', 0, 0, tiled=True)  36.5 us
    all_to_all x1, blocking collectives, shards(): arrived_sums = lax.all_to_all(chip_sums, 'z', 0, 0, tiled=True)  28.6 us
    all_to_all x1, starting transfers between devices, shards(): arrived = lax.all_to_all(outgoing, 'pairs', 0, 0, tiled=True)  10.6 us
    pallas_call x1, Pallas kernels, correlate(): pl.pallas_call(lambda s, p, o: corr_kernel(s, p, o, win=win, scale=scale,...  10 us
    ppermute x1, starting transfers between devices, shards(): to_even = lax.ppermute(lagged[0], 'c', [(1, 0)])  5.18 us
    dot_general x1, matrix products, shards(): jnp.dot(pick_recv.astype(jnp.bfloat16), trace_pool, preferred_element_typ...  3.57 us
    ppermute x1, waiting for transfers between devices, shards(): to_odd = lax.ppermute(lagged[1], 'c', [(0, 1)])  3.36 us
  transfers between devices with their start and end apart: 3, of which 3 were waited for; matrix products, arithmetic and copies ran while one was open for 1% of the time, Pallas kernels for 0%

profile of v9, /device:TPU:1, one launch (start us, length us, event | category | flops | bytes accessed | tf_op | source)
XLA Modules:
  0.0 114.8 jit_solution(13219634718561620156)
XLA Ops:
  0.0 0.0 copy-start
  0.0 1.0 convert_reduce_fusion.1
  1.0 1.1 fusion.8
  2.2 0.1 constant_dynamic-slice_fusion
  2.3 0.1 copy.9
  2.4 1.0 fusion.9
  3.4 0.1 reshape.80
  3.5 0.1 rev.3
  3.6 0.1 reshape_reshape.3
  3.8 0.6 convolution_convert_fusion.1
  4.4 2.0 %copy.12 = bf16[32,16,1536]{2,1,0:T(8,128)(2,1)} copy(bf16[32,16,1536]{2,0,1:T(8,128)(2,1)S(1)} %bitcast.26) | data formatting | bytes 3145728 | tf_op jit(solution)/shard_map/reshape | solution.py:110
  6.5 10.6 %all-to-all-start = ((bf16[32,16,1536]{2,1,0:T(8,128)(2,1)}), bf16[32,16,1536]{2,1,0:T(8,128)(2,1)S(1)}, u32[]{:S(2)}, u32[]{:S(2)}) async-start(bf16[32,16,1536]{2,1,0:T(8,128)(2,1)} %copy.12), calls=%async_computation | async-start | bytes 3145728 | tf_op jit(solution)/shard_map/all_to_all | solution.py:111
  17.1 0.1 copy.8
  17.2 0.1 iota_compare_fusion.1
  17.3 0.1 lt.30
  17.4 0.1 add.32
  17.5 0.1 convert_element_type.26
  17.6 0.9 reshape.87.s
  18.5 36.5 %all-to-all-done = bf16[32,16,1536]{2,1,0:T(8,128)(2,1)S(1)} async-done(((bf16[32,16,1536]{2,1,0:T(8,128)(2,1)}), bf16[32,16,1536]{2,1,0:T(8,128)(2,1)S(1)}, u32[]{:S(2)}, u32[]{:S(2)}) %all-to-all-start) | async-done | bytes 1572896 | tf_op jit(solution)/shard_map/all_to_all | solution.py:111
  55.0 1.9 %reshape.82 = bf16[192,4096]{1,0:T(8,128)(2,1)S(1)} reshape(bf16[32,16,1536]{2,1,0:T(8,128)(2,1)S(1)} %all-to-all-done) | data formatting | bytes 3145728 | tf_op jit(solution)/shard_map/reshape | solution.py:112
  56.8 3.6 %convolution_convert_fusion = bf16[576,4096]{1,0:T(8,128)(2,1)} fusion(bf16[192,4096]{1,0:T(8,128)(2,1)S(1)} %reshape.82, s32[576]{0:T(1024)S(1)} %add.32, pred[576]{0:T(1024)(128)(4,1)S(1)} %lt.30), kind=kOutput, calls=%fused_computation | convolution fusion | flops 908550144 | bytes 6294336 | tf_op jit(solution)/shard_map/dot_general | solution.py:117
  60.4 10.0 %xcorr.1 = f32[2,8,40,1024]{3,2,1,0:T(8,128)} custom-call(f32[12,1,5120]{2,1,0:T(1,128)} %reshape.87.s, bf16[12,48,4096]{2,1,0:T(8,128)(2,1)} %bitcast.25), custom_call_target="tpu_custom_call" | custom-call | flops 4831838208 | bytes 7323648 | tf_op jit(solution)/shard_map/xcorr/pallas_call | solution.py:76
  70.4 1.9 %slice_bitcast_fusion.1 = (f32[8,40,1024]{2,1,0:T(8,128)S(1)}, f32[8,40,1024]{2,1,0:T(8,128)S(1)}) fusion(f32[2,8,40,1024]{3,2,1,0:T(8,128)} %xcorr.1), kind=kLoop, calls=%fused_computation.7 | loop fusion | bytes 5242880 | tf_op jit(solution)/shard_map/squeeze | solution.py:130
  72.3 5.2 %collective-permute-start = (f32[8,40,1024]{2,1,0:T(8,128)S(1)}, f32[8,40,1024]{2,1,0:T(8,128)}, u32[]{:S(2)}, u32[]{:S(2)}) collective-permute-start(f32[8,40,1024]{2,1,0:T(8,128)S(1)} %get-tuple-element.5), channel_id=1, source_target_pairs={{32,0},{33,1},{34,2},{35,3},{36,4},{37,5},{38,6},{39,7},{40,8},{41... | collective-permute-start | bytes 3932168 | tf_op jit(solution)/shard_map/ppermute | solution.py:129
  77.5 1.3 %collective-permute-start.1 = (f32[8,40,1024]{2,1,0:T(8,128)S(1)}, f32[8,40,1024]{2,1,0:T(8,128)}, u32[]{:S(2)}, u32[]{:S(2)}) collective-permute-start(f32[8,40,1024]{2,1,0:T(8,128)S(1)} %get-tuple-element.6), channel_id=1, source_target_pairs={{0,32},{1,33},{2,34},{3,35},{4,36},{5,37},{6,38},{7,39},{8,40},{9,... | collective-permute-start | bytes 3932168 | tf_op jit(solution)/shard_map/ppermute | solution.py:128
  78.8 0.4 collective-permute-done
  79.2 3.4 %collective-permute-done.1 = f32[8,40,1024]{2,1,0:T(8,128)} collective-permute-done((f32[8,40,1024]{2,1,0:T(8,128)S(1)}, f32[8,40,1024]{2,1,0:T(8,128)}, u32[]{:S(2)}, u32[]{:S(2)}) %collective-permute-start.1) | collective-permute-done | bytes 1310752 | tf_op jit(solution)/shard_map/ppermute | solution.py:128
  82.5 2.2 %fusion.1 = bf16[8,36,1024]{2,1,0:T(8,128)(2,1)S(1)} fusion(f32[8,40,1024]{2,1,0:T(8,128)} %collective-permute-done.1, f32[8,40,1024]{2,1,0:T(8,128)S(1)} %get-tuple-element.6, f32[8,40,1024]{2,1,0:T(8,128)} %collective-permute-done, f32[8,40,1024]{2,1,0:T(8,128)S(1)} %get-tuple-element.5, pred[]{:T(512)S(6)} %eq.31), kind=kLoop, calls=%fused_computation.4 | loop fusion | flops 1179648 | bytes 5308417 | tf_op jit(solution)/shard_map/convert.4
  84.7 0.6 reshape.84
  85.3 28.6 %all_to_all.10 = bf16[8,32,1152]{2,1,0:T(8,128)(2,1)S(1)} all-to-all(bf16[8,32,1152]{2,1,0:T(8,128)(2,1)S(1)} %reshape.84), channel_id=1, replica_groups=mesh['z'=8,'c'=2,'pairs'=32] {'z'}, dimensions={0} | all-to-all | bytes 1179648 | tf_op jit(solution)/shard_map/all_to_all | solution.py:132
  113.9 0.1 convert_reduce_fusion
  114.0 0.8 reshape.85
  (12 shorter events, 0.1 us)
Async XLA Ops:
  0.0 2.2 %copy-start = (s32[32,32,2]{1,2,0:T(2,128)S(1)}, s32[32,32,2]{1,2,0:T(2,128)}, u32[]{:S(2)}) copy-start(s32[32,32,2]{1,2,0:T(2,128)} %param.6) | copy-start | bytes 24580
  6.5 10.7 %copy-start.3 = (s32[1,12]{1,0:T(1,128)S(1)}, s32[1,12]{1,0:T(1,128)}, u32[]{:S(2)}) copy-start(s32[1,12]{1,0:T(1,128)} %param.9) | copy-start | bytes 148
  6.5 10.9 %copy-start.1 = (s32[1,12,48]{2,0,1:T(1,128)S(1)}, s32[1,12,48]{2,0,1:T(1,128)}, u32[]{:S(2)}) copy-start(s32[1,12,48]{2,0,1:T(1,128)} %param.8) | copy-start | bytes 6916
  6.5 10.9 %copy-start.2 = (s32[1,12,48]{2,0,1:T(1,128)S(1)}, s32[1,12,48]{2,0,1:T(1,128)}, u32[]{:S(2)}) copy-start(s32[1,12,48]{2,0,1:T(1,128)} %param.7) | copy-start | bytes 6916
  6.5 48.5 %all-to-all-start = ((bf16[32,16,1536]{2,1,0:T(8,128)(2,1)}), bf16[32,16,1536]{2,1,0:T(8,128)(2,1)S(1)}, u32[]{:S(2)}, u32[]{:S(2)}) async-start(bf16[32,16,1536]{2,1,0:T(8,128)(2,1)} %copy.12), calls=%async_computation | async-start | bytes 3145728 | tf_op jit(solution)/shard_map/all_to_all | solution.py:111
  72.3 6.9 %collective-permute-start = (f32[8,40,1024]{2,1,0:T(8,128)S(1)}, f32[8,40,1024]{2,1,0:T(8,128)}, u32[]{:S(2)}, u32[]{:S(2)}) collective-permute-start(f32[8,40,1024]{2,1,0:T(8,128)S(1)} %get-tuple-element.5), channel_id=1, source_target_pairs={{32,0},{33,1},{34,2},{35,3},{36,4},{37,5},{38,6},{39,7},{40,8},{41... | collective-permute-start | bytes 3932168 | tf_op jit(solution)/shard_map/ppermute | solution.py:129
  77.5 5.0 %collective-permute-start.1 = (f32[8,40,1024]{2,1,0:T(8,128)S(1)}, f32[8,40,1024]{2,1,0:T(8,128)}, u32[]{:S(2)}, u32[]{:S(2)}) collective-permute-start(f32[8,40,1024]{2,1,0:T(8,128)S(1)} %get-tuple-element.6), channel_id=1, source_target_pairs={{0,32},{1,33},{2,34},{3,35},{4,36},{5,37},{6,38},{7,39},{8,40},{9,... | collective-permute-start | bytes 3932168 | tf_op jit(solution)/shard_map/ppermute | solution.py:128

commit v10 on v6

--- a/solution.py
+++ b/solution.py
@@ -12,11 +12,22 @@
 LANE = 128
 
 
-def normalize(traces):
-    values = traces.astype(jnp.float32)
+def white_kernel(x_ref, o_ref):
+    values = x_ref[...].astype(jnp.float32)
     values = values - jnp.mean(values, axis=-1, keepdims=True)
     power_mean = jnp.mean(values * values, axis=-1, keepdims=True)
-    return (values * lax.rsqrt(power_mean + 1e-06)).astype(jnp.bfloat16)
+    o_ref[...] = (values * lax.rsqrt(power_mean + 1e-06)).astype(o_ref.dtype)
+
+
+def normalize(traces):
+    shape = traces.shape
+    rows = traces.reshape(-1, shape[-1])
+    out = pl.pallas_call(
+        white_kernel,
+        out_shape=jax.ShapeDtypeStruct(rows.shape, jnp.bfloat16),
+        name="whiten",
+    )(rows)
+    return out.reshape(shape)
 
 
 def flip_lanes(rows):

time: 110 us -> 111 us (level)
  other arithmetic: 3.64 us -> 0.47 us
  local copies, waits for them, and re-layouts: 9 us -> 11.4 us
  Pallas kernels: 10.1 us -> 11.9 us
    reduce_sum x2 -> x0, other arithmetic: 2.15 us -> none  [the longest x1 1.11 us: normalize(): power_mean = jnp.mean(values * values, axis=-1, keepdims=True)]
    unnamed x8 -> x13, local copies, waits for them, and re-layouts: 0.02 us -> 1.94 us
    pallas_call x0 -> x1, Pallas kernels: none -> 1.81 us  [normalize(): pl.pallas_call(white_kernel, out_shape=jax.ShapeDtypeStruct(rows.shape, j...]
where the time goes in v10:
time: 111 us; the launch traced here: 110 us
  waiting for transfers between devices  39.3 us (35%)
  blocking collectives  28.2 us (25%)
  starting transfers between devices  14.7 us (13%)
  Pallas kernels  11.9 us (11%)
  local copies, waits for them, and re-layouts  11.4 us (10%)
  matrix products  4.22 us (4%)
    all_to_all x1, waiting for transfers between devices, shards(): arrived = lax.all_to_all(outgoing, 'pairs', 0, 0, tiled=True)  36.7 us
    all_to_all x1, blocking collectives, shards(): arrived_sums = lax.all_to_all(chip_sums, 'z', 0, 0, tiled=True)  28.2 us
    all_to_all x1, starting transfers between devices, shards(): arrived = lax.all_to_all(outgoing, 'pairs', 0, 0, tiled=True)  10.6 us
    pallas_call x1, Pallas kernels, correlate(): pl.pallas_call(lambda s, p, o: corr_kernel(s, p, o, win=win, scale=scale,...  10.1 us
    ppermute x1, starting transfers between devices, shards(): got = lax.ppermute(given, 'c', [(0, 1), (1, 0)])  4.1 us
    dot_general x1, matrix products, shards(): jnp.dot(pick_recv.astype(jnp.bfloat16), trace_pool, preferred_element_typ...  3.57 us
    ppermute x1, waiting for transfers between devices, shards(): got = lax.ppermute(given, 'c', [(0, 1), (1, 0)])  2.64 us
  transfers between devices with their start and end apart: 2, of which 2 were waited for; matrix products, arithmetic and copies ran while one was open for 1% of the time, Pallas kernels for 0%

profile of v10, /device:TPU:1, one launch (start us, length us, event | category | flops | bytes accessed | tf_op | source)
XLA Modules:
  0.0 110.3 jit_solution(7297059038934466069)
XLA Ops:
  0.0 0.0 copy-start
  0.0 1.0 copy.8
  1.0 0.7 reshape.56.x_ref
  1.7 1.8 %whiten.1 = bf16[12,4096]{1,0:T(8,128)(2,1)} custom-call(bf16[12,4096]{1,0:T(8,128)(2,1)} %reshape.56.x_ref), custom_call_target="tpu_custom_call" | custom-call | tf_op jit(solution)/shard_map/whiten/pallas_call | solution.py:25
  3.5 0.9 copy.13
  4.5 0.1 rev.3
  4.6 0.1 reshape_reshape.7
  4.8 0.0 copy-done
  4.8 0.1 constant_dynamic-slice_fusion
  4.9 0.1 copy.9
  5.0 0.7 convolution_convert_fusion.1
  5.6 2.0 %copy.11 = bf16[32,16,1536]{2,1,0:T(8,128)(2,1)} copy(bf16[32,16,1536]{2,0,1:T(8,128)(2,1)S(1)} %bitcast.30) | data formatting | bytes 3145728 | tf_op jit(solution)/shard_map/reshape | solution.py:118
  7.7 10.6 %all-to-all-start = ((bf16[32,16,1536]{2,1,0:T(8,128)(2,1)}), bf16[32,16,1536]{2,1,0:T(8,128)(2,1)S(1)}, u32[]{:S(2)}, u32[]{:S(2)}) async-start(bf16[32,16,1536]{2,1,0:T(8,128)(2,1)} %copy.11), calls=%async_computation | async-start | bytes 3145728 | tf_op jit(solution)/shard_map/all_to_all | solution.py:119
  18.3 0.0 copy-done.1
  18.3 0.9 reshape.66.s
  19.2 0.0 copy-done.2
  19.2 0.0 copy-done.3
  19.2 0.1 add.28
  19.3 0.1 iota_compare_fusion.1
  19.4 0.1 lt.37
  19.5 36.7 %all-to-all-done = bf16[32,16,1536]{2,1,0:T(8,128)(2,1)S(1)} async-done(((bf16[32,16,1536]{2,1,0:T(8,128)(2,1)}), bf16[32,16,1536]{2,1,0:T(8,128)(2,1)S(1)}, u32[]{:S(2)}, u32[]{:S(2)}) %all-to-all-start) | async-done | bytes 1572896 | tf_op jit(solution)/shard_map/all_to_all | solution.py:119
  56.2 1.9 %reshape.60 = bf16[192,4096]{1,0:T(8,128)(2,1)S(1)} reshape(bf16[32,16,1536]{2,1,0:T(8,128)(2,1)S(1)} %all-to-all-done) | data formatting | bytes 3145728 | tf_op jit(solution)/shard_map/reshape | solution.py:120
  58.0 3.6 %convolution_convert_fusion = bf16[576,4096]{1,0:T(8,128)(2,1)} fusion(bf16[192,4096]{1,0:T(8,128)(2,1)S(1)} %reshape.60, s32[576]{0:T(1024)S(1)} %add.28, pred[576]{0:T(1024)(128)(4,1)S(1)} %lt.37), kind=kOutput, calls=%fused_computation | convolution fusion | flops 908550144 | bytes 6294336 | tf_op jit(solution)/shard_map/dot_general | solution.py:125
  61.6 10.1 %xcorr.1 = f32[16,40,1024]{2,1,0:T(8,128)} custom-call(f32[12,1,5120]{2,1,0:T(1,128)} %reshape.66.s, bf16[12,48,4096]{2,1,0:T(8,128)(2,1)} %bitcast.29), custom_call_target="tpu_custom_call" | custom-call | flops 4831838208 | bytes 7323648 | tf_op jit(solution)/shard_map/xcorr/pallas_call | solution.py:84
  71.7 1.9 %dynamic-slice_bitcast_fusion.1 = (f32[8,40,1024]{2,1,0:T(8,128)S(1)}, f32[8,40,1024]{2,1,0:T(8,128)S(1)}) fusion(f32[8,2,40,1024]{3,2,1,0:T(8,128)} %bitcast.31, s32[]{:T(128)S(6)} %select_n.12, s32[]{:T(128)S(6)} %select_n.13), kind=kLoop, calls=%fused_computation.5 | loop fusion | bytes 5242888 | tf_op jit(solution)/shard_map/jit(dynamic_index_in_dim)/squeeze | solution.py:137
  73.6 4.1 %collective-permute-start = (f32[8,40,1024]{2,1,0:T(8,128)S(1)}, f32[8,40,1024]{2,1,0:T(8,128)S(1)}, u32[]{:S(2)}, u32[]{:S(2)}) collective-permute-start(f32[8,40,1024]{2,1,0:T(8,128)S(1)} %get-tuple-element.6), channel_id=1, source_target_pairs={{0,32},{32,0},{1,33},{33,1},{2,34},{34,2},{3,35},{35,3},{4,36},{36... | collective-permute-start | bytes 3932168 | tf_op jit(solution)/shard_map/ppermute | solution.py:139
  77.7 2.6 %collective-permute-done = f32[8,40,1024]{2,1,0:T(8,128)S(1)} collective-permute-done((f32[8,40,1024]{2,1,0:T(8,128)S(1)}, f32[8,40,1024]{2,1,0:T(8,128)S(1)}, u32[]{:S(2)}, u32[]{:S(2)}) %collective-permute-start) | collective-permute-done | bytes 1310752 | tf_op jit(solution)/shard_map/ppermute | solution.py:139
  80.3 0.3 fusion
  80.6 0.6 reshape.63
  81.2 28.2 %all_to_all.10 = bf16[8,32,1152]{2,1,0:T(8,128)(2,1)S(1)} all-to-all(bf16[8,32,1152]{2,1,0:T(8,128)(2,1)S(1)} %reshape.63), channel_id=1, replica_groups=mesh['z'=8,'c'=2,'pairs'=32] {'z'}, dimensions={0} | all-to-all | bytes 1179648 | tf_op jit(solution)/shard_map/all_to_all | solution.py:141
  109.5 0.1 convert_reduce_fusion
  109.5 0.8 reshape.64
  (8 shorter events, 0.1 us)
Async XLA Ops:
  0.0 4.8 %copy-start = (s32[32,32,2]{1,2,0:T(2,128)S(1)}, s32[32,32,2]{1,2,0:T(2,128)}, u32[]{:S(2)}) copy-start(s32[32,32,2]{1,2,0:T(2,128)} %param.6) | copy-start | bytes 24580
  7.6 10.7 %copy-start.1 = (bf16[12,4096]{1,0:T(8,128)(2,1)S(1)}, bf16[12,4096]{1,0:T(8,128)(2,1)}, u32[]{:S(2)}) copy-start(bf16[12,4096]{1,0:T(8,128)(2,1)} %whiten.1) | copy-start | bytes 294916
  7.6 11.6 %copy-start.2 = (s32[1,12,48]{2,0,1:T(1,128)S(1)}, s32[1,12,48]{2,0,1:T(1,128)}, u32[]{:S(2)}) copy-start(s32[1,12,48]{2,0,1:T(1,128)} %param.8) | copy-start | bytes 6916
  7.6 11.6 %copy-start.3 = (s32[1,12,48]{2,0,1:T(1,128)S(1)}, s32[1,12,48]{2,0,1:T(1,128)}, u32[]{:S(2)}) copy-start(s32[1,12,48]{2,0,1:T(1,128)} %param.7) | copy-start | bytes 6916
  7.7 11.7 %copy-start.4 = (s32[1,12]{1,0:T(1,128)S(1)}, s32[1,12]{1,0:T(1,128)}, u32[]{:S(2)}) copy-start(s32[1,12]{1,0:T(1,128)} %param.9) | copy-start | bytes 148
  7.7 48.5 %all-to-all-start = ((bf16[32,16,1536]{2,1,0:T(8,128)(2,1)}), bf16[32,16,1536]{2,1,0:T(8,128)(2,1)S(1)}, u32[]{:S(2)}, u32[]{:S(2)}) async-start(bf16[32,16,1536]{2,1,0:T(8,128)(2,1)} %copy.11), calls=%async_computation | async-start | bytes 3145728 | tf_op jit(solution)/shard_map/all_to_all | solution.py:119
  73.6 6.8 %collective-permute-start = (f32[8,40,1024]{2,1,0:T(8,128)S(1)}, f32[8,40,1024]{2,1,0:T(8,128)S(1)}, u32[]{:S(2)}, u32[]{:S(2)}) collective-permute-start(f32[8,40,1024]{2,1,0:T(8,128)S(1)} %get-tuple-element.6), channel_id=1, source_target_pairs={{0,32},{32,0},{1,33},{33,1},{2,34},{34,2},{3,35},{35,3},{4,36},{36... | collective-permute-start | bytes 3932168 | tf_op jit(solution)/shard_map/ppermute | solution.py:139

commit v11 on v6

--- a/solution.py
+++ b/solution.py
@@ -47,7 +47,7 @@
     return jnp.concatenate(acc, axis=1)
 
 
-def corr_kernel(src_ref, p_ref, o_ref, *, win, scale, block_rows):
+def corr_kernel(core_ref, src_ref, p_ref, kept_ref, sent_ref, o_ref, *, win, scale, block_rows):
     group, rows = p_ref.shape[0], p_ref.shape[1]
     pad = o_ref.shape[1] - block_rows
     if pad:
@@ -61,30 +61,43 @@
             take = min(block_rows - at, (u + 1) * rows - first)
             o_ref[blk, at: at + take, :] = cc[first - u * rows: first - u * rows + take]
             first += take
+    even_core = core_ref[0] == 0
+    for half in range(kept_ref.shape[0]):
+        even, odd = o_ref[2 * half], o_ref[2 * half + 1]
+        kept_ref[half] = jnp.where(even_core, even, odd)
+        sent_ref[half] = jnp.where(even_core, odd, even)
 
 
-def correlate(src, partner_rows, scale, block_rows):
+def correlate(core, src, partner_rows, scale, block_rows):
     traces, rows, win = partner_rows.shape
     span = src.shape[-1]
     group = block_rows // math.gcd(block_rows, rows)
     blocks = group * rows // block_rows
+    if blocks % 2:
+        group, blocks = 2 * group, 2 * blocks
     padded = -(-block_rows // 8) * 8
     flops = 2 * traces * rows * win * LAGS
+    half_shape = jax.ShapeDtypeStruct((traces * rows // block_rows // 2, padded, LAGS), jnp.float32)
+    out_spec = pl.BlockSpec((blocks // 2, padded, LAGS), lambda g, c: (g, 0, 0))
     return pl.pallas_call(
-        lambda s, p, o: corr_kernel(s, p, o, win=win, scale=scale, block_rows=block_rows),
-        grid=(traces // group,),
-        in_specs=[
-            pl.BlockSpec((group, 1, span), lambda g: (g, 0, 0)),
-            pl.BlockSpec((group, rows, win), lambda g: (g, 0, 0)),
-        ],
-        out_specs=pl.BlockSpec((blocks, padded, LAGS), lambda g: (g, 0, 0)),
-        out_shape=jax.ShapeDtypeStruct((traces * rows // block_rows, padded, LAGS), jnp.float32),
+        lambda c, s, p, k, o, w: corr_kernel(c, s, p, k, o, w, win=win, scale=scale, block_rows=block_rows),
+        grid_spec=pltpu.PrefetchScalarGridSpec(
+            num_scalar_prefetch=1,
+            grid=(traces // group,),
+            in_specs=[
+                pl.BlockSpec((group, 1, span), lambda g, c: (g, 0, 0)),
+                pl.BlockSpec((group, rows, win), lambda g, c: (g, 0, 0)),
+            ],
+            out_specs=[out_spec, out_spec],
+            scratch_shapes=[pltpu.VMEM((blocks, padded, LAGS), jnp.float32)],
+        ),
+        out_shape=[half_shape, half_shape],
         cost_estimate=pl.CostEstimate(
             flops=flops, transcendentals=0,
             bytes_accessed=traces * (rows * win * 2 + span * 4 + rows * LAGS * 4),
         ),
         name="xcorr",
-    )(src.reshape(traces, 1, span), partner_rows)
+    )(core.reshape(1), src.reshape(traces, 1, span), partner_rows)
 
 
 def shards(record, requested, partners, codes, counts):
@@ -120,11 +133,8 @@
     total_windows = window_count * tm_count
     scale = 1.0 / math.sqrt(window_len * total_windows)
     block_rows = trace_count * per_trace // tm_count
-    lagged = correlate(src, picked, scale, block_rows)
-    lagged = lagged.reshape(chips, cores, lagged.shape[1], LAGS)
-    core = lax.axis_index("c")
-    kept = lax.dynamic_index_in_dim(lagged, core, axis=1, keepdims=False)
-    given = lax.dynamic_index_in_dim(lagged, cores - 1 - core, axis=1, keepdims=False)
+    core = lax.axis_index("c").astype(jnp.int32)
+    kept, given = correlate(core, src, picked, scale, block_rows)
     got = lax.ppermute(given, "c", [(0, 1), (1, 0)])
     chip_sums = (kept + got)[:, :block_rows].astype(jnp.bfloat16).reshape(chips, 32, block_rows * LAGS // 32)
     arrived_sums = lax.all_to_all(chip_sums, "z", 0, 0, tiled=True)

time: 110 us -> 110 us (level)
  local copies, waits for them, and re-layouts: 9 us -> 7.12 us
  other arithmetic: 3.64 us -> 4.9 us
    squeeze x1 -> x0, local copies, waits for them, and re-layouts: 1.89 us -> none  [shards(): kept = lax.dynamic_index_in_dim(lagged, core, axis=1, keepdims=False)]
    another operation x1, other arithmetic: 0.27 us -> 1.51 us
where the time goes in v11:
time: 110 us; the launch traced here: 109 us
  waiting for transfers between devices  39.3 us (36%)
  blocking collectives  28.2 us (26%)
  starting transfers between devices  14.7 us (13%)
  Pallas kernels  10 us (9%)
  local copies, waits for them, and re-layouts  7.12 us (6%)
  other arithmetic  4.9 us (4%)
  matrix products  4.2 us (4%)
    all_to_all x1, waiting for transfers between devices, shards(): arrived = lax.all_to_all(outgoing, 'pairs', 0, 0, tiled=True)  36.5 us
    all_to_all x1, blocking collectives, shards(): arrived_sums = lax.all_to_all(chip_sums, 'z', 0, 0, tiled=True)  28.2 us
    all_to_all x1, starting transfers between devices, shards(): arrived = lax.all_to_all(outgoing, 'pairs', 0, 0, tiled=True)  10.6 us
    pallas_call x1, Pallas kernels, correlate(): pl.pallas_call(lambda c, s, p, k, o, w: corr_kernel(c, s, p, k, o, w, win...  10 us
    ppermute x1, starting transfers between devices, shards(): got = lax.ppermute(given, 'c', [(0, 1), (1, 0)])  4.09 us
    dot_general x1, matrix products, shards(): jnp.dot(pick_recv.astype(jnp.bfloat16), trace_pool, preferred_element_typ...  3.57 us
    ppermute x1, waiting for transfers between devices, shards(): got = lax.ppermute(given, 'c', [(0, 1), (1, 0)])  2.85 us
  transfers between devices with their start and end apart: 2, of which 2 were waited for; matrix products, arithmetic and copies ran while one was open for 1% of the time, Pallas kernels for 0%

profile of v11, /device:TPU:1, one launch (start us, length us, event | category | flops | bytes accessed | tf_op | source)
XLA Modules:
  0.0 108.7 jit_solution(4744221244594524551)
XLA Ops:
  0.0 0.0 copy-start
  0.0 1.0 convert_reduce_fusion.1
  1.0 1.1 %fusion.7 = f32[4,3]{0,1:T(4,128)S(1)} fusion(bf16[4,3,1,4096]{3,0,2,1:T(4,128)(2,1)} %param.5, f32[4,3]{0,1:T(4,128)S(1)} %broadcast_multiply_fusion), kind=kLoop, calls=%fused_computation.13 | loop fusion | flops 196596 | bytes 98400 | tf_op jit(solution)/shard_map/reduce_sum | solution.py:18
  2.2 0.0 copy-done
  2.2 0.1 constant_dynamic-slice_fusion
  2.3 0.1 copy.9
  2.4 1.0 fusion.8
  3.4 0.1 reshape.84
  3.5 0.1 rev.3
  3.6 0.1 reshape_reshape.3
  3.8 0.6 convolution_convert_fusion.1
  4.4 2.0 %copy.12 = bf16[32,16,1536]{2,1,0:T(8,128)(2,1)} copy(bf16[32,16,1536]{2,0,1:T(8,128)(2,1)S(1)} %bitcast.23) | data formatting | bytes 3145728 | tf_op jit(solution)/shard_map/reshape | solution.py:120
  6.5 10.6 %all-to-all-start = ((bf16[32,16,1536]{2,1,0:T(8,128)(2,1)}), bf16[32,16,1536]{2,1,0:T(8,128)(2,1)S(1)}, u32[]{:S(2)}, u32[]{:S(2)}) async-start(bf16[32,16,1536]{2,1,0:T(8,128)(2,1)} %copy.12), calls=%async_computation | async-start | bytes 3145728 | tf_op jit(solution)/shard_map/all_to_all | solution.py:121
  17.1 0.1 copy.8
  17.2 0.1 iota_compare_fusion.1
  17.3 0.1 lt.30
  17.4 0.0 copy-done.1
  17.4 0.0 copy-done.2
  17.4 0.1 add.29
  17.5 0.1 convert_element_type.26
  17.6 0.9 reshape.91.s
  18.5 36.5 %all-to-all-done = bf16[32,16,1536]{2,1,0:T(8,128)(2,1)S(1)} async-done(((bf16[32,16,1536]{2,1,0:T(8,128)(2,1)}), bf16[32,16,1536]{2,1,0:T(8,128)(2,1)S(1)}, u32[]{:S(2)}, u32[]{:S(2)}) %all-to-all-start) | async-done | bytes 1572896 | tf_op jit(solution)/shard_map/all_to_all | solution.py:121
  55.0 1.9 %reshape.86 = bf16[192,4096]{1,0:T(8,128)(2,1)S(1)} reshape(bf16[32,16,1536]{2,1,0:T(8,128)(2,1)S(1)} %all-to-all-done) | data formatting | bytes 3145728 | tf_op jit(solution)/shard_map/reshape | solution.py:122
  56.8 3.6 %convolution_convert_fusion = bf16[576,4096]{1,0:T(8,128)(2,1)} fusion(bf16[192,4096]{1,0:T(8,128)(2,1)S(1)} %reshape.86, s32[576]{0:T(1024)S(1)} %add.29, pred[576]{0:T(1024)(128)(4,1)S(1)} %lt.30), kind=kOutput, calls=%fused_computation | convolution fusion | flops 908550144 | bytes 6294336 | tf_op jit(solution)/shard_map/dot_general | solution.py:127
  60.4 10.0 %xcorr.1 = (f32[8,40,1024]{2,1,0:T(8,128)}, f32[8,40,1024]{2,1,0:T(8,128)}) custom-call(s32[1]{0:T(128)} %bitcast.c, f32[12,1,5120]{2,1,0:T(1,128)} %reshape.91.s, bf16[12,48,4096]{2,1,0:T(8,128)(2,1)} %bitcast.22), custom_call_target="tpu_custom_call" | custom-call | flops 4831838208 | bytes 7323648 | tf_op jit(solution)/shard_map/xcorr/pallas_call | solution.py:82
  70.4 4.1 %collective-permute-start = (f32[8,40,1024]{2,1,0:T(8,128)}, f32[8,40,1024]{2,1,0:T(8,128)S(1)}, u32[]{:S(2)}, u32[]{:S(2)}) collective-permute-start(f32[8,40,1024]{2,1,0:T(8,128)} %get-tuple-element.8), channel_id=1, source_target_pairs={{0,32},{32,0},{1,33},{33,1},{2,34},{34,2},{3,35},{35,3},{4,36},{36... | collective-permute-start | bytes 3932168 | tf_op jit(solution)/shard_map/ppermute | solution.py:138
  74.5 2.9 %collective-permute-done = f32[8,40,1024]{2,1,0:T(8,128)S(1)} collective-permute-done((f32[8,40,1024]{2,1,0:T(8,128)}, f32[8,40,1024]{2,1,0:T(8,128)S(1)}, u32[]{:S(2)}, u32[]{:S(2)}) %collective-permute-start) | collective-permute-done | bytes 1310752 | tf_op jit(solution)/shard_map/ppermute | solution.py:138
  77.4 1.5 %fusion = bf16[8,36,1024]{2,1,0:T(8,128)(2,1)S(1)} fusion(f32[8,40,1024]{2,1,0:T(8,128)S(1)} %collective-permute-done, f32[8,40,1024]{2,1,0:T(8,128)} %get-tuple-element.7), kind=kLoop, calls=%fused_computation.3 | loop fusion | flops 589824 | bytes 2949120 | tf_op jit(solution)/shard_map/convert.4
  78.9 0.6 reshape.88
  79.6 28.2 %all_to_all.10 = bf16[8,32,1152]{2,1,0:T(8,128)(2,1)S(1)} all-to-all(bf16[8,32,1152]{2,1,0:T(8,128)(2,1)S(1)} %reshape.88), channel_id=1, replica_groups=mesh['z'=8,'c'=2,'pairs'=32] {'z'}, dimensions={0} | all-to-all | bytes 1179648 | tf_op jit(solution)/shard_map/all_to_all | solution.py:140
  107.8 0.1 convert_reduce_fusion
  107.9 0.8 reshape.89
  (9 shorter events, 0.1 us)
Async XLA Ops:
  0.0 2.2 %copy-start = (s32[32,32,2]{1,2,0:T(2,128)S(1)}, s32[32,32,2]{1,2,0:T(2,128)}, u32[]{:S(2)}) copy-start(s32[32,32,2]{1,2,0:T(2,128)} %param.6) | copy-start | bytes 24580
  6.5 10.7 %copy-start.3 = (s32[1,12]{1,0:T(1,128)S(1)}, s32[1,12]{1,0:T(1,128)}, u32[]{:S(2)}) copy-start(s32[1,12]{1,0:T(1,128)} %param.9) | copy-start | bytes 148
  6.5 10.9 %copy-start.1 = (s32[1,12,48]{2,0,1:T(1,128)S(1)}, s32[1,12,48]{2,0,1:T(1,128)}, u32[]{:S(2)}) copy-start(s32[1,12,48]{2,0,1:T(1,128)} %param.8) | copy-start | bytes 6916
  6.5 10.9 %copy-start.2 = (s32[1,12,48]{2,0,1:T(1,128)S(1)}, s32[1,12,48]{2,0,1:T(1,128)}, u32[]{:S(2)}) copy-start(s32[1,12,48]{2,0,1:T(1,128)} %param.7) | copy-start | bytes 6916
  6.5 48.5 %all-to-all-start = ((bf16[32,16,1536]{2,1,0:T(8,128)(2,1)}), bf16[32,16,1536]{2,1,0:T(8,128)(2,1)S(1)}, u32[]{:S(2)}, u32[]{:S(2)}) async-start(bf16[32,16,1536]{2,1,0:T(8,128)(2,1)} %copy.12), calls=%async_computation | async-start | bytes 3145728 | tf_op jit(solution)/shard_map/all_to_all | solution.py:121
  70.4 7.0 %collective-permute-start = (f32[8,40,1024]{2,1,0:T(8,128)}, f32[8,40,1024]{2,1,0:T(8,128)S(1)}, u32[]{:S(2)}, u32[]{:S(2)}) collective-permute-start(f32[8,40,1024]{2,1,0:T(8,128)} %get-tuple-element.8), channel_id=1, source_target_pairs={{0,32},{32,0},{1,33},{33,1},{2,34},{34,2},{3,35},{35,3},{4,36},{36... | collective-permute-start | bytes 3932168 | tf_op jit(solution)/shard_map/ppermute | solution.py:138

commit v12 on v11

--- a/solution.py
+++ b/solution.py
@@ -75,7 +75,7 @@
     blocks = group * rows // block_rows
     if blocks % 2:
         group, blocks = 2 * group, 2 * blocks
-    padded = -(-block_rows // 8) * 8
+    padded = block_rows
     flops = 2 * traces * rows * win * LAGS
     half_shape = jax.ShapeDtypeStruct((traces * rows // block_rows // 2, padded, LAGS), jnp.float32)
     out_spec = pl.BlockSpec((blocks // 2, padded, LAGS), lambda g, c: (g, 0, 0))

time: 110 us -> 111 us (level)
  local copies, waits for them, and re-layouts: 7.12 us -> 9.23 us
    pallas_call x0 -> x1, local copies, waits for them, and re-layouts: none -> 2.11 us  [correlate(): pl.pallas_call(lambda c, s, p, k, o, w: corr_kernel(c, s, p, k, o, w, win...]
    another operation x1 -> x0, other arithmetic: 1.51 us -> none
where the time goes in v12:
time: 111 us; the launch traced here: 110 us
  waiting for transfers between devices  38.9 us (35%)
  blocking collectives  28.2 us (25%)
  starting transfers between devices  14.7 us (13%)
  Pallas kernels  10 us (9%)
  local copies, waits for them, and re-layouts  9.23 us (8%)
  matrix products  4.2 us (4%)
  other arithmetic  4.17 us (4%)
    all_to_all x1, waiting for transfers between devices, shards(): arrived = lax.all_to_all(outgoing, 'pairs', 0, 0, tiled=True)  36.5 us
    all_to_all x1, blocking collectives, shards(): arrived_sums = lax.all_to_all(chip_sums, 'z', 0, 0, tiled=True)  28.2 us
    all_to_all x1, starting transfers between devices, shards(): arrived = lax.all_to_all(outgoing, 'pairs', 0, 0, tiled=True)  10.6 us
    pallas_call x1, Pallas kernels, correlate(): pl.pallas_call(lambda c, s, p, k, o, w: corr_kernel(c, s, p, k, o, w, win...  10 us
    ppermute x1, starting transfers between devices, shards(): got = lax.ppermute(given, 'c', [(0, 1), (1, 0)])  4.1 us
    dot_general x1, matrix products, shards(): jnp.dot(pick_recv.astype(jnp.bfloat16), trace_pool, preferred_element_typ...  3.57 us
    ppermute x1, waiting for transfers between devices, shards(): got = lax.ppermute(given, 'c', [(0, 1), (1, 0)])  2.45 us
  transfers between devices with their start and end apart: 2, of which 2 were waited for; matrix products, arithmetic and copies ran while one was open for 1% of the time, Pallas kernels for 0%

profile of v12, /device:TPU:1, one launch (start us, length us, event | category | flops | bytes accessed | tf_op | source)
XLA Modules:
  0.0 109.7 jit_solution(4041459764481253118)
XLA Ops:
  0.0 0.0 copy-start
  0.0 1.0 convert_reduce_fusion.1
  1.0 1.1 %fusion.7 = f32[4,3]{0,1:T(4,128)S(1)} fusion(bf16[4,3,1,4096]{3,0,2,1:T(4,128)(2,1)} %param.5, f32[4,3]{0,1:T(4,128)S(1)} %broadcast_multiply_fusion), kind=kLoop, calls=%fused_computation.13 | loop fusion | flops 196596 | bytes 98400 | tf_op jit(solution)/shard_map/reduce_sum | solution.py:18
  2.2 0.0 copy-done
  2.2 0.1 constant_dynamic-slice_fusion
  2.3 0.1 copy.14
  2.4 1.0 fusion.8
  3.4 0.1 reshape.84
  3.5 0.1 rev.3
  3.6 0.1 reshape_reshape.3
  3.8 0.6 convolution_convert_fusion.1
  4.4 2.0 %copy.17 = bf16[32,16,1536]{2,1,0:T(8,128)(2,1)} copy(bf16[32,16,1536]{2,0,1:T(8,128)(2,1)S(1)} %bitcast.23) | data formatting | bytes 3145728 | tf_op jit(solution)/shard_map/reshape | solution.py:120
  6.5 10.6 %all-to-all-start = ((bf16[32,16,1536]{2,1,0:T(8,128)(2,1)}), bf16[32,16,1536]{2,1,0:T(8,128)(2,1)S(1)}, u32[]{:S(2)}, u32[]{:S(2)}) async-start(bf16[32,16,1536]{2,1,0:T(8,128)(2,1)} %copy.17), calls=%async_computation | async-start | bytes 3145728 | tf_op jit(solution)/shard_map/all_to_all | solution.py:121
  17.1 0.1 copy.13
  17.2 0.0 copy-done.4
  17.2 0.1 iota_compare_fusion.1
  17.3 0.1 lt.30
  17.4 0.1 add.29
  17.5 0.1 convert_element_type.28
  17.6 0.9 reshape.91.s
  18.5 36.5 %all-to-all-done = bf16[32,16,1536]{2,1,0:T(8,128)(2,1)S(1)} async-done(((bf16[32,16,1536]{2,1,0:T(8,128)(2,1)}), bf16[32,16,1536]{2,1,0:T(8,128)(2,1)S(1)}, u32[]{:S(2)}, u32[]{:S(2)}) %all-to-all-start) | async-done | bytes 1572896 | tf_op jit(solution)/shard_map/all_to_all | solution.py:121
  55.0 1.9 %reshape.86 = bf16[192,4096]{1,0:T(8,128)(2,1)S(1)} reshape(bf16[32,16,1536]{2,1,0:T(8,128)(2,1)S(1)} %all-to-all-done) | data formatting | bytes 3145728 | tf_op jit(solution)/shard_map/reshape | solution.py:122
  56.8 3.6 %convolution_convert_fusion = bf16[576,4096]{1,0:T(8,128)(2,1)} fusion(bf16[192,4096]{1,0:T(8,128)(2,1)S(1)} %reshape.86, s32[576]{0:T(1024)S(1)} %add.29, pred[576]{0:T(1024)(128)(4,1)S(1)} %lt.30), kind=kOutput, calls=%fused_computation | convolution fusion | flops 908550144 | bytes 6294336 | tf_op jit(solution)/shard_map/dot_general | solution.py:127
  60.4 10.0 %xcorr.1 = (f32[8,36,1024]{2,1,0:T(8,128)}, f32[8,36,1024]{2,1,0:T(8,128)}) custom-call(s32[1]{0:T(128)} %bitcast.c, f32[12,1,5120]{2,1,0:T(1,128)} %reshape.91.s, bf16[12,48,4096]{2,1,0:T(8,128)(2,1)} %bitcast.22), custom_call_target="tpu_custom_call" | custom-call | flops 4831838208 | bytes 7323648 | tf_op jit(solution)/shard_map/xcorr/pallas_call | solution.py:82
  70.4 2.1 %copy.18 = f32[8,36,1024]{2,0,1:T(8,128)S(1)} copy(f32[8,36,1024]{2,1,0:T(8,128)} %get-tuple-element.8) | data formatting | bytes 2359296 | tf_op jit(solution)/shard_map/xcorr/pallas_call | solution.py:82
  72.5 4.1 %collective-permute-start = (f32[8,36,1024]{2,0,1:T(8,128)S(1)}, f32[8,36,1024]{2,0,1:T(8,128)S(1)}, u32[]{:S(2)}, u32[]{:S(2)}) collective-permute-start(f32[8,36,1024]{2,0,1:T(8,128)S(1)} %copy.18), channel_id=1, source_target_pairs={{0,32},{32,0},{1,33},{33,1},{2,34},{34,2},{3,35},{35,3},{4,36},{36... | collective-permute-start | bytes 3538952 | tf_op jit(solution)/shard_map/ppermute | solution.py:138
  76.7 2.5 %collective-permute-done = f32[8,36,1024]{2,0,1:T(8,128)S(1)} collective-permute-done((f32[8,36,1024]{2,0,1:T(8,128)S(1)}, f32[8,36,1024]{2,0,1:T(8,128)S(1)}, u32[]{:S(2)}, u32[]{:S(2)}) %collective-permute-start) | collective-permute-done | bytes 1179680 | tf_op jit(solution)/shard_map/ppermute | solution.py:138
  79.1 0.8 fusion
  79.9 0.6 reshape.88
  80.5 28.2 %all_to_all.10 = bf16[8,32,1152]{2,1,0:T(8,128)(2,1)S(1)} all-to-all(bf16[8,32,1152]{2,1,0:T(8,128)(2,1)S(1)} %reshape.88), channel_id=1, replica_groups=mesh['z'=8,'c'=2,'pairs'=32] {'z'}, dimensions={0} | all-to-all | bytes 1179648 | tf_op jit(solution)/shard_map/all_to_all | solution.py:140
  108.8 0.1 convert_reduce_fusion
  108.9 0.8 reshape.89
  (12 shorter events, 0.1 us)
Async XLA Ops:
  0.0 2.2 %copy-start = (s32[32,32,2]{1,2,0:T(2,128)S(1)}, s32[32,32,2]{1,2,0:T(2,128)}, u32[]{:S(2)}) copy-start(s32[32,32,2]{1,2,0:T(2,128)} %param.6) | copy-start | bytes 24580
  6.5 10.7 %copy-start.4 = (s32[1,12]{1,0:T(1,128)S(1)}, s32[1,12]{1,0:T(1,128)}, u32[]{:S(2)}) copy-start(s32[1,12]{1,0:T(1,128)} %param.9) | copy-start | bytes 148
  6.5 10.9 %copy-start.2 = (s32[1,12,48]{2,0,1:T(1,128)S(1)}, s32[1,12,48]{2,0,1:T(1,128)}, u32[]{:S(2)}) copy-start(s32[1,12,48]{2,0,1:T(1,128)} %param.8) | copy-start | bytes 6916
  6.5 10.9 %copy-start.3 = (s32[1,12,48]{2,0,1:T(1,128)S(1)}, s32[1,12,48]{2,0,1:T(1,128)}, u32[]{:S(2)}) copy-start(s32[1,12,48]{2,0,1:T(1,128)} %param.7) | copy-start | bytes 6916
  6.5 48.5 %all-to-all-start = ((bf16[32,16,1536]{2,1,0:T(8,128)(2,1)}), bf16[32,16,1536]{2,1,0:T(8,128)(2,1)S(1)}, u32[]{:S(2)}, u32[]{:S(2)}) async-start(bf16[32,16,1536]{2,1,0:T(8,128)(2,1)} %copy.17), calls=%async_computation | async-start | bytes 3145728 | tf_op jit(solution)/shard_map/all_to_all | solution.py:121
  70.4 8.7 %copy-start.1 = (f32[8,36,1024]{2,1,0:T(8,128)S(1)}, f32[8,36,1024]{2,1,0:T(8,128)}, u32[]{:S(2)}) copy-start(f32[8,36,1024]{2,1,0:T(8,128)} %get-tuple-element.7) | copy-start | bytes 3538948
  72.5 6.6 %collective-permute-start = (f32[8,36,1024]{2,0,1:T(8,128)S(1)}, f32[8,36,1024]{2,0,1:T(8,128)S(1)}, u32[]{:S(2)}, u32[]{:S(2)}) collective-permute-start(f32[8,36,1024]{2,0,1:T(8,128)S(1)} %copy.18), channel_id=1, source_target_pairs={{0,32},{32,0},{1,33},{33,1},{2,34},{34,2},{3,35},{35,3},{4,36},{36... | collective-permute-start | bytes 3538952 | tf_op jit(solution)/shard_map/ppermute | solution.py:138

commit v13 on v11

--- a/solution.py
+++ b/solution.py
@@ -124,8 +124,7 @@
     live_rows = (jnp.arange(per_trace, dtype=jnp.int32)[None, :] < counts[0][:, None]).reshape(-1)
     pool_rows = owners * capacity * comp_count
     pick_recv = (row_ids[:, None] == jnp.arange(pool_rows, dtype=jnp.int32)[None, :]) & live_rows[:, None]
-    picked = jnp.dot(pick_recv.astype(jnp.bfloat16), trace_pool, preferred_element_type=jnp.float32)
-    picked = picked.astype(jnp.bfloat16).reshape(trace_count, per_trace, window_len)
+    pick_recv = pick_recv.astype(jnp.bfloat16).reshape(2, trace_count // 2 * per_trace, pool_rows)
     half = LAGS // 2
     own = whitened.reshape(trace_count, window_len).astype(jnp.float32)
     span = ((window_len + LAGS + LANE - 1) // LANE) * LANE
@@ -134,9 +133,16 @@
     scale = 1.0 / math.sqrt(window_len * total_windows)
     block_rows = trace_count * per_trace // tm_count
     core = lax.axis_index("c").astype(jnp.int32)
-    kept, given = correlate(core, src, picked, scale, block_rows)
-    got = lax.ppermute(given, "c", [(0, 1), (1, 0)])
-    chip_sums = (kept + got)[:, :block_rows].astype(jnp.bfloat16).reshape(chips, 32, block_rows * LAGS // 32)
+    sums = []
+    for part in range(2):
+        picked = jnp.dot(pick_recv[part], trace_pool, preferred_element_type=jnp.float32)
+        picked = picked.astype(jnp.bfloat16).reshape(trace_count // 2, per_trace, window_len)
+        own_part = src[part * trace_count // 2: (part + 1) * trace_count // 2]
+        kept, given = correlate(core, own_part, picked, scale, block_rows)
+        got = lax.ppermute(given, "c", [(0, 1), (1, 0)])
+        sums.append(kept + got)
+    chip_sums = jnp.concatenate(sums, axis=0)
+    chip_sums = chip_sums[:, :block_rows].astype(jnp.bfloat16).reshape(chips, 32, block_rows * LAGS // 32)
     arrived_sums = lax.all_to_all(chip_sums, "z", 0, 0, tiled=True)
     total = jnp.sum(arrived_sums.astype(jnp.float32), axis=0)
     return total.reshape(1, block_rows, LAGS)

time: 110 us -> 113 us (1.027)
  Pallas kernels: 10 us -> 12.3 us
  starting transfers between devices: 14.7 us -> 16.8 us
  waiting for transfers between devices: 39.3 us -> 37.8 us
    pallas_call x1 -> x2, Pallas kernels: 10 us -> 12.3 us  [correlate(): pl.pallas_call(lambda c, s, p, k, o, w: corr_kernel(c, s, p, k, o, w, win...]
    ppermute x1 -> x2, starting transfers between devices: 4.09 us -> 6.14 us  [shards(): got = lax.ppermute(given, 'c', [(0, 1), (1, 0)])]
    another operation x1 -> x2, other arithmetic: 1.51 us -> 0.15 us
    dot_general x1 -> x2, matrix products: 3.57 us -> 4.4 us  [shards(): jnp.dot(pick_recv[part], trace_pool, preferred_element_type=jnp.float32)]
    ppermute x1 -> x2, waiting for transfers between devices: 2.85 us -> 2.17 us  [shards(): got = lax.ppermute(given, 'c', [(0, 1), (1, 0)])]
  transfers between devices with their start and end apart: 2 -> 3, of which waited for: 2 -> 2; matrix products, arithmetic and copies ran while one was open for 1% -> 4% of each run, Pallas kernels for 0% -> 5%
where the time goes in v13:
time: 113 us; the launch traced here: 112 us
  waiting for transfers between devices  37.8 us (33%)
  blocking collectives  28.6 us (25%)
  starting transfers between devices  16.8 us (15%)
  Pallas kernels  12.3 us (11%)
  local copies, waits for them, and re-layouts  7.78 us (7%)
  matrix products  5.04 us (4%)
  other arithmetic  3.8 us (3%)
    all_to_all x1, waiting for transfers between devices, shards(): arrived = lax.all_to_all(outgoing, 'pairs', 0, 0, tiled=True)  35.6 us
    all_to_all x1, blocking collectives, shards(): arrived_sums = lax.all_to_all(chip_sums, 'z', 0, 0, tiled=True)  28.6 us
    pallas_call x2, Pallas kernels, correlate(): pl.pallas_call(lambda c, s, p, k, o, w: corr_kernel(c, s, p, k, o, w, win...  12.3 us
    all_to_all x1, starting transfers between devices, shards(): arrived = lax.all_to_all(outgoing, 'pairs', 0, 0, tiled=True)  10.6 us
    ppermute x2, starting transfers between devices, shards(): got = lax.ppermute(given, 'c', [(0, 1), (1, 0)])  6.14 us
    dot_general x2, matrix products, shards(): jnp.dot(pick_recv[part], trace_pool, preferred_element_type=jnp.float32)  4.4 us
  transfers between devices with their start and end apart: 3, of which 2 were waited for; matrix products, arithmetic and copies ran while one was open for 4% of the time, Pallas kernels for 5%

profile of v13, /device:TPU:1, one launch (start us, length us, event | category | flops | bytes accessed | tf_op | source)
XLA Modules:
  0.0 112.2 jit_solution(5971188470180205816)
XLA Ops:
  0.0 1.0 convert_reduce_fusion.1
  1.0 1.1 fusion.5
  2.2 0.1 constant_dynamic-slice_fusion
  2.3 0.1 copy.10
  2.4 1.0 fusion.6
  3.4 0.1 reshape.93
  3.5 0.1 rev.3
  3.6 0.1 reshape_reshape.3
  3.8 0.6 convolution_convert_fusion.2
  4.4 2.0 %copy.13 = bf16[32,16,1536]{2,1,0:T(8,128)(2,1)} copy(bf16[32,16,1536]{2,0,1:T(8,128)(2,1)S(1)} %bitcast.26) | data formatting | bytes 3145728 | tf_op jit(solution)/shard_map/reshape | solution.py:120
  6.5 10.6 %all-to-all-start = ((bf16[32,16,1536]{2,1,0:T(8,128)(2,1)}), bf16[32,16,1536]{2,1,0:T(8,128)(2,1)S(1)}, u32[]{:S(2)}, u32[]{:S(2)}) async-start(bf16[32,16,1536]{2,1,0:T(8,128)(2,1)} %copy.13), calls=%async_computation | async-start | bytes 3145728 | tf_op jit(solution)/shard_map/all_to_all | solution.py:121
  17.1 0.1 copy.9
  17.2 0.1 iota_compare_fusion.1
  17.3 0.1 lt.30
  17.5 0.1 convert_element_type.29
  17.7 0.8 copy.14.s
  18.4 0.7 reshape.97.s
  19.2 0.2 fusion
  19.4 35.6 %all-to-all-done = bf16[32,16,1536]{2,1,0:T(8,128)(2,1)S(1)} async-done(((bf16[32,16,1536]{2,1,0:T(8,128)(2,1)}), bf16[32,16,1536]{2,1,0:T(8,128)(2,1)S(1)}, u32[]{:S(2)}, u32[]{:S(2)}) %all-to-all-start) | async-done | bytes 1572896 | tf_op jit(solution)/shard_map/all_to_all | solution.py:121
  55.0 1.9 %reshape.95 = bf16[192,4096]{1,0:T(8,128)(2,1)S(1)} reshape(bf16[32,16,1536]{2,1,0:T(8,128)(2,1)S(1)} %all-to-all-done) | data formatting | bytes 3145728 | tf_op jit(solution)/shard_map/reshape | solution.py:122
  56.8 2.2 %convolution_convert_fusion.1 = bf16[288,4096]{1,0:T(8,128)(2,1)} fusion(bf16[192,4096]{1,0:T(8,128)(2,1)S(1)} %reshape.95, pred[576,192]{1,0:T(32,128)(4,1)S(1)} %fusion), kind=kOutput, calls=%fused_computation.1 | convolution fusion | flops 454164480 | bytes 4005888 | tf_op jit(solution)/shard_map/dot_general | solution.py:138
  59.0 6.1 %xcorr.2 = (f32[4,40,1024]{2,1,0:T(8,128)}, f32[4,40,1024]{2,1,0:T(8,128)}) custom-call(s32[1]{0:T(128)} %bitcast.c, f32[6,1,5120]{2,1,0:T(1,128)} %copy.14.s, bf16[6,48,4096]{2,1,0:T(8,128)(2,1)} %bitcast.28), custom_call_target="tpu_custom_call" | custom-call | flops 2415919104 | bytes 3661824 | tf_op jit(solution)/shard_map/xcorr/pallas_call | solution.py:82
  65.1 4.1 %collective-permute-start = (f32[4,40,1024]{2,1,0:T(8,128)}, f32[4,40,1024]{2,1,0:T(8,128)S(1)}, u32[]{:S(2)}, u32[]{:S(2)}) collective-permute-start(f32[4,40,1024]{2,1,0:T(8,128)} %get-tuple-element.10), channel_id=1, source_target_pairs={{0,32},{32,0},{1,33},{33,1},{2,34},{34,2},{3,35},{35,3},{4,36},{36... | collective-permute-start | bytes 1966088 | tf_op jit(solution)/shard_map/ppermute | solution.py:142
  69.2 2.2 %convolution_convert_fusion = bf16[288,4096]{1,0:T(8,128)(2,1)} fusion(bf16[192,4096]{1,0:T(8,128)(2,1)S(1)} %reshape.95, pred[576,192]{1,0:T(32,128)(4,1)S(1)} %fusion), kind=kOutput, calls=%fused_computation | convolution fusion | flops 454164480 | bytes 4005888 | tf_op jit(solution)/shard_map/dot_general | solution.py:138
  71.4 6.2 %xcorr.3 = (f32[4,40,1024]{2,1,0:T(8,128)}, f32[4,40,1024]{2,1,0:T(8,128)}) custom-call(s32[1]{0:T(128)} %bitcast.c, f32[6,1,5120]{2,1,0:T(1,128)} %reshape.97.s, bf16[6,48,4096]{2,1,0:T(8,128)(2,1)} %bitcast.27), custom_call_target="tpu_custom_call" | custom-call | flops 2415919104 | bytes 3661824 | tf_op jit(solution)/shard_map/xcorr/pallas_call | solution.py:82
  77.6 2.0 %collective-permute-start.1 = (f32[4,40,1024]{2,1,0:T(8,128)}, f32[4,40,1024]{2,1,0:T(8,128)S(1)}, u32[]{:S(2)}, u32[]{:S(2)}) collective-permute-start(f32[4,40,1024]{2,1,0:T(8,128)} %get-tuple-element.12), channel_id=1, source_target_pairs={{0,32},{32,0},{1,33},{33,1},{2,34},{34,2},{3,35},{35,3},{4,36},{36... | collective-permute-start | bytes 1966088 | tf_op jit(solution)/shard_map/ppermute | solution.py:142
  79.7 0.1 add_convert_fusion.1
  79.8 2.2 %collective-permute-done.1 = f32[4,40,1024]{2,1,0:T(8,128)S(1)} collective-permute-done((f32[4,40,1024]{2,1,0:T(8,128)}, f32[4,40,1024]{2,1,0:T(8,128)S(1)}, u32[]{:S(2)}, u32[]{:S(2)}) %collective-permute-start.1) | collective-permute-done | bytes 655392 | tf_op jit(solution)/shard_map/ppermute | solution.py:142
  82.1 0.6 reshape.99
  82.7 28.6 %all_to_all.10 = bf16[8,32,1152]{2,1,0:T(8,128)(2,1)S(1)} all-to-all(bf16[8,32,1152]{2,1,0:T(8,128)(2,1)S(1)} %reshape.99), channel_id=1, replica_groups=mesh['z'=8,'c'=2,'pairs'=32] {'z'}, dimensions={0} | all-to-all | bytes 1179648 | tf_op jit(solution)/shard_map/all_to_all | solution.py:146
  111.3 0.1 convert_reduce_fusion
  111.4 0.8 reshape.100
  (22 shorter events, 0.3 us)
Async XLA Ops:
  0.0 2.2 %copy-start = (s32[32,32,2]{1,2,0:T(2,128)S(1)}, s32[32,32,2]{1,2,0:T(2,128)}, u32[]{:S(2)}) copy-start(s32[32,32,2]{1,2,0:T(2,128)} %param.6) | copy-start | bytes 24580
  6.5 10.7 %copy-start.5 = (s32[1,12]{1,0:T(1,128)S(1)}, s32[1,12]{1,0:T(1,128)}, u32[]{:S(2)}) copy-start(s32[1,12]{1,0:T(1,128)} %param.9) | copy-start | bytes 148
  6.5 10.9 %copy-start.3 = (s32[1,12,48]{2,0,1:T(1,128)S(1)}, s32[1,12,48]{2,0,1:T(1,128)}, u32[]{:S(2)}) copy-start(s32[1,12,48]{2,0,1:T(1,128)} %param.8) | copy-start | bytes 6916
  6.5 10.9 %copy-start.4 = (s32[1,12,48]{2,0,1:T(1,128)S(1)}, s32[1,12,48]{2,0,1:T(1,128)}, u32[]{:S(2)}) copy-start(s32[1,12,48]{2,0,1:T(1,128)} %param.7) | copy-start | bytes 6916
  6.5 48.5 %all-to-all-start = ((bf16[32,16,1536]{2,1,0:T(8,128)(2,1)}), bf16[32,16,1536]{2,1,0:T(8,128)(2,1)S(1)}, u32[]{:S(2)}, u32[]{:S(2)}) async-start(bf16[32,16,1536]{2,1,0:T(8,128)(2,1)} %copy.13), calls=%async_computation | async-start | bytes 3145728 | tf_op jit(solution)/shard_map/all_to_all | solution.py:121
  65.1 14.5 %collective-permute-start = (f32[4,40,1024]{2,1,0:T(8,128)}, f32[4,40,1024]{2,1,0:T(8,128)S(1)}, u32[]{:S(2)}, u32[]{:S(2)}) collective-permute-start(f32[4,40,1024]{2,1,0:T(8,128)} %get-tuple-element.10), channel_id=1, source_target_pairs={{0,32},{32,0},{1,33},{33,1},{2,34},{34,2},{3,35},{35,3},{4,36},{36... | collective-permute-start | bytes 1966088 | tf_op jit(solution)/shard_map/ppermute | solution.py:142
  71.4 8.2 %copy-start.1 = (f32[4,40,1024]{2,1,0:T(8,128)S(1)}, f32[4,40,1024]{2,1,0:T(8,128)}, u32[]{:S(2)}) copy-start(f32[4,40,1024]{2,1,0:T(8,128)} %get-tuple-element.9) | copy-start | bytes 1966084
  77.6 4.3 %copy-start.2 = (f32[4,40,1024]{2,1,0:T(8,128)S(1)}, f32[4,40,1024]{2,1,0:T(8,128)}, u32[]{:S(2)}) copy-start(f32[4,40,1024]{2,1,0:T(8,128)} %get-tuple-element.11) | copy-start | bytes 1966084
  77.6 4.3 %collective-permute-start.1 = (f32[4,40,1024]{2,1,0:T(8,128)}, f32[4,40,1024]{2,1,0:T(8,128)S(1)}, u32[]{:S(2)}, u32[]{:S(2)}) collective-permute-start(f32[4,40,1024]{2,1,0:T(8,128)} %get-tuple-element.12), channel_id=1, source_target_pairs={{0,32},{32,0},{1,33},{33,1},{2,34},{34,2},{3,35},{35,3},{4,36},{36... | collective-permute-start | bytes 1966088 | tf_op jit(solution)/shard_map/ppermute | solution.py:142

commit v14 on v11

--- a/solution.py
+++ b/solution.py
@@ -116,16 +116,16 @@
     asked_of_me = lax.dynamic_index_in_dim(requested, own_index, axis=1, keepdims=False)
     pick_send = (asked_of_me[:, :, None] == jnp.arange(local_stations, dtype=jnp.int32)[None, None, :])
     outgoing = jnp.einsum("eis,sru->eiru", pick_send.astype(jnp.bfloat16), mine,
-                          preferred_element_type=jnp.float32)
-    outgoing = outgoing.astype(jnp.bfloat16).reshape(owners, capacity * 8, per_station // 8)
+                          preferred_element_type=jnp.bfloat16)
+    outgoing = outgoing.reshape(owners, capacity * 8, per_station // 8)
     arrived = lax.all_to_all(outgoing, "pairs", 0, 0, tiled=True)
     trace_pool = arrived.reshape(owners * capacity * comp_count, window_count * window_len)
     row_ids = (partners[0] * comp_count + codes[0]).reshape(-1)
     live_rows = (jnp.arange(per_trace, dtype=jnp.int32)[None, :] < counts[0][:, None]).reshape(-1)
     pool_rows = owners * capacity * comp_count
     pick_recv = (row_ids[:, None] == jnp.arange(pool_rows, dtype=jnp.int32)[None, :]) & live_rows[:, None]
-    picked = jnp.dot(pick_recv.astype(jnp.bfloat16), trace_pool, preferred_element_type=jnp.float32)
-    picked = picked.astype(jnp.bfloat16).reshape(trace_count, per_trace, window_len)
+    picked = jnp.dot(pick_recv.astype(jnp.bfloat16), trace_pool, preferred_element_type=jnp.bfloat16)
+    picked = picked.reshape(trace_count, per_trace, window_len)
     half = LAGS // 2
     own = whitened.reshape(trace_count, window_len).astype(jnp.float32)
     span = ((window_len + LAGS + LANE - 1) // LANE) * LANE

time: 110 us -> 110 us (level)
  no operation moved by 1% of the time
where the time goes in v14:
time: 110 us; the launch traced here: 109 us
  waiting for transfers between devices  39.5 us (36%)
  blocking collectives  28.2 us (26%)
  starting transfers between devices  14.7 us (13%)
  Pallas kernels  10 us (9%)
  local copies, waits for them, and re-layouts  6.96 us (6%)
  other arithmetic  4.88 us (4%)
  matrix products  4.2 us (4%)
    all_to_all x1, waiting for transfers between devices, shards(): arrived = lax.all_to_all(outgoing, 'pairs', 0, 0, tiled=True)  36.6 us
    all_to_all x1, blocking collectives, shards(): arrived_sums = lax.all_to_all(chip_sums, 'z', 0, 0, tiled=True)  28.2 us
    all_to_all x1, starting transfers between devices, shards(): arrived = lax.all_to_all(outgoing, 'pairs', 0, 0, tiled=True)  10.6 us
    pallas_call x1, Pallas kernels, correlate(): pl.pallas_call(lambda c, s, p, k, o, w: corr_kernel(c, s, p, k, o, w, win...  10 us
    ppermute x1, starting transfers between devices, shards(): got = lax.ppermute(given, 'c', [(0, 1), (1, 0)])  4.09 us
    dot_general x1, matrix products, shards(): jnp.dot(pick_recv.astype(jnp.bfloat16), trace_pool, preferred_element_typ...  3.57 us
    ppermute x1, waiting for transfers between devices, shards(): got = lax.ppermute(given, 'c', [(0, 1), (1, 0)])  2.85 us
  transfers between devices with their start and end apart: 2, of which 2 were waited for; matrix products, arithmetic and copies ran while one was open for 1% of the time, Pallas kernels for 0%

profile of v14, /device:TPU:1, one launch (start us, length us, event | category | flops | bytes accessed | tf_op | source)
XLA Modules:
  0.0 108.7 jit_solution(872481264983057282)
XLA Ops:
  0.0 0.0 copy-start
  0.0 1.0 convert_reduce_fusion.1
  1.0 1.1 %fusion.9 = f32[4,3]{0,1:T(4,128)S(1)} fusion(bf16[4,3,1,4096]{3,0,2,1:T(4,128)(2,1)} %param.5, f32[4,3]{0,1:T(4,128)S(1)} %broadcast_multiply_fusion), kind=kLoop, calls=%fused_computation.13 | loop fusion | flops 196596 | bytes 98400 | tf_op jit(solution)/shard_map/reduce_sum | solution.py:18
  2.2 0.0 copy-done
  2.2 0.1 constant_dynamic-slice_fusion
  2.3 0.1 copy.15
  2.4 1.0 fusion.10
  3.4 0.1 reshape.111
  3.5 0.1 rev.3
  3.6 0.1 reshape_reshape.3
  3.8 0.6 fusion.11
  4.4 2.0 %copy.18 = bf16[32,16,1536]{2,1,0:T(8,128)(2,1)} copy(bf16[32,16,1536]{2,0,1:T(8,128)(2,1)S(1)} %bitcast.27) | data formatting | bytes 3145728 | tf_op jit(solution)/shard_map/reshape | solution.py:120
  6.5 0.0 copy-start.1
  6.5 10.6 %all-to-all-start = ((bf16[32,16,1536]{2,1,0:T(8,128)(2,1)}), bf16[32,16,1536]{2,1,0:T(8,128)(2,1)S(1)}, u32[]{:S(2)}, u32[]{:S(2)}) async-start(bf16[32,16,1536]{2,1,0:T(8,128)(2,1)} %copy.18), calls=%async_computation | async-start | bytes 3145728 | tf_op jit(solution)/shard_map/all_to_all | solution.py:121
  17.1 0.1 copy.14
  17.2 0.0 copy-done.1
  17.2 0.0 copy-done.2
  17.2 0.1 convert_element_type.20
  17.4 0.9 reshape.117.s
  18.2 0.0 copy-done.3
  18.2 0.1 iota_compare_fusion.1
  18.3 36.6 %all-to-all-done = bf16[32,16,1536]{2,1,0:T(8,128)(2,1)S(1)} async-done(((bf16[32,16,1536]{2,1,0:T(8,128)(2,1)}), bf16[32,16,1536]{2,1,0:T(8,128)(2,1)S(1)}, u32[]{:S(2)}, u32[]{:S(2)}) %all-to-all-start) | async-done | bytes 1572896 | tf_op jit(solution)/shard_map/all_to_all | solution.py:121
  55.0 1.9 %reshape.120 = bf16[192,4096,1]{1,0,2:T(8,128)(2,1)S(1)} reshape(bf16[32,16,1536]{2,1,0:T(8,128)(2,1)S(1)} %all-to-all-done) | data formatting | bytes 3145728 | tf_op jit(solution)/shard_map/reshape | solution.py:122
  56.8 3.6 %fusion.3.p = bf16[12,48,4096]{2,1,0:T(8,128)(2,1)} fusion(bf16[192,4096,1]{1,0,2:T(8,128)(2,1)S(1)} %reshape.120, s32[12,48]{1,0:T(8,128)S(1)} %bitcast.28, pred[12,48]{1,0:T(8,128)(4,1)S(1)} %iota_compare_fusion.1), kind=kOutput, calls=%fused_computation.6 | convolution fusion | flops 906190848 | bytes 6294336 | tf_op jit(solution)/shard_map/dot_general | solution.py:127
  60.4 10.0 %xcorr.1 = (f32[8,40,1024]{2,1,0:T(8,128)}, f32[8,40,1024]{2,1,0:T(8,128)}) custom-call(s32[1]{0:T(128)} %bitcast.c, f32[12,1,5120]{2,1,0:T(1,128)} %reshape.117.s, bf16[12,48,4096]{2,1,0:T(8,128)(2,1)} %fusion.3.p), custom_call_target="tpu_custom_call" | custom-call | flops 4831838208 | bytes 7323648 | tf_op jit(solution)/shard_map/xcorr/pallas_call | solution.py:82
  70.4 4.1 %collective-permute-start = (f32[8,40,1024]{2,1,0:T(8,128)}, f32[8,40,1024]{2,1,0:T(8,128)S(1)}, u32[]{:S(2)}, u32[]{:S(2)}) collective-permute-start(f32[8,40,1024]{2,1,0:T(8,128)} %get-tuple-element.8), channel_id=1, source_target_pairs={{0,32},{32,0},{1,33},{33,1},{2,34},{34,2},{3,35},{35,3},{4,36},{36... | collective-permute-start | bytes 3932168 | tf_op jit(solution)/shard_map/ppermute | solution.py:138
  74.5 2.9 %collective-permute-done = f32[8,40,1024]{2,1,0:T(8,128)S(1)} collective-permute-done((f32[8,40,1024]{2,1,0:T(8,128)}, f32[8,40,1024]{2,1,0:T(8,128)S(1)}, u32[]{:S(2)}, u32[]{:S(2)}) %collective-permute-start) | collective-permute-done | bytes 1310752 | tf_op jit(solution)/shard_map/ppermute | solution.py:138
  77.4 1.5 %fusion = bf16[8,36,1024]{2,1,0:T(8,128)(2,1)S(1)} fusion(f32[8,40,1024]{2,1,0:T(8,128)S(1)} %collective-permute-done, f32[8,40,1024]{2,1,0:T(8,128)} %get-tuple-element.7), kind=kLoop, calls=%fused_computation.1 | loop fusion | flops 589824 | bytes 2949120 | tf_op jit(solution)/shard_map/convert.4
  78.9 0.6 reshape.114
  79.6 28.2 %all_to_all.10 = bf16[8,32,1152]{2,1,0:T(8,128)(2,1)S(1)} all-to-all(bf16[8,32,1152]{2,1,0:T(8,128)(2,1)S(1)} %reshape.114), channel_id=1, replica_groups=mesh['z'=8,'c'=2,'pairs'=32] {'z'}, dimensions={0} | all-to-all | bytes 1179648 | tf_op jit(solution)/shard_map/all_to_all | solution.py:140
  107.8 0.1 convert_reduce_fusion
  107.9 0.8 reshape.115
  (8 shorter events, 0.1 us)
Async XLA Ops:
  0.0 2.2 %copy-start = (s32[32,32,2]{1,2,0:T(2,128)S(1)}, s32[32,32,2]{1,2,0:T(2,128)}, u32[]{:S(2)}) copy-start(s32[32,32,2]{1,2,0:T(2,128)} %param.6) | copy-start | bytes 24580
  6.5 10.7 %copy-start.1 = (s32[1,12,48]{2,0,1:T(1,128)S(1)}, s32[1,12,48]{2,0,1:T(1,128)}, u32[]{:S(2)}) copy-start(s32[1,12,48]{2,0,1:T(1,128)} %param.8) | copy-start | bytes 6916
  6.5 10.8 %copy-start.2 = (s32[1,12,48]{2,0,1:T(1,128)S(1)}, s32[1,12,48]{2,0,1:T(1,128)}, u32[]{:S(2)}) copy-start(s32[1,12,48]{2,0,1:T(1,128)} %param.7) | copy-start | bytes 6916
  6.5 11.8 %copy-start.3 = (s32[1,12]{1,0:T(1,128)S(1)}, s32[1,12]{1,0:T(1,128)}, u32[]{:S(2)}) copy-start(s32[1,12]{1,0:T(1,128)} %param.9) | copy-start | bytes 148
  6.5 48.5 %all-to-all-start = ((bf16[32,16,1536]{2,1,0:T(8,128)(2,1)}), bf16[32,16,1536]{2,1,0:T(8,128)(2,1)S(1)}, u32[]{:S(2)}, u32[]{:S(2)}) async-start(bf16[32,16,1536]{2,1,0:T(8,128)(2,1)} %copy.18), calls=%async_computation | async-start | bytes 3145728 | tf_op jit(solution)/shard_map/all_to_all | solution.py:121
  70.4 7.0 %collective-permute-start = (f32[8,40,1024]{2,1,0:T(8,128)}, f32[8,40,1024]{2,1,0:T(8,128)S(1)}, u32[]{:S(2)}, u32[]{:S(2)}) collective-permute-start(f32[8,40,1024]{2,1,0:T(8,128)} %get-tuple-element.8), channel_id=1, source_target_pairs={{0,32},{32,0},{1,33},{33,1},{2,34},{34,2},{3,35},{35,3},{4,36},{36... | collective-permute-start | bytes 3932168 | tf_op jit(solution)/shard_map/ppermute | solution.py:138
